TPU v7x, 256 devices: a whole 4x4x8 slice. The times are simulated.
256 devices in a mesh: dp: 2 (over core), expert: 8 (over y, x_lo), mp: 16 (over z, x_hi).
Axes of the slice: x: 4 (x_hi: 2, x_lo: 2; x = x_hi * 2 + x_lo), y: 4, z: 8, core: 2. Of those that a mesh axis runs over, the one named last changes fastest.
Arguments:
- hidden_in: bfloat16 [8192, 2048], P(('dp', 'expert')), may hold values from -6 to 6
- norm_gain: float32 [2048], replicated, may hold values from 0.1 to 1.9
- router_w: bfloat16 [2048, 8], replicated, may hold values from -0.0625 to 0.0625
- choices: int32 [8192, 2], P(('dp', 'expert')), may hold values from 0 to 7, all different within a row; in each aligned block of 512 rows (0 to 511, 512 to 1023, ...) at most 192 rows name the same one
- w_gate: bfloat16 [8, 2048, 5632], P('expert', None, 'mp'), may hold values from -0.125 to 0.125
- w_up: bfloat16 [8, 2048, 5632], P('expert', None, 'mp'), may hold values from -0.125 to 0.125
- w_down: bfloat16 [8, 5632, 2048], P('expert', 'mp'), may hold values from -0.109375 to 0.109375
Outputs:
- block_out: bfloat16 [8192, 2048], P(('dp', 'expert'), 'mp')
Inputs may be any that keep to these rules, and one draw needn't show every extreme that they name: `choices`: each row names two different experts. Among the 512 rows of one block of tokens no expert is named more than 192 times, and in every draw some expert is named exactly 192 times in some block.
All inputs are finite; a program needn't handle non-finite values.
Results may differ from a plain program's by a relative error of at most 0.012.
Values may be sent and summed in bfloat16 or wider, within the bound.
No kernel may reach another device: no remote copies, remote signals or barrier semaphores. Data moves between devices by JAX's collectives and lax.ppermute only.
A program may use at most 128 MiB of HBM per device.

v0:
```python
import jax
import jax.numpy as jnp
from jax import lax
from jax.sharding import PartitionSpec as P

eps_norm = 1e-06


def pair_slots(choice_ids, expert_count):
    flat_ids = choice_ids.reshape(-1)
    onehot = (flat_ids[:, None] == jnp.arange(expert_count, dtype=jnp.int32)[None, :]).astype(
        jnp.int32
    )
    earlier = jnp.cumsum(onehot, axis=0) - onehot
    slot_ids = jnp.sum(earlier * onehot, axis=1)
    return (flat_ids, slot_ids)


def pair_weights(normed, router_w, choice_ids):
    logits = jnp.dot(normed, router_w, preferred_element_type=jnp.float32)
    picked = jnp.take_along_axis(logits, choice_ids, axis=1)
    first_weight = jax.nn.sigmoid(picked[:, 0] - picked[:, 1])
    return jnp.stack([first_weight, 1.0 - first_weight], axis=1)


def per_device(hidden_in, norm_gain, router_w, choices, w_gate, w_up, w_down):
    experts = lax.axis_size("expert")
    mp_count = lax.axis_size("mp")
    tokens_dev, model_width = hidden_in.shape
    capacity = 3 * tokens_dev // experts
    slice_width = model_width // mp_count
    wide_in = hidden_in.astype(jnp.float32)
    normed = (
        wide_in
        * lax.rsqrt(jnp.mean(wide_in * wide_in, axis=1, keepdims=True) + eps_norm)
        * norm_gain
    ).astype(jnp.bfloat16)
    weights = pair_weights(normed, router_w, choices)
    flat_ids, slot_ids = pair_slots(choices, experts)
    row_index = flat_ids * capacity + slot_ids
    sources = jnp.repeat(normed, 2, axis=0)
    buffer = jnp.zeros((experts * capacity, model_width), jnp.bfloat16).at[row_index].set(sources)
    buffer = buffer.reshape(experts, capacity, model_width)
    column = lax.axis_index("mp") * slice_width
    arrived = lax.all_to_all(buffer, "expert", split_axis=0, concat_axis=0, tiled=True)
    expert_rows = arrived.reshape(experts * capacity, model_width)
    gate_proj = jnp.dot(expert_rows, w_gate[0], preferred_element_type=jnp.float32)
    up_proj = jnp.dot(expert_rows, w_up[0], preferred_element_type=jnp.float32)
    hidden = (jax.nn.silu(gate_proj) * up_proj).astype(jnp.bfloat16)
    partial_value = jnp.dot(hidden, w_down[0], preferred_element_type=jnp.float32).astype(
        jnp.bfloat16
    )
    partial_value = partial_value.reshape(experts, capacity, model_width)
    residual = lax.dynamic_slice_in_dim(wide_in, column, slice_width, 1)
    summed = lax.psum_scatter(
        partial_value.astype(jnp.float32).astype(jnp.bfloat16),
        "mp",
        scatter_dimension=2,
        tiled=True,
    ).astype(jnp.float32)
    returned = lax.all_to_all(
        summed.astype(jnp.bfloat16), "expert", split_axis=0, concat_axis=0, tiled=True
    ).astype(summed.dtype)
    picked = returned.reshape(experts * capacity, slice_width)[row_index].reshape(
        tokens_dev, 2, slice_width
    )
    mixture = jnp.sum(picked * weights[:, :, None], axis=1)
    return (residual + mixture).astype(jnp.bfloat16)


def solution(mesh):
    placed = (
        P(("dp", "expert"), None),
        P(),
        P(),
        P(("dp", "expert"), None),
        P("expert", None, "mp"),
        P("expert", None, "mp"),
        P("expert", "mp", None),
    )
    return jax.shard_map(
        per_device, mesh=mesh, in_specs=placed, out_specs=P(("dp", "expert"), "mp"), check_vma=False
    )
```

profile of v0, /device:TPU:2, one launch (start us, length us, event | category | flops | bytes accessed | tf_op | source)
XLA Modules:
  0.0 425.7 jit_solution(3803062863727629220)
XLA Ops:
  7.4 1.6 copy.37
  11.2 2.1 multiply_reduce_fusion
  16.5 5.0 %reduce-window.6 = s32[8,8,128]{2,1,0:T(8,128)} reduce-window(s32[8,8,128]{2,1,0:T(8,128)} %fusion.12, s32[]{:T(128)} %constant.14.clone.1), window={size=1x1x128 pad=0_0x0_0x127_0}, to_apply=%region_0.0 | reduce-window | flops 1040384 | bytes 65540 | tf_op jit(solution)/shard_map/reduce-window
  22.7 1.5 add_bitcast_fusion
  26.8 3.7 broadcast_in_dim.9
  30.6 7.2 %reshape.115 = bf16[1024,2048]{1,0:T(8,128)(2,1)} reshape(bf16[512,2,2048]{2,1,0:T(2,128)(2,1)} %broadcast_in_dim.9) | data formatting | bytes 8388608 | tf_op jit(solution)/shard_map/reshape | solution.py:41
  37.8 11.2 %scatter_custom_fusion = bf16[1536,2048]{1,0:T(8,128)(2,1)} fusion(s32[1024]{0:T(1024)S(1)} %bitcast.58, bf16[1024,2048]{1,0:T(8,128)(2,1)} %reshape.115, bf16[]{:T(256)} %constant.18.clone.1), kind=kCustom, calls=%fused_computation.6 | custom fusion | bytes 6291968 | tf_op jit(solution)/shard_map/scatter | solution.py:42
  49.0 77.4 %all_to_all.10 = bf16[8,192,2048]{2,1,0:T(8,128)(2,1)S(1)} all-to-all(bf16[8,192,2048]{2,1,0:T(8,128)(2,1)} %bitcast.51), channel_id=1, replica_groups=mesh['dp'=2,'expert'=8,'mp'=16] {'expert'}, dimensions={0} | all-to-all | bytes 12582912 | tf_op jit(solution)/shard_map/all_to_all | solution.py:45
  126.5 2.7 copy-done.4
  129.2 3.8 fusion.5
  132.9 11.4 %convolution_convert_fusion = bf16[1536,2048]{1,0:T(8,128)(2,1)} fusion(bf16[1,352,2048]{2,1,0:T(8,128)(2,1)S(1)} %copy-done, bf16[1536,2048]{1,0:T(8,128)(2,1)} %bitcast.54, f32[1536,352]{0,1:T(8,128)} %fusion.5, bf16[1,2048,352]{1,2,0:T(8,128)(2,1)S(1)} %copy-done.9), kind=kOutput, calls=%fused_computation.3 | convolution fusion | flops 4435574784 | bytes 17629184 | tf_op jit(solution)/shard_map/dot_general | solution.py:50
  144.3 12.8 %copy.42 = bf16[8,192,2048]{1,0,2:T(8,128)(2,1)} copy(bf16[8,192,2048]{2,1,0:T(8,128)(2,1)} %bitcast.52) | data formatting | bytes 12582912
  157.1 13.5 %reshape.124 = bf16[2048,1536]{1,0:T(8,128)(2,1)} reshape(bf16[2048,8,192]{2,1,0:T(8,128)(2,1)} %bitcast.50) | data formatting | bytes 12582912
  171.7 2.2 fusion.15
  173.9 6.5 %gather_fusion.1 = f32[1024]{0:T(1024)S(1)} fusion(f32[512,8]{0,1:T(8,128)S(1)} %fusion.15, s32[1024]{0:T(1024)S(1)} %reshape.105), kind=kCustom, calls=%fused_computation.1 | custom fusion | bytes 16384 | tf_op jit(solution)/shard_map/jit(take_along_axis)/gather | solution.py:21
  182.4 211.1 %reduce-scatter.4.cloned.1.call-done = bf16[128,1536]{1,0:T(8,128)(2,1)} async-done(((bf16[2048,1536]{1,0:T(8,128)(2,1)}), bf16[128,1536]{1,0:T(8,128)(2,1)}) %reduce-scatter.4.cloned.1.call-update) | async-done | bytes 393232
  393.5 2.2 reshape.125
  395.7 2.2 copy.43
  397.9 5.7 %all-to-all-start.1 = ((bf16[8,192,128]{2,1,0:T(8,128)(2,1)}), bf16[8,192,128]{2,1,0:T(8,128)(2,1)}, u32[]{:S(2)}, u32[]{:S(2)}) async-start(bf16[8,192,128]{2,1,0:T(8,128)(2,1)} %copy.43), calls=%async_computation.1 | async-start | bytes 786432 | tf_op jit(solution)/shard_map/all_to_all | solution.py:61
  403.7 2.5 convert_element_type.27
  406.3 4.3 all-to-all-done.1
  411.6 2.8 gather_fusion
  414.4 2.8 multiply_reduce_fusion.1
  417.2 1.6 add_convert_fusion
  (44 shorter events, 14.3 us)
Async XLA Ops:
  6.5 126.4 %copy-start = (bf16[1,352,2048]{2,1,0:T(8,128)(2,1)S(1)}, bf16[1,352,2048]{2,1,0:T(8,128)(2,1)}, u32[]{:S(2)}) copy-start(bf16[1,352,2048]{2,1,0:T(8,128)(2,1)} %param.13) | copy-start | bytes 4325380
  6.5 17.7 %copy-start.1 = (bf16[512,2048]{1,0:T(8,128)(2,1)S(1)}, bf16[512,2048]{1,0:T(8,128)(2,1)}, u32[]{:S(2)}) copy-start(bf16[512,2048]{1,0:T(8,128)(2,1)} %param.7) | copy-start | bytes 6291460
  6.5 387.0 %reduce-scatter.4.cloned.1.call-start = ((), (), s32[]{:S(2)}) async-start(), calls=%async_computation.3 | async-start | bytes 6684672
  25.5 1.4 copy-start.3
  30.5 7.2 %copy-start.5 = (s32[1,8,8,128]{3,2,1,0:T(8,128)S(1)}, s32[1,8,8,128]{3,2,1,0:T(8,128)}, u32[]{:S(2)}) copy-start(s32[1,8,8,128]{3,2,1,0:T(8,128)} %add_bitcast_fusion) | copy-start | bytes 98308
  49.0 80.1 %copy-start.8 = (bf16[1,2048,352]{1,2,0:T(8,128)(2,1)S(1)}, bf16[1,2048,352]{1,2,0:T(8,128)(2,1)}, u32[]{:S(2)}) copy-start(bf16[1,2048,352]{1,2,0:T(8,128)(2,1)} %param.11) | copy-start | bytes 4325380
  126.5 2.7 copy-start.4
  129.2 3.8 copy-start.9
  170.6 0.7 copy-start.6
  170.6 1.0 copy-start.7
  180.4 223.2 %copy-start.2 = (bf16[512,2048]{1,0:T(8,128)(2,1)S(1)}, bf16[512,2048]{1,0:T(8,128)(2,1)}, u32[]{:S(2)}) copy-start(bf16[512,2048]{1,0:T(8,128)(2,1)} %param.7) | copy-start | bytes 6291460
  397.9 12.6 %all-to-all-start.1 = ((bf16[8,192,128]{2,1,0:T(8,128)(2,1)}), bf16[8,192,128]{2,1,0:T(8,128)(2,1)}, u32[]{:S(2)}, u32[]{:S(2)}) async-start(bf16[8,192,128]{2,1,0:T(8,128)(2,1)} %copy.43), calls=%async_computation.1 | async-start | bytes 786432 | tf_op jit(solution)/shard_map/all_to_all | solution.py:61
Sparse Core Ops, SparseCore 0:
  170.8 222.6 reduce-scatter.3
where the time goes:
time: 427 us; the launch traced here: 426 us
  waiting for transfers between devices  215 us (50%)
  blocking collectives  77.4 us (18%)
  local copies, waits for them, and re-layouts  76.3 us (18%)
  other arithmetic  20.1 us (5%)
  matrix products  17.4 us (4%)
  between operations  13.5 us (3%)
  starting transfers between devices  5.72 us (1%)
    unnamed x2, waiting for transfers between devices  211 us
    all_to_all x1, blocking collectives, per_device(): lax.all_to_all(buffer, 'expert', split_axis=0, concat_axis=0, tiled=True)  77.4 us
    unnamed x25, local copies, waits for them, and re-layouts  37.1 us
    dot_general x1, matrix products, per_device(): jnp.dot(hidden, w_down[0], preferred_element_type=jnp.float32)  11.4 us
    scatter x1, local copies, waits for them, and re-layouts, per_device(): jnp.zeros((experts * capacity, model_width), jnp.bfloat16).at[row_index]  11.2 us
    gather x5, local copies, waits for them, and re-layouts, pair_weights(): picked = jnp.take_along_axis(logits, choice_ids, axis=1)  8.79 us
  transfers between devices with their start and end apart: 2, of which 2 were waited for; matrix products, arithmetic and copies ran while one was open for 3% of the time, Pallas kernels for 0%

commit v1 on v0

v1 whole, which is shorter than its diff:
```python
import numpy as np

import jax
import jax.numpy as jnp
from jax import lax
from jax.sharding import Mesh
from jax.sharding import PartitionSpec as P

eps_norm = 1e-06


def pair_rows(choices, experts, capacity):
    flat_ids = choices.reshape(-1)
    pairs = flat_ids.shape[0]
    onehot = (flat_ids[:, None] == jnp.arange(experts, dtype=jnp.int32)[None, :]).astype(jnp.bfloat16)
    before = (
        jnp.arange(pairs, dtype=jnp.int32)[None, :] < jnp.arange(pairs, dtype=jnp.int32)[:, None]
    ).astype(jnp.bfloat16)
    earlier = jnp.dot(before, onehot, preferred_element_type=jnp.float32)
    slot_ids = jnp.sum(earlier * onehot.astype(jnp.float32), axis=1).astype(jnp.int32)
    return (flat_ids * capacity + slot_ids).reshape(-1, 2)


def pair_weights(normed, router_w, choice_ids):
    logits = jnp.dot(normed, router_w, preferred_element_type=jnp.float32)
    picked = jnp.take_along_axis(logits, choice_ids, axis=1)
    first_weight = jax.nn.sigmoid(picked[:, 0] - picked[:, 1])
    return jnp.stack([first_weight, 1.0 - first_weight], axis=1)


def make_per_device(expert_axes, mp_axes, experts, mp_count):
    def per_device(hidden_in, norm_gain, router_w, choices, w_gate, w_up, w_down):
        tokens_dev, model_width = hidden_in.shape
        capacity = 3 * tokens_dev // experts
        slice_width = model_width // mp_count
        rows_total = experts * capacity
        wide_in = hidden_in.astype(jnp.float32)
        normed = (
            wide_in
            * lax.rsqrt(jnp.mean(wide_in * wide_in, axis=1, keepdims=True) + eps_norm)
            * norm_gain
        ).astype(jnp.bfloat16)
        weights = pair_weights(normed, router_w, choices)
        rows = pair_rows(choices, experts, capacity)
        slots = jnp.arange(rows_total, dtype=jnp.int32)
        pick0 = rows[:, 0][None, :] == slots[:, None]
        pick1 = rows[:, 1][None, :] == slots[:, None]
        dispatch = (pick0 | pick1).astype(jnp.bfloat16)
        buffer = jnp.dot(dispatch, normed, preferred_element_type=jnp.float32).astype(jnp.bfloat16)
        buffer = buffer.reshape(experts, capacity, model_width)
        arrived = lax.all_to_all(buffer, expert_axes, split_axis=0, concat_axis=0, tiled=True)
        expert_rows = arrived.reshape(rows_total, model_width)
        gate_proj = jnp.dot(expert_rows, w_gate[0], preferred_element_type=jnp.float32)
        up_proj = jnp.dot(expert_rows, w_up[0], preferred_element_type=jnp.float32)
        hidden = (jax.nn.silu(gate_proj) * up_proj).astype(jnp.bfloat16)
        partial_t = lax.dot_general(
            w_down[0], hidden, (((0,), (1,)), ((), ())), preferred_element_type=jnp.float32
        ).astype(jnp.bfloat16)
        summed = partial_t
        for axis in mp_axes:
            summed = lax.psum_scatter(summed, axis, scatter_dimension=0, tiled=True)
        summed = summed.reshape(slice_width, experts, capacity)
        returned = lax.all_to_all(summed, expert_axes, split_axis=1, concat_axis=1, tiled=True)
        returned = returned.reshape(slice_width, rows_total)
        column = lax.axis_index(mp_axes) * slice_width
        residual = lax.dynamic_slice_in_dim(wide_in, column, slice_width, 1)
        sel0 = (rows[:, 0][:, None] == slots[None, :]).astype(jnp.bfloat16)
        sel1 = (rows[:, 1][:, None] == slots[None, :]).astype(jnp.bfloat16)
        dims = (((1,), (1,)), ((), ()))
        out0 = lax.dot_general(sel0, returned, dims, preferred_element_type=jnp.float32)
        out1 = lax.dot_general(sel1, returned, dims, preferred_element_type=jnp.float32)
        mixture = out0 * weights[:, 0:1] + out1 * weights[:, 1:2]
        return (residual + mixture).astype(jnp.bfloat16)

    return per_device


def x_parts(devices):
    coords = [getattr(d, "coords", None) for d in devices]
    if any(c is None for c in coords):
        return 1
    return len({c[0] for c in coords})


def solution(mesh):
    n_dp, n_expert, n_mp = (mesh.shape[a] for a in ("dp", "expert", "mp"))
    devs = np.asarray(mesh.devices).reshape(n_dp, n_expert, n_mp)
    ex = x_parts(devs[0, :, 0])
    mx = x_parts(devs[0, 0, :])
    if n_expert % ex or n_mp % mx:
        ex, mx = 1, 1
    fine = Mesh(
        devs.reshape(n_dp, n_expert // ex, ex, n_mp // mx, mx), ("dp", "ey", "ex", "mz", "mx")
    )
    expert_axes = ("ey", "ex")
    mp_axes = ("mz", "mx")
    tok = ("dp",) + expert_axes
    placed = (
        P(tok, None),
        P(),
        P(),
        P(tok, None),
        P(expert_axes, None, mp_axes),
        P(expert_axes, None, mp_axes),
        P(expert_axes, mp_axes, None),
    )
    return jax.shard_map(
        make_per_device(expert_axes, mp_axes, n_expert, n_mp),
        mesh=fine,
        in_specs=placed,
        out_specs=P(tok, mp_axes),
        check_vma=False,
    )
```

time: 427 us -> 240 us (0.56)
  waiting for transfers between devices: 215 us -> 94.2 us
  local copies, waits for them, and re-layouts: 76.3 us -> 18.8 us
  other arithmetic: 20.1 us -> 3.7 us
  matrix products: 17.4 us -> 26.2 us
    unnamed x2 -> x3, waiting for transfers between devices: 211 us -> 10.1 us
    reduce_scatter x0 -> x1, waiting for transfers between devices: none -> 76.8 us  [per_device(): summed = lax.psum_scatter(summed, axis, scatter_dimension=0, tiled=True)]
    unnamed x25 -> x13, local copies, waits for them, and re-layouts: 37.1 us -> 8.55 us
    scatter x1 -> x0, local copies, waits for them, and re-layouts: 11.2 us -> none  [per_device(): jnp.zeros((experts * capacity, model_width), jnp.bfloat16).at[row_index]]
    dot_general x1 -> x5, matrix products: 11.4 us -> 20.1 us  [the longest x1 11.8 us: per_device(): lax.dot_general(w_down[0], hidden, (((0,), (1,)), ((), ())), preferred_el...]
    reshape x1 -> x0, local copies, waits for them, and re-layouts: 7.19 us -> none  [per_device(): sources = jnp.repeat(normed, 2, axis=0)]
    another operation x3 -> x0, other arithmetic: 5.21 us -> none
  transfers between devices with their start and end apart: 2 -> 3, of which waited for: 2 -> 3; matrix products, arithmetic and copies ran while one was open for 3% -> 5% of each run, Pallas kernels for 0% -> 0%
where the time goes in v1:
time: 240 us; the launch traced here: 239 us
  waiting for transfers between devices  94.2 us (39%)
  blocking collectives  77.2 us (32%)
  matrix products  26.2 us (11%)
  local copies, waits for them, and re-layouts  18.8 us (8%)
  between operations  13.5 us (6%)
  starting transfers between devices  5.8 us (2%)
  other arithmetic  3.7 us (2%)
    all_to_all x1, blocking collectives, per_device(): lax.all_to_all(buffer, expert_axes, split_axis=0, concat_axis=0, tiled=True)  77.2 us
    reduce_scatter x1, waiting for transfers between devices, per_device(): summed = lax.psum_scatter(summed, axis, scatter_dimension=0, tiled=True)  76.8 us
    dot_general x1, matrix products, per_device(): lax.dot_general(w_down[0], hidden, (((0,), (1,)), ((), ())), preferred_el...  11.8 us
    unnamed x3, waiting for transfers between devices  10.1 us
    unnamed x13, local copies, waits for them, and re-layouts  8.55 us
    all_to_all x1, waiting for transfers between devices, per_device(): lax.all_to_all(summed, expert_axes, split_axis=1, concat_axis=1, tiled=True)  7.31 us
    gather x5, local copies, waits for them, and re-layouts, pair_weights(): picked = jnp.take_along_axis(logits, choice_ids, axis=1)  7.15 us
    all_to_all x1, starting transfers between devices, per_device(): lax.all_to_all(summed, expert_axes, split_axis=1, concat_axis=1, tiled=True)  5.75 us
  transfers between devices with their start and end apart: 3, of which 3 were waited for; matrix products, arithmetic and copies ran while one was open for 5% of the time, Pallas kernels for 0%

profile of v1, /device:TPU:2, one launch (start us, length us, event | category | flops | bytes accessed | tf_op | source)
XLA Modules:
  0.0 239.4 jit_solution(11677232093577638369)
XLA Ops:
  6.5 1.7 copy.32
  8.2 1.1 eq.71
  9.3 0.5 fusion.21
  9.8 0.9 convert_element_type.42
  10.7 1.1 copy.33
  11.8 0.7 multiply_add_fusion
  12.5 0.5 multiply_reduce_fusion
  13.0 4.8 %convolution_convert_fusion.1 = bf16[1536,2048]{1,0:T(8,128)(2,1)S(1)} fusion(s32[512]{0:T(512)S(1)} %bitcast.36, s32[512]{0:T(512)S(1)} %bitcast.38, f32[2048]{0:T(1024)} %param.8, f32[512]{0:T(512)S(1)} %add_rsqrt_fusion, bf16[512,2048]{1,0:T(8,128)(2,1)S(1)} %copy-done.1), kind=kOutput, calls=%fused_computation.2 | convolution fusion | flops 3230924800 | bytes 8402944 | tf_op jit(solution)/shard_map/dot_general | solution.py:49
  17.8 77.2 %all_to_all.10 = bf16[8,192,2048]{2,1,0:T(8,128)(2,1)S(1)} all-to-all(bf16[8,192,2048]{2,1,0:T(8,128)(2,1)S(1)} %bitcast.33), channel_id=1, replica_groups=mesh['dp'=2,'ey'=4,'ex'=2,'mz'=8,'mx'=2] {'ey','ex'}, dimensions={0} | all-to-all | bytes 12582912 | tf_op jit(solution)/shard_map/all_to_all | solution.py:51
  95.1 2.7 %copy-done.2 = bf16[8,192,2048]{2,1,0:T(8,128)(2,1)} copy-done((bf16[8,192,2048]{2,1,0:T(8,128)(2,1)}, bf16[8,192,2048]{2,1,0:T(8,128)(2,1)S(1)}, u32[]{:S(2)}) %copy-start.2) | copy-done | bytes 6291480
  97.7 3.8 %fusion.13 = f32[1536,352]{0,1:T(8,128)} fusion(bf16[1536,2048]{1,0:T(8,128)(2,1)S(1)} %bitcast.31, bf16[1,2048,352]{1,2,0:T(8,128)(2,1)S(1)} %copy-done.4), kind=kOutput, calls=%fused_computation.23 | convolution fusion | flops 2214592512 | bytes 9895936 | tf_op jit(solution)/shard_map/dot_general | solution.py:53
  101.5 11.8 %fusion = bf16[2048,1536]{0,1:T(8,128)(2,1)} fusion(bf16[1,352,2048]{2,1,0:T(8,128)(2,1)S(1)} %copy-done, bf16[1536,2048]{1,0:T(8,128)(2,1)} %bitcast.32, f32[1536,352]{0,1:T(8,128)} %fusion.13, bf16[1,2048,352]{1,2,0:T(8,128)(2,1)} %param.12), kind=kOutput, calls=%fused_computation.3 | convolution fusion | flops 4435574784 | bytes 17629184 | tf_op jit(solution)/shard_map/dot_general | solution.py:56
  113.4 76.8 %reduce-scatter.5.cloned.1.call-done = bf16[256,1536]{0,1:T(8,128)(2,1)} async-done(((bf16[2048,1536]{0,1:T(8,128)(2,1)}), bf16[256,1536]{0,1:T(8,128)(2,1)}) %reduce-scatter.5.cloned.1.call-update) | async-done | bytes 786448 | tf_op jit(solution)/shard_map/reduce_scatter | solution.py:61
  190.2 2.3 copy.36
  192.5 2.5 %convert_element_type.38 = f32[512,2048]{1,0:T(8,128)} convert(bf16[512,2048]{1,0:T(8,128)(2,1)S(1)} %copy-done.1) | non-fusion elementwise | flops 1048576 | bytes 6291456 | tf_op jit(solution)/shard_map/convert_element_type | solution.py:37
  195.3 2.3 fusion.24
  197.6 6.5 %gather_fusion = f32[1024]{0:T(1024)S(1)} fusion(f32[512,8]{0,1:T(8,128)S(1)} %fusion.24, s32[1024]{0:T(1024)S(1)} %reshape.42), kind=kCustom, calls=%fused_computation | custom fusion | bytes 16384 | tf_op jit(solution)/shard_map/jit(take_along_axis)/gather | solution.py:26
  204.2 0.2 reshape.45
  204.5 10.1 %reduce-scatter.7.cloned.1.call-done = bf16[128,1536]{1,0:T(8,128)(2,1)} async-done(((bf16[256,1536]{1,0:T(8,128)(2,1)}), bf16[128,1536]{1,0:T(8,128)(2,1)}) %reduce-scatter.7.cloned.1.call-update) | async-done | bytes 393232
  214.5 1.9 copy.37
  216.5 5.8 %all-to-all-start.1 = ((bf16[128,8,192]{0,2,1:T(8,128)(2,1)}), bf16[128,8,192]{0,2,1:T(8,128)(2,1)S(1)}, u32[]{:S(2)}, u32[]{:S(2)}) async-start(bf16[128,8,192]{0,2,1:T(8,128)(2,1)} %bitcast.8), calls=%async_computation.2 | async-start | bytes 786432 | tf_op jit(solution)/shard_map/all_to_all | solution.py:63
  222.2 7.3 %all-to-all-done.1 = bf16[128,8,192]{0,2,1:T(8,128)(2,1)S(1)} async-done(((bf16[128,8,192]{0,2,1:T(8,128)(2,1)}), bf16[128,8,192]{0,2,1:T(8,128)(2,1)S(1)}, u32[]{:S(2)}, u32[]{:S(2)}) %all-to-all-start.1) | async-done | bytes 393248 | tf_op jit(solution)/shard_map/all_to_all | solution.py:63
  229.5 0.7 fusion.17
  230.2 2.3 fusion.19
  (22 shorter events, 0.6 us)
Async XLA Ops:
  6.5 95.0 %copy-start = (bf16[1,352,2048]{2,1,0:T(8,128)(2,1)S(1)}, bf16[1,352,2048]{2,1,0:T(8,128)(2,1)}, u32[]{:S(2)}) copy-start(bf16[1,352,2048]{2,1,0:T(8,128)(2,1)} %param.13) | copy-start | bytes 4325380
  6.5 6.0 %copy-start.1 = (bf16[512,2048]{1,0:T(8,128)(2,1)S(1)}, bf16[512,2048]{1,0:T(8,128)(2,1)}, u32[]{:S(2)}) copy-start(bf16[512,2048]{1,0:T(8,128)(2,1)} %param.7) | copy-start | bytes 6291460
  6.5 183.6 %reduce-scatter.5.cloned.1.call-start = ((), (), s32[]{:S(2)}) async-start(), calls=%async_computation.4 | async-start | bytes 7077888 | tf_op jit(solution)/shard_map/reduce_scatter | solution.py:61
  17.8 79.9 %copy-start.4 = (bf16[1,2048,352]{1,2,0:T(8,128)(2,1)S(1)}, bf16[1,2048,352]{1,2,0:T(8,128)(2,1)}, u32[]{:S(2)}) copy-start(bf16[1,2048,352]{1,2,0:T(8,128)(2,1)} %param.11) | copy-start | bytes 4325380
  95.0 2.7 %copy-start.2 = (bf16[8,192,2048]{2,1,0:T(8,128)(2,1)}, bf16[8,192,2048]{2,1,0:T(8,128)(2,1)S(1)}, u32[]{:S(2)}) copy-start(bf16[8,192,2048]{2,1,0:T(8,128)(2,1)S(1)} %all_to_all.10) | copy-start | bytes 18874372
  113.3 101.2 %reduce-scatter.7.cloned.1.call-start = ((), (), s32[]{:S(2)}) async-start(), calls=%async_computation.5 | async-start | bytes 1179648
  192.5 2.5 %copy-start.3 = (s32[512,2]{0,1:T(2,128)S(1)}, s32[512,2]{0,1:T(2,128)}, u32[]{:S(2)}) copy-start(s32[512,2]{0,1:T(2,128)} %param.10) | copy-start | bytes 12292
  216.5 13.1 %all-to-all-start.1 = ((bf16[128,8,192]{0,2,1:T(8,128)(2,1)}), bf16[128,8,192]{0,2,1:T(8,128)(2,1)S(1)}, u32[]{:S(2)}, u32[]{:S(2)}) async-start(bf16[128,8,192]{0,2,1:T(8,128)(2,1)} %bitcast.8), calls=%async_computation.2 | async-start | bytes 786432 | tf_op jit(solution)/shard_map/all_to_all | solution.py:63
Sparse Core Ops, SparseCore 0:
  113.5 76.6 reduce-scatter.4
  192.7 21.8 reduce-scatter.6

commit v2 on v1

--- a/solution.py
+++ b/solution.py
@@ -28,7 +28,7 @@
     return jnp.stack([first_weight, 1.0 - first_weight], axis=1)
 
 
-def make_per_device(expert_axes, mp_axes, experts, mp_count):
+def make_per_device(expert_axes, mp_axes, experts, mp_count, n_chunks=2):
     def per_device(hidden_in, norm_gain, router_w, choices, w_gate, w_up, w_down):
         tokens_dev, model_width = hidden_in.shape
         capacity = 3 * tokens_dev // experts
@@ -48,20 +48,26 @@
         dispatch = (pick0 | pick1).astype(jnp.bfloat16)
         buffer = jnp.dot(dispatch, normed, preferred_element_type=jnp.float32).astype(jnp.bfloat16)
         buffer = buffer.reshape(experts, capacity, model_width)
-        arrived = lax.all_to_all(buffer, expert_axes, split_axis=0, concat_axis=0, tiled=True)
-        expert_rows = arrived.reshape(rows_total, model_width)
-        gate_proj = jnp.dot(expert_rows, w_gate[0], preferred_element_type=jnp.float32)
-        up_proj = jnp.dot(expert_rows, w_up[0], preferred_element_type=jnp.float32)
-        hidden = (jax.nn.silu(gate_proj) * up_proj).astype(jnp.bfloat16)
-        partial_t = lax.dot_general(
-            w_down[0], hidden, (((0,), (1,)), ((), ())), preferred_element_type=jnp.float32
-        ).astype(jnp.bfloat16)
-        summed = partial_t
-        for axis in mp_axes:
-            summed = lax.psum_scatter(summed, axis, scatter_dimension=0, tiled=True)
-        summed = summed.reshape(slice_width, experts, capacity)
-        returned = lax.all_to_all(summed, expert_axes, split_axis=1, concat_axis=1, tiled=True)
-        returned = returned.reshape(slice_width, rows_total)
+        chunk = capacity // n_chunks
+        pieces = []
+        for c in range(n_chunks):
+            part = buffer[:, c * chunk:(c + 1) * chunk]
+            arrived = lax.all_to_all(part, expert_axes, split_axis=0, concat_axis=0, tiled=True)
+            expert_rows = arrived.reshape(experts * chunk, model_width)
+            gate_proj = jnp.dot(expert_rows, w_gate[0], preferred_element_type=jnp.float32)
+            up_proj = jnp.dot(expert_rows, w_up[0], preferred_element_type=jnp.float32)
+            hidden = (jax.nn.silu(gate_proj) * up_proj).astype(jnp.bfloat16)
+            partial_t = lax.dot_general(
+                w_down[0], hidden, (((0,), (1,)), ((), ())), preferred_element_type=jnp.float32
+            ).astype(jnp.bfloat16)
+            summed = partial_t
+            for axis in mp_axes:
+                summed = lax.psum_scatter(summed, axis, scatter_dimension=0, tiled=True)
+            summed = summed.reshape(slice_width, experts, chunk)
+            pieces.append(
+                lax.all_to_all(summed, expert_axes, split_axis=1, concat_axis=1, tiled=True)
+            )
+        returned = jnp.concatenate(pieces, axis=2).reshape(slice_width, rows_total)
         column = lax.axis_index(mp_axes) * slice_width
         residual = lax.dynamic_slice_in_dim(wide_in, column, slice_width, 1)
         sel0 = (rows[:, 0][:, None] == slots[None, :]).astype(jnp.bfloat16)

time: 240 us -> 242 us (level)
  waiting for transfers between devices: 94.2 us -> 73.1 us
  blocking collectives: 77.2 us -> 84.3 us
  local copies, waits for them, and re-layouts: 18.8 us -> 25.4 us
  starting transfers between devices: 5.8 us -> 11.7 us
  matrix products: 26.2 us -> 30.6 us
    reduce_scatter x1 -> x2, waiting for transfers between devices: 76.8 us -> 46.3 us  [per_device(): summed = lax.psum_scatter(summed, axis, scatter_dimension=0, tiled=True)]
    unnamed x3 -> x6, waiting for transfers between devices: 10.1 us -> 21 us
    all_to_all x1 -> x2, blocking collectives: 77.2 us -> 84.3 us  [per_device(): lax.all_to_all(part, expert_axes, split_axis=0, concat_axis=0, tiled=True)]
    all_to_all x1 -> x2, starting transfers between devices: 5.75 us -> 11.5 us  [per_device(): lax.all_to_all(summed, expert_axes, split_axis=1, concat_axis=1, tiled=True)]
    dot_general x1 -> x2, matrix products: 11.8 us -> 16.1 us  [per_device(): lax.dot_general(w_down[0], hidden, (((0,), (1,)), ((), ())), preferred_el...]
    unnamed x13 -> x21, local copies, waits for them, and re-layouts: 8.55 us -> 12.6 us
    slice x0 -> x1, local copies, waits for them, and re-layouts: none -> 2.54 us  [per_device(): part = buffer[:, c * chunk:(c + 1) * chunk]]
    all_to_all x1 -> x2, waiting for transfers between devices: 7.31 us -> 5.75 us  [per_device(): lax.all_to_all(summed, expert_axes, split_axis=1, concat_axis=1, tiled=True)]
  transfers between devices with their start and end apart: 3 -> 6, of which waited for: 3 -> 4; matrix products, arithmetic and copies ran while one was open for 5% -> 12% of each run, Pallas kernels for 0% -> 0%
where the time goes in v2:
time: 242 us; the launch traced here: 241 us
  blocking collectives  84.3 us (35%)
  waiting for transfers between devices  73.1 us (30%)
  matrix products  30.6 us (13%)
  local copies, waits for them, and re-layouts  25.4 us (10%)
  between operations  13.3 us (5%)
  starting transfers between devices  11.7 us (5%)
  other arithmetic  3.04 us (1%)
    all_to_all x2, blocking collectives, per_device(): lax.all_to_all(part, expert_axes, split_axis=0, concat_axis=0, tiled=True)  84.3 us
    reduce_scatter x2, waiting for transfers between devices, per_device(): summed = lax.psum_scatter(summed, axis, scatter_dimension=0, tiled=True)  46.3 us
    unnamed x6, waiting for transfers between devices  21 us
    dot_general x2, matrix products, per_device(): lax.dot_general(w_down[0], hidden, (((0,), (1,)), ((), ())), preferred_el...  16.1 us
    unnamed x21, local copies, waits for them, and re-layouts  12.6 us
    all_to_all x2, starting transfers between devices, per_device(): lax.all_to_all(summed, expert_axes, split_axis=1, concat_axis=1, tiled=True)  11.5 us
    gather x5, local copies, waits for them, and re-layouts, pair_weights(): picked = jnp.take_along_axis(logits, choice_ids, axis=1)  7.15 us
    all_to_all x2, waiting for transfers between devices, per_device(): lax.all_to_all(summed, expert_axes, split_axis=1, concat_axis=1, tiled=True)  5.75 us
  transfers between devices with their start and end apart: 6, of which 4 were waited for; matrix products, arithmetic and copies ran while one was open for 12% of the time, Pallas kernels for 0%

profile of v2, /device:TPU:2, one launch (start us, length us, event | category | flops | bytes accessed | tf_op | source)
XLA Modules:
  0.0 241.3 jit_solution(11559449472173752603)
XLA Ops:
  12.5 4.1 %convolution_convert_fusion = bf16[1536,2048]{1,0:T(8,128)(2,1)S(1)} fusion(s32[512]{0:T(512)S(1)} %bitcast.61, s32[512]{0:T(512)S(1)} %bitcast.63, f32[2048]{0:T(1024)S(1)} %copy-done.7, f32[512]{0:T(512)S(1)} %add_rsqrt_fusion, bf16[512,2048]{1,0:T(8,128)(2,1)S(1)} %copy-done.1), kind=kOutput, calls=%fused_computation.1 | convolution fusion | flops 3230924800 | bytes 8402944 | tf_op jit(solution)/shard_map/dot_general | solution.py:49
  16.6 2.5 %fusion.52 = (bf16[8,96,2048]{2,1,0:T(8,128)(2,1)S(1)}, bf16[8,96,2048]{2,1,0:T(8,128)(2,1)}) fusion(bf16[8,192,2048]{2,1,0:T(8,128)(2,1)S(1)} %bitcast.54), kind=kLoop, calls=%fused_computation.60 | loop fusion | bytes 12582912 | tf_op jit(solution)/shard_map/slice | solution.py:54
  19.2 43.0 %all_to_all.20 = bf16[8,96,2048]{2,1,0:T(8,128)(2,1)S(1)} all-to-all(bf16[8,96,2048]{2,1,0:T(8,128)(2,1)S(1)} %get-tuple-element.7), channel_id=1, replica_groups=mesh['dp'=2,'ey'=4,'ex'=2,'mz'=8,'mx'=2] {'ey','ex'}, dimensions={0} | all-to-all | bytes 6291456 | tf_op jit(solution)/shard_map/all_to_all | solution.py:55
  62.1 1.7 copy-done.2
  63.8 2.4 fusion.19
  66.2 8.0 %fusion.5 = bf16[2048,768]{0,1:T(8,128)(2,1)} fusion(bf16[1,352,2048]{2,1,0:T(8,128)(2,1)S(1)} %copy-done, bf16[768,2048]{1,0:T(8,128)(2,1)} %bitcast.56, bf16[1,2048,352]{1,2,0:T(8,128)(2,1)} %param.12, f32[768,352]{0,1:T(8,128)} %fusion.19), kind=kOutput, calls=%fused_computation.15 | convolution fusion | flops 2217787392 | bytes 10256384 | tf_op jit(solution)/shard_map/dot_general | solution.py:60
  74.3 41.3 %all_to_all.21 = bf16[8,96,2048]{2,1,0:T(8,128)(2,1)S(1)} all-to-all(bf16[8,96,2048]{2,1,0:T(8,128)(2,1)} %get-tuple-element.8), channel_id=1, replica_groups=mesh['dp'=2,'ey'=4,'ex'=2,'mz'=8,'mx'=2] {'ey','ex'}, dimensions={0} | all-to-all | bytes 6291456 | tf_op jit(solution)/shard_map/all_to_all | solution.py:55
  115.7 1.7 copy-done.3
  117.4 2.3 fusion.17
  119.7 8.1 %fusion.6 = bf16[2048,768]{0,1:T(8,128)(2,1)} fusion(bf16[1,352,2048]{2,1,0:T(8,128)(2,1)S(1)} %copy-done, bf16[768,2048]{1,0:T(8,128)(2,1)} %bitcast.58, bf16[1,2048,352]{1,2,0:T(8,128)(2,1)} %param.12, f32[768,352]{0,1:T(8,128)} %fusion.17), kind=kOutput, calls=%fused_computation.16 | convolution fusion | flops 2217787392 | bytes 10256384 | tf_op jit(solution)/shard_map/dot_general | solution.py:60
  127.9 1.9 copy.36
  129.9 46.3 %reduce-scatter.11.cloned.1.call-done = bf16[256,768]{0,1:T(8,128)(2,1)} async-done(((bf16[2048,768]{0,1:T(8,128)(2,1)}), bf16[256,768]{0,1:T(8,128)(2,1)}) %reduce-scatter.11.cloned.1.call-update) | async-done | bytes 393232 | tf_op jit(solution)/shard_map/reduce_scatter | solution.py:65
  176.1 1.9 copy.38
  178.1 2.5 %convert_element_type.47 = f32[512,2048]{1,0:T(8,128)} convert(bf16[512,2048]{1,0:T(8,128)(2,1)S(1)} %copy-done.1) | non-fusion elementwise | flops 1048576 | bytes 6291456 | tf_op jit(solution)/shard_map/convert_element_type | solution.py:37
  180.9 2.3 fusion.44
  183.2 6.5 %gather_fusion = f32[1024]{0:T(1024)S(1)} fusion(f32[512,8]{0,1:T(8,128)S(1)} %fusion.44, s32[1024]{0:T(1024)S(1)} %reshape.50), kind=kCustom, calls=%fused_computation | custom fusion | bytes 16384 | tf_op jit(solution)/shard_map/jit(take_along_axis)/gather | solution.py:26
  190.1 6.8 %reduce-scatter.13.cloned.1.call-done = bf16[128,768]{1,0:T(8,128)(2,1)} async-done(((bf16[256,768]{1,0:T(8,128)(2,1)}), bf16[128,768]{1,0:T(8,128)(2,1)}) %reduce-scatter.13.cloned.1.call-update) | async-done | bytes 196624
  196.9 1.7 copy.37
  198.6 5.8 %all-to-all-start.1 = ((bf16[128,8,96]{0,2,1:T(8,128)(2,1)}), bf16[128,8,96]{0,2,1:T(8,128)(2,1)S(1)}, u32[]{:S(2)}, u32[]{:S(2)}) async-start(bf16[128,8,96]{0,2,1:T(8,128)(2,1)} %bitcast.8), calls=%async_computation.2 | async-start | bytes 393216 | tf_op jit(solution)/shard_map/all_to_all | solution.py:68
  204.4 14.1 %reduce-scatter.15.cloned.1.call-done = bf16[128,768]{1,0:T(8,128)(2,1)} async-done(((bf16[256,768]{1,0:T(8,128)(2,1)}), bf16[128,768]{1,0:T(8,128)(2,1)}) %reduce-scatter.15.cloned.1.call-update) | async-done | bytes 196624
  218.5 1.7 copy.39
  220.3 5.8 %all-to-all-start.3 = ((bf16[128,8,96]{0,2,1:T(8,128)(2,1)}), bf16[128,8,96]{0,2,1:T(8,128)(2,1)S(1)}, u32[]{:S(2)}, u32[]{:S(2)}) async-start(bf16[128,8,96]{0,2,1:T(8,128)(2,1)} %bitcast.11), calls=%async_computation.5 | async-start | bytes 393216 | tf_op jit(solution)/shard_map/all_to_all | solution.py:68
  226.0 5.8 %all-to-all-done.3 = bf16[128,8,96]{0,2,1:T(8,128)(2,1)S(1)} async-done(((bf16[128,8,96]{0,2,1:T(8,128)(2,1)}), bf16[128,8,96]{0,2,1:T(8,128)(2,1)S(1)}, u32[]{:S(2)}, u32[]{:S(2)}) %all-to-all-start.3) | async-done | bytes 196640 | tf_op jit(solution)/shard_map/all_to_all | solution.py:68
  232.5 2.3 fusion.37
  (43 shorter events, 7.5 us)
Async XLA Ops:
  6.5 59.7 %copy-start = (bf16[1,352,2048]{2,1,0:T(8,128)(2,1)S(1)}, bf16[1,352,2048]{2,1,0:T(8,128)(2,1)}, u32[]{:S(2)}) copy-start(bf16[1,352,2048]{2,1,0:T(8,128)(2,1)} %param.13) | copy-start | bytes 4325380
  6.5 5.3 %copy-start.4 = (s32[512,2]{0,1:T(2,128)S(1)}, s32[512,2]{0,1:T(2,128)}, u32[]{:S(2)}) copy-start(s32[512,2]{0,1:T(2,128)} %param.10) | copy-start | bytes 12292
  6.5 5.3 %copy-start.1 = (bf16[512,2048]{1,0:T(8,128)(2,1)S(1)}, bf16[512,2048]{1,0:T(8,128)(2,1)}, u32[]{:S(2)}) copy-start(bf16[512,2048]{1,0:T(8,128)(2,1)} %param.7) | copy-start | bytes 6291460
  6.5 121.3 %reduce-scatter.9.cloned.1.call-start = ((), (), s32[]{:S(2)}) async-start(), calls=%async_computation.8 | async-start | bytes 3538944 | tf_op jit(solution)/shard_map/reduce_scatter | solution.py:65
  11.8 0.7 copy-start.7
  19.2 44.7 %copy-start.5 = (bf16[1,2048,352]{1,2,0:T(8,128)(2,1)S(1)}, bf16[1,2048,352]{1,2,0:T(8,128)(2,1)}, u32[]{:S(2)}) copy-start(bf16[1,2048,352]{1,2,0:T(8,128)(2,1)} %param.11) | copy-start | bytes 4325380
  62.1 1.7 copy-start.2
  74.2 101.9 %reduce-scatter.11.cloned.1.call-start = ((), (), s32[]{:S(2)}) async-start(), calls=%async_computation.9 | async-start | bytes 3538944 | tf_op jit(solution)/shard_map/reduce_scatter | solution.py:65
  74.3 43.1 %copy-start.6 = (bf16[1,2048,352]{1,2,0:T(8,128)(2,1)S(1)}, bf16[1,2048,352]{1,2,0:T(8,128)(2,1)}, u32[]{:S(2)}) copy-start(bf16[1,2048,352]{1,2,0:T(8,128)(2,1)} %param.11) | copy-start | bytes 4325380
  115.7 1.7 copy-start.3
  127.8 69.1 %reduce-scatter.13.cloned.1.call-start = ((), (), s32[]{:S(2)}) async-start(), calls=%async_computation.10 | async-start | bytes 589824
  129.8 88.7 %reduce-scatter.15.cloned.1.call-start = ((), (), s32[]{:S(2)}) async-start(), calls=%async_computation.11 | async-start | bytes 589824
  198.6 21.6 %all-to-all-start.1 = ((bf16[128,8,96]{0,2,1:T(8,128)(2,1)}), bf16[128,8,96]{0,2,1:T(8,128)(2,1)S(1)}, u32[]{:S(2)}, u32[]{:S(2)}) async-start(bf16[128,8,96]{0,2,1:T(8,128)(2,1)} %bitcast.8), calls=%async_computation.2 | async-start | bytes 393216 | tf_op jit(solution)/shard_map/all_to_all | solution.py:68
  220.3 11.5 %all-to-all-start.3 = ((bf16[128,8,96]{0,2,1:T(8,128)(2,1)}), bf16[128,8,96]{0,2,1:T(8,128)(2,1)S(1)}, u32[]{:S(2)}, u32[]{:S(2)}) async-start(bf16[128,8,96]{0,2,1:T(8,128)(2,1)} %bitcast.11), calls=%async_computation.5 | async-start | bytes 393216 | tf_op jit(solution)/shard_map/all_to_all | solution.py:68
Sparse Core Ops, SparseCore 0:
  74.4 48.5 reduce-scatter.8
  127.9 48.1 reduce-scatter.10
  178.6 18.2 reduce-scatter.12
  199.2 19.2 reduce-scatter.14

commit v3 on v2

--- a/solution.py
+++ b/solution.py
@@ -26,6 +26,18 @@
     picked = jnp.take_along_axis(logits, choice_ids, axis=1)
     first_weight = jax.nn.sigmoid(picked[:, 0] - picked[:, 1])
     return jnp.stack([first_weight, 1.0 - first_weight], axis=1)
+
+
+def pair_exchange(summed, axis):
+    n = lax.axis_size(axis)
+    if n == 1:
+        return summed
+    own = lax.axis_index(axis)
+    width = summed.shape[0] // 2
+    keep = lax.dynamic_slice_in_dim(summed, own * width, width, 0)
+    give = lax.dynamic_slice_in_dim(summed, (1 - own) * width, width, 0)
+    got = lax.ppermute(give, axis, [(0, 1), (1, 0)])
+    return (keep.astype(jnp.float32) + got.astype(jnp.float32)).astype(jnp.bfloat16)
 
 
 def make_per_device(expert_axes, mp_axes, experts, mp_count, n_chunks=2):
@@ -60,9 +72,8 @@
             partial_t = lax.dot_general(
                 w_down[0], hidden, (((0,), (1,)), ((), ())), preferred_element_type=jnp.float32
             ).astype(jnp.bfloat16)
-            summed = partial_t
-            for axis in mp_axes:
-                summed = lax.psum_scatter(summed, axis, scatter_dimension=0, tiled=True)
+            summed = lax.psum_scatter(partial_t, mp_axes[0], scatter_dimension=0, tiled=True)
+            summed = pair_exchange(summed, mp_axes[1])
             summed = summed.reshape(slice_width, experts, chunk)
             pieces.append(
                 lax.all_to_all(summed, expert_axes, split_axis=1, concat_axis=1, tiled=True)

time: 242 us -> 213 us (0.88)
  waiting for transfers between devices: 73.1 us -> 41 us
  local copies, waits for them, and re-layouts: 25.4 us -> 20.3 us
  other arithmetic: 3.04 us -> 7.11 us
  starting transfers between devices: 11.7 us -> 14.8 us
    unnamed x6 -> x2, waiting for transfers between devices: 21 us -> 0.03 us
    reduce_scatter x2, waiting for transfers between devices: 46.3 us -> 31.1 us  [per_device(): lax.psum_scatter(partial_t, mp_axes[0], scatter_dimension=0, tiled=True)]
    unnamed x21, local copies, waits for them, and re-layouts: 12.6 us -> 5.66 us
    ppermute x0 -> x2, starting transfers between devices: none -> 4.42 us  [pair_exchange(): got = lax.ppermute(give, axis, [(0, 1), (1, 0)])]
    all_to_all x2, waiting for transfers between devices: 5.75 us -> 9.88 us  [per_device(): lax.all_to_all(summed, expert_axes, split_axis=1, concat_axis=1, tiled=True)]
  transfers between devices with their start and end apart: 6 -> 6, of which waited for: 4 -> 3; matrix products, arithmetic and copies ran while one was open for 12% -> 13% of each run, Pallas kernels for 0% -> 0%
where the time goes in v3:
time: 213 us; the launch traced here: 212 us
  blocking collectives  84.2 us (40%)
  waiting for transfers between devices  41 us (19%)
  matrix products  30.9 us (15%)
  local copies, waits for them, and re-layouts  20.3 us (10%)
  starting transfers between devices  14.8 us (7%)
  between operations  13.5 us (6%)
  other arithmetic  7.11 us (3%)
    all_to_all x2, blocking collectives, per_device(): lax.all_to_all(part, expert_axes, split_axis=0, concat_axis=0, tiled=True)  84.2 us
    reduce_scatter x2, waiting for transfers between devices, per_device(): lax.psum_scatter(partial_t, mp_axes[0], scatter_dimension=0, tiled=True)  31.1 us
    dot_general x2, matrix products, per_device(): lax.dot_general(w_down[0], hidden, (((0,), (1,)), ((), ())), preferred_el...  16.2 us
    all_to_all x2, starting transfers between devices, per_device(): lax.all_to_all(summed, expert_axes, split_axis=1, concat_axis=1, tiled=True)  10.3 us
    all_to_all x2, waiting for transfers between devices, per_device(): lax.all_to_all(summed, expert_axes, split_axis=1, concat_axis=1, tiled=True)  9.88 us
    gather x5, local copies, waits for them, and re-layouts, pair_weights(): picked = jnp.take_along_axis(logits, choice_ids, axis=1)  7.15 us
    unnamed x21, local copies, waits for them, and re-layouts  5.66 us
    dot_general x2, matrix products, per_device(): jnp.dot(expert_rows, w_gate[0], preferred_element_type=jnp.float32)  4.81 us
  transfers between devices with their start and end apart: 6, of which 3 were waited for; matrix products, arithmetic and copies ran while one was open for 13% of the time, Pallas kernels for 0%

profile of v3, /device:TPU:2, one launch (start us, length us, event | category | flops | bytes accessed | tf_op | source)
XLA Modules:
  0.0 211.8 jit_solution(18163104470064570233)
XLA Ops:
  6.5 1.7 copy.24
  8.2 1.1 eq.71
  12.5 4.1 %convolution_convert_fusion = bf16[1536,2048]{1,0:T(8,128)(2,1)S(1)} fusion(s32[512]{0:T(512)S(1)} %bitcast.59, s32[512]{0:T(512)S(1)} %bitcast.61, f32[2048]{0:T(1024)S(1)} %copy-done.8, f32[512]{0:T(512)S(1)} %add_rsqrt_fusion, bf16[512,2048]{1,0:T(8,128)(2,1)S(1)} %copy-done.1), kind=kOutput, calls=%fused_computation.1 | convolution fusion | flops 3230924800 | bytes 8402944 | tf_op jit(solution)/shard_map/dot_general | solution.py:61
  16.6 2.6 %fusion.52 = (bf16[8,96,2048]{2,1,0:T(8,128)(2,1)}, bf16[8,96,2048]{2,1,0:T(8,128)(2,1)S(1)}) fusion(bf16[8,192,2048]{2,1,0:T(8,128)(2,1)S(1)} %bitcast.52), kind=kLoop, calls=%fused_computation.64 | loop fusion | bytes 12582912 | tf_op jit(solution)/shard_map/slice | solution.py:66
  19.2 43.0 %all_to_all.20 = bf16[8,96,2048]{2,1,0:T(8,128)(2,1)S(1)} all-to-all(bf16[8,96,2048]{2,1,0:T(8,128)(2,1)S(1)} %get-tuple-element.8), channel_id=1, replica_groups=mesh['dp'=2,'ey'=4,'ex'=2,'mz'=8,'mx'=2] {'ey','ex'}, dimensions={0} | all-to-all | bytes 6291456 | tf_op jit(solution)/shard_map/all_to_all | solution.py:67
  62.1 1.7 copy-done.2
  63.9 2.4 %fusion.17 = f32[768,352]{0,1:T(8,128)} fusion(bf16[768,2048]{1,0:T(8,128)(2,1)S(1)} %bitcast.53, bf16[1,2048,352]{1,2,0:T(8,128)(2,1)S(1)} %copy-done.6), kind=kOutput, calls=%fused_computation.27 | convolution fusion | flops 1107296256 | bytes 5668864 | tf_op jit(solution)/shard_map/dot_general | solution.py:69
  66.3 8.0 %fusion.6 = bf16[2048,768]{0,1:T(8,128)(2,1)} fusion(bf16[1,352,2048]{2,1,0:T(8,128)(2,1)S(1)} %copy-done, bf16[768,2048]{1,0:T(8,128)(2,1)} %bitcast.54, bf16[1,2048,352]{1,2,0:T(8,128)(2,1)} %param.12, f32[768,352]{0,1:T(8,128)} %fusion.17), kind=kOutput, calls=%fused_computation.16 | convolution fusion | flops 2217787392 | bytes 10256384 | tf_op jit(solution)/shard_map/dot_general | solution.py:72
  74.4 41.2 %all_to_all.21 = bf16[8,96,2048]{2,1,0:T(8,128)(2,1)S(1)} all-to-all(bf16[8,96,2048]{2,1,0:T(8,128)(2,1)} %get-tuple-element.7), channel_id=1, replica_groups=mesh['dp'=2,'ey'=4,'ex'=2,'mz'=8,'mx'=2] {'ey','ex'}, dimensions={0} | all-to-all | bytes 6291456 | tf_op jit(solution)/shard_map/all_to_all | solution.py:67
  115.6 1.7 copy-done.3
  117.3 2.4 %fusion.19 = f32[768,352]{0,1:T(8,128)} fusion(bf16[768,2048]{1,0:T(8,128)(2,1)S(1)} %bitcast.55, bf16[1,2048,352]{1,2,0:T(8,128)(2,1)S(1)} %copy-done.6), kind=kOutput, calls=%fused_computation.29 | convolution fusion | flops 1107296256 | bytes 5668864 | tf_op jit(solution)/shard_map/dot_general | solution.py:69
  119.7 8.2 %fusion.5 = bf16[2048,768]{0,1:T(8,128)(2,1)} fusion(bf16[1,352,2048]{2,1,0:T(8,128)(2,1)S(1)} %copy-done, bf16[768,2048]{1,0:T(8,128)(2,1)} %bitcast.56, bf16[1,2048,352]{1,2,0:T(8,128)(2,1)} %param.12, f32[768,352]{0,1:T(8,128)} %fusion.19), kind=kOutput, calls=%fused_computation.15 | convolution fusion | flops 2217787392 | bytes 10256384 | tf_op jit(solution)/shard_map/dot_general | solution.py:72
  128.6 2.3 %fusion.44 = f32[512,8]{0,1:T(8,128)S(1)} fusion(bf16[2048,8]{0,1:T(8,128)(2,1)S(1)} %copy-done.7, f32[2048]{0:T(1024)S(1)} %copy-done.9, f32[512]{0:T(512)S(1)} %add_rsqrt_fusion, bf16[512,2048]{1,0:T(8,128)(2,1)} %param.7), kind=kOutput, calls=%fused_computation.42 | convolution fusion | flops 20971520 | bytes 2156544 | tf_op jit(solution)/shard_map/dot_general | solution.py:25
  130.9 6.5 %gather_fusion = f32[1024]{0:T(1024)S(1)} fusion(f32[512,8]{0,1:T(8,128)S(1)} %fusion.44, s32[1024]{0:T(1024)S(1)} %reshape.50), kind=kCustom, calls=%fused_computation | custom fusion | bytes 16384 | tf_op jit(solution)/shard_map/jit(take_along_axis)/gather | solution.py:26
  138.7 2.2 %collective-permute-start.1 = (bf16[128,768]{0,1:T(8,128)(2,1)S(1)}, bf16[128,768]{0,1:T(8,128)(2,1)S(1)}, u32[]{:S(2)}, u32[]{:S(2)}) collective-permute-start(bf16[128,768]{0,1:T(8,128)(2,1)S(1)} %constant_dynamic-slice_fusion), channel_id=1, source_target_pairs={{0,1},{1,0},{2,3},{3,2},{4,5},{5,4},{6,7},{7,6},{8,9},{9,8},{10,11... | collective-permute-start | bytes 589832 | tf_op jit(solution)/shard_map/ppermute | solution.py:39
  140.9 4.1 %convert_element_type.65 = f32[512,2048]{1,0:T(8,128)} convert(bf16[512,2048]{1,0:T(8,128)(2,1)} %param.7) | non-fusion elementwise | flops 1048576 | bytes 6291456 | tf_op jit(solution)/shard_map/convert_element_type | solution.py:49
  145.1 31.1 %reduce-scatter.3.cloned.1.call-done = bf16[256,768]{0,1:T(8,128)(2,1)} async-done(((bf16[2048,768]{0,1:T(8,128)(2,1)}), bf16[256,768]{0,1:T(8,128)(2,1)}) %reduce-scatter.3.cloned.1.call-update) | async-done | bytes 393232 | tf_op jit(solution)/shard_map/reduce_scatter | solution.py:75
  177.1 2.2 %collective-permute-start = (bf16[128,768]{0,1:T(8,128)(2,1)S(1)}, bf16[128,768]{0,1:T(8,128)(2,1)S(1)}, u32[]{:S(2)}, u32[]{:S(2)}) collective-permute-start(bf16[128,768]{0,1:T(8,128)(2,1)S(1)} %constant_dynamic-slice_fusion.1), channel_id=1, source_target_pairs={{0,1},{1,0},{2,3},{3,2},{4,5},{5,4},{6,7},{7,6},{8,9},{9,8},{10,11... | collective-permute-start | bytes 589832 | tf_op jit(solution)/shard_map/ppermute | solution.py:39
  180.1 5.8 %all-to-all-start.3 = ((bf16[128,8,96]{0,2,1:T(8,128)(2,1)}), bf16[128,8,96]{0,2,1:T(8,128)(2,1)S(1)}, u32[]{:S(2)}, u32[]{:S(2)}) async-start(bf16[128,8,96]{0,2,1:T(8,128)(2,1)} %bitcast.11), calls=%async_computation.5 | async-start | bytes 393216 | tf_op jit(solution)/shard_map/all_to_all | solution.py:79
  185.9 1.7 add_convert_fusion.1
  187.5 4.1 %all-to-all-done.3 = bf16[128,8,96]{0,2,1:T(8,128)(2,1)S(1)} async-done(((bf16[128,8,96]{0,2,1:T(8,128)(2,1)}), bf16[128,8,96]{0,2,1:T(8,128)(2,1)S(1)}, u32[]{:S(2)}, u32[]{:S(2)}) %all-to-all-start.3) | async-done | bytes 196640 | tf_op jit(solution)/shard_map/all_to_all | solution.py:79
  191.7 4.5 %all-to-all-start.1 = ((bf16[128,8,96]{0,2,1:T(8,128)(2,1)}), bf16[128,8,96]{0,2,1:T(8,128)(2,1)S(1)}, u32[]{:S(2)}, u32[]{:S(2)}) async-start(bf16[128,8,96]{0,2,1:T(8,128)(2,1)} %bitcast.8), calls=%async_computation.2 | async-start | bytes 393216 | tf_op jit(solution)/shard_map/all_to_all | solution.py:79
  196.2 5.8 %all-to-all-done.1 = bf16[128,8,96]{0,2,1:T(8,128)(2,1)S(1)} async-done(((bf16[128,8,96]{0,2,1:T(8,128)(2,1)}), bf16[128,8,96]{0,2,1:T(8,128)(2,1)S(1)}, u32[]{:S(2)}, u32[]{:S(2)}) %all-to-all-start.1) | async-done | bytes 196640 | tf_op jit(solution)/shard_map/all_to_all | solution.py:79
  202.7 2.3 %fusion.37 = bf16[512,128]{1,0:T(8,128)(2,1)} fusion(f32[512,128]{1,0:T(8,128)S(1)} %fusion.35, bf16[128,1536]{0,1:T(8,128)(2,1)S(1)} %bitcast.58, s32[512]{0:T(512)S(1)} %bitcast.60, f32[512,2048]{1,0:T(8,128)} %convert_element_type.65, s32[]{:T(128)S(6)} %select_n.19, f32[512]{0:T(512)S(1)} %bitcast.63), kind=kOutput, calls=%fused_computation.39 | convolution fusion | flops 202375168 | bytes 1052676 | tf_op jit(solution)/shard_map/dot_general | solution.py:88
  (45 shorter events, 7.6 us)
Async XLA Ops:
  6.5 59.7 %copy-start = (bf16[1,352,2048]{2,1,0:T(8,128)(2,1)S(1)}, bf16[1,352,2048]{2,1,0:T(8,128)(2,1)}, u32[]{:S(2)}) copy-start(bf16[1,352,2048]{2,1,0:T(8,128)(2,1)} %param.13) | copy-start | bytes 4325380
  6.5 5.3 %copy-start.5 = (s32[512,2]{0,1:T(2,128)S(1)}, s32[512,2]{0,1:T(2,128)}, u32[]{:S(2)}) copy-start(s32[512,2]{0,1:T(2,128)} %param.10) | copy-start | bytes 12292
  6.5 5.3 %copy-start.1 = (bf16[512,2048]{1,0:T(8,128)(2,1)S(1)}, bf16[512,2048]{1,0:T(8,128)(2,1)}, u32[]{:S(2)}) copy-start(bf16[512,2048]{1,0:T(8,128)(2,1)} %param.7) | copy-start | bytes 6291460
  6.5 131.2 %reduce-scatter.5.cloned.1.call-start = ((), (), s32[]{:S(2)}) async-start(), calls=%async_computation.7 | async-start | bytes 3538944 | tf_op jit(solution)/shard_map/reduce_scatter | solution.py:75
  11.8 0.7 copy-start.8
  19.2 44.7 %copy-start.6 = (bf16[1,2048,352]{1,2,0:T(8,128)(2,1)S(1)}, bf16[1,2048,352]{1,2,0:T(8,128)(2,1)}, u32[]{:S(2)}) copy-start(bf16[1,2048,352]{1,2,0:T(8,128)(2,1)} %param.11) | copy-start | bytes 4325380
  62.1 1.7 copy-start.2
  74.3 101.9 %reduce-scatter.3.cloned.1.call-start = ((), (), s32[]{:S(2)}) async-start(), calls=%async_computation.6 | async-start | bytes 3538944 | tf_op jit(solution)/shard_map/reduce_scatter | solution.py:75
  115.6 1.7 copy-start.3
  127.8 0.8 copy-start.7
  127.8 0.8 copy-start.9
  138.7 40.6 %collective-permute-start.1 = (bf16[128,768]{0,1:T(8,128)(2,1)S(1)}, bf16[128,768]{0,1:T(8,128)(2,1)S(1)}, u32[]{:S(2)}, u32[]{:S(2)}) collective-permute-start(bf16[128,768]{0,1:T(8,128)(2,1)S(1)} %constant_dynamic-slice_fusion), channel_id=1, source_target_pairs={{0,1},{1,0},{2,3},{3,2},{4,5},{5,4},{6,7},{7,6},{8,9},{9,8},{10,11... | collective-permute-start | bytes 589832 | tf_op jit(solution)/shard_map/ppermute | solution.py:39
  140.9 38.4 %copy-start.4 = (bf16[256,768]{0,1:T(8,128)(2,1)S(1)}, bf16[256,768]{0,1:T(8,128)(2,1)}, u32[]{:S(2)}) copy-start(bf16[256,768]{0,1:T(8,128)(2,1)} %reduce-scatter.5.cloned.1.call-done) | copy-start | bytes 1179652
  177.1 8.8 %collective-permute-start = (bf16[128,768]{0,1:T(8,128)(2,1)S(1)}, bf16[128,768]{0,1:T(8,128)(2,1)S(1)}, u32[]{:S(2)}, u32[]{:S(2)}) collective-permute-start(bf16[128,768]{0,1:T(8,128)(2,1)S(1)} %constant_dynamic-slice_fusion.1), channel_id=1, source_target_pairs={{0,1},{1,0},{2,3},{3,2},{4,5},{5,4},{6,7},{7,6},{8,9},{9,8},{10,11... | collective-permute-start | bytes 589832 | tf_op jit(solution)/shard_map/ppermute | solution.py:39
  180.1 11.6 %all-to-all-start.3 = ((bf16[128,8,96]{0,2,1:T(8,128)(2,1)}), bf16[128,8,96]{0,2,1:T(8,128)(2,1)S(1)}, u32[]{:S(2)}, u32[]{:S(2)}) async-start(bf16[128,8,96]{0,2,1:T(8,128)(2,1)} %bitcast.11), calls=%async_computation.5 | async-start | bytes 393216 | tf_op jit(solution)/shard_map/all_to_all | solution.py:79
  191.7 10.3 %all-to-all-start.1 = ((bf16[128,8,96]{0,2,1:T(8,128)(2,1)}), bf16[128,8,96]{0,2,1:T(8,128)(2,1)S(1)}, u32[]{:S(2)}, u32[]{:S(2)}) async-start(bf16[128,8,96]{0,2,1:T(8,128)(2,1)} %bitcast.8), calls=%async_computation.2 | async-start | bytes 393216 | tf_op jit(solution)/shard_map/all_to_all | solution.py:79
Sparse Core Ops, SparseCore 0:
  74.4 48.5 reduce-scatter.4
  128.0 48.1 reduce-scatter.2

commit v4 on v3

--- a/solution.py
+++ b/solution.py
@@ -9,23 +9,25 @@
 eps_norm = 1e-06
 
 
-def pair_rows(choices, experts, capacity):
-    flat_ids = choices.reshape(-1)
-    pairs = flat_ids.shape[0]
-    onehot = (flat_ids[:, None] == jnp.arange(experts, dtype=jnp.int32)[None, :]).astype(jnp.bfloat16)
-    before = (
-        jnp.arange(pairs, dtype=jnp.int32)[None, :] < jnp.arange(pairs, dtype=jnp.int32)[:, None]
+def pair_slots(choices, experts):
+    tokens = choices.shape[0]
+    ids = jnp.arange(experts, dtype=jnp.int32)[None, :]
+    oh0 = (choices[:, 0:1] == ids).astype(jnp.float32)
+    oh1 = (choices[:, 1:2] == ids).astype(jnp.float32)
+    tri = (
+        jnp.arange(tokens, dtype=jnp.int32)[None, :] < jnp.arange(tokens, dtype=jnp.int32)[:, None]
     ).astype(jnp.bfloat16)
-    earlier = jnp.dot(before, onehot, preferred_element_type=jnp.float32)
-    slot_ids = jnp.sum(earlier * onehot.astype(jnp.float32), axis=1).astype(jnp.int32)
-    return (flat_ids * capacity + slot_ids).reshape(-1, 2)
+    cnt = jnp.dot(tri, (oh0 + oh1).astype(jnp.bfloat16), preferred_element_type=jnp.float32)
+    slot0 = jnp.sum(cnt * oh0, axis=1)
+    slot1 = jnp.sum((cnt + oh0) * oh1, axis=1)
+    return slot0.astype(jnp.int32), slot1.astype(jnp.int32), oh0, oh1
 
 
-def pair_weights(normed, router_w, choice_ids):
-    logits = jnp.dot(normed, router_w, preferred_element_type=jnp.float32)
-    picked = jnp.take_along_axis(logits, choice_ids, axis=1)
-    first_weight = jax.nn.sigmoid(picked[:, 0] - picked[:, 1])
-    return jnp.stack([first_weight, 1.0 - first_weight], axis=1)
+def pair_weights(logits, oh0, oh1):
+    picked0 = jnp.sum(logits * oh0, axis=1)
+    picked1 = jnp.sum(logits * oh1, axis=1)
+    first_weight = jax.nn.sigmoid(picked0 - picked1)
+    return first_weight, 1.0 - first_weight
 
 
 def pair_exchange(summed, axis):
@@ -52,18 +54,22 @@
             * lax.rsqrt(jnp.mean(wide_in * wide_in, axis=1, keepdims=True) + eps_norm)
             * norm_gain
         ).astype(jnp.bfloat16)
-        weights = pair_weights(normed, router_w, choices)
-        rows = pair_rows(choices, experts, capacity)
-        slots = jnp.arange(rows_total, dtype=jnp.int32)
-        pick0 = rows[:, 0][None, :] == slots[:, None]
-        pick1 = rows[:, 1][None, :] == slots[:, None]
-        dispatch = (pick0 | pick1).astype(jnp.bfloat16)
-        buffer = jnp.dot(dispatch, normed, preferred_element_type=jnp.float32).astype(jnp.bfloat16)
-        buffer = buffer.reshape(experts, capacity, model_width)
+        slot0, slot1, oh0, oh1 = pair_slots(choices, experts)
         chunk = capacity // n_chunks
-        pieces = []
+        e0, e1 = choices[:, 0], choices[:, 1]
+        chunk_rows = jnp.arange(experts * chunk, dtype=jnp.int32)
+        column = lax.axis_index(mp_axes) * slice_width
+        residual = lax.dynamic_slice_in_dim(wide_in, column, slice_width, 1)
+        mixture = None
+        results = []
         for c in range(n_chunks):
-            part = buffer[:, c * chunk:(c + 1) * chunk]
+            r0 = jnp.where(slot0 // chunk == c, e0 * chunk + slot0 % chunk, -1)
+            r1 = jnp.where(slot1 // chunk == c, e1 * chunk + slot1 % chunk, -1)
+            dispatch = (
+                (r0[None, :] == chunk_rows[:, None]) | (r1[None, :] == chunk_rows[:, None])
+            ).astype(jnp.bfloat16)
+            part = jnp.dot(dispatch, normed, preferred_element_type=jnp.float32).astype(jnp.bfloat16)
+            part = part.reshape(experts, chunk, model_width)
             arrived = lax.all_to_all(part, expert_axes, split_axis=0, concat_axis=0, tiled=True)
             expert_rows = arrived.reshape(experts * chunk, model_width)
             gate_proj = jnp.dot(expert_rows, w_gate[0], preferred_element_type=jnp.float32)
@@ -75,18 +81,19 @@
             summed = lax.psum_scatter(partial_t, mp_axes[0], scatter_dimension=0, tiled=True)
             summed = pair_exchange(summed, mp_axes[1])
             summed = summed.reshape(slice_width, experts, chunk)
-            pieces.append(
-                lax.all_to_all(summed, expert_axes, split_axis=1, concat_axis=1, tiled=True)
-            )
-        returned = jnp.concatenate(pieces, axis=2).reshape(slice_width, rows_total)
-        column = lax.axis_index(mp_axes) * slice_width
-        residual = lax.dynamic_slice_in_dim(wide_in, column, slice_width, 1)
-        sel0 = (rows[:, 0][:, None] == slots[None, :]).astype(jnp.bfloat16)
-        sel1 = (rows[:, 1][:, None] == slots[None, :]).astype(jnp.bfloat16)
+            returned = lax.all_to_all(summed, expert_axes, split_axis=1, concat_axis=1, tiled=True)
+            returned = returned.reshape(slice_width, experts * chunk)
+            results.append((r0, r1, returned))
+        logits = jnp.dot(normed, router_w, preferred_element_type=jnp.float32)
+        w0, w1 = pair_weights(logits, oh0, oh1)
         dims = (((1,), (1,)), ((), ()))
-        out0 = lax.dot_general(sel0, returned, dims, preferred_element_type=jnp.float32)
-        out1 = lax.dot_general(sel1, returned, dims, preferred_element_type=jnp.float32)
-        mixture = out0 * weights[:, 0:1] + out1 * weights[:, 1:2]
+        for r0, r1, returned in results:
+            sel0 = (r0[:, None] == chunk_rows[None, :]).astype(jnp.bfloat16)
+            sel1 = (r1[:, None] == chunk_rows[None, :]).astype(jnp.bfloat16)
+            out0 = lax.dot_general(sel0, returned, dims, preferred_element_type=jnp.float32)
+            out1 = lax.dot_general(sel1, returned, dims, preferred_element_type=jnp.float32)
+            term = out0 * w0[:, None] + out1 * w1[:, None]
+            mixture = term if mixture is None else mixture + term
         return (residual + mixture).astype(jnp.bfloat16)
 
     return per_device

time: 213 us -> 210 us (0.986)
  local copies, waits for them, and re-layouts: 20.3 us -> 7.52 us
  waiting for transfers between devices: 41 us -> 48.3 us
  other arithmetic: 7.11 us -> 11.4 us
    reduce_scatter x2, waiting for transfers between devices: 31.1 us -> 38.8 us  [per_device(): lax.psum_scatter(partial_t, mp_axes[0], scatter_dimension=0, tiled=True)]
    gather x5 -> x0, local copies, waits for them, and re-layouts: 7.15 us -> none  [pair_weights(): picked = jnp.take_along_axis(logits, choice_ids, axis=1)]
    unnamed x21 -> x32, local copies, waits for them, and re-layouts: 5.66 us -> 4.1 us
    dot_general x1 -> x2, matrix products: 4.1 us -> 4.77 us  [per_device(): jnp.dot(dispatch, normed, preferred_element_type=jnp.float32)]
  transfers between devices with their start and end apart: 6 -> 6, of which waited for: 3 -> 3; matrix products, arithmetic and copies ran while one was open for 13% -> 12% of each run, Pallas kernels for 0% -> 0%
where the time goes in v4:
time: 210 us; the launch traced here: 209 us
  blocking collectives  83.2 us (40%)
  waiting for transfers between devices  48.3 us (23%)
  matrix products  30.4 us (14%)
  starting transfers between devices  14.6 us (7%)
  between operations  13.6 us (6%)
  other arithmetic  11.4 us (5%)
  local copies, waits for them, and re-layouts  7.52 us (4%)
    all_to_all x2, blocking collectives, per_device(): lax.all_to_all(part, expert_axes, split_axis=0, concat_axis=0, tiled=True)  83.2 us
    reduce_scatter x2, waiting for transfers between devices, per_device(): lax.psum_scatter(partial_t, mp_axes[0], scatter_dimension=0, tiled=True)  38.8 us
    dot_general x2, matrix products, per_device(): lax.dot_general(w_down[0], hidden, (((0,), (1,)), ((), ())), preferred_el...  16.1 us
    all_to_all x2, starting transfers between devices, per_device(): lax.all_to_all(summed, expert_axes, split_axis=1, concat_axis=1, tiled=True)  10.3 us
    all_to_all x2, waiting for transfers between devices, per_device(): lax.all_to_all(summed, expert_axes, split_axis=1, concat_axis=1, tiled=True)  9.46 us
    dot_general x2, matrix products, per_device(): jnp.dot(dispatch, normed, preferred_element_type=jnp.float32)  4.77 us
    dot_general x2, matrix products, per_device(): jnp.dot(expert_rows, w_gate[0], preferred_element_type=jnp.float32)  4.68 us
    ppermute x2, starting transfers between devices, pair_exchange(): got = lax.ppermute(give, axis, [(0, 1), (1, 0)])  4.3 us
  transfers between devices with their start and end apart: 6, of which 3 were waited for; matrix products, arithmetic and copies ran while one was open for 12% of the time, Pallas kernels for 0%

profile of v4, /device:TPU:2, one launch (start us, length us, event | category | flops | bytes accessed | tf_op | source)
XLA Modules:
  0.0 209.1 jit_solution(11091074428230317658)
XLA Ops:
  7.4 2.1 %multiply_reduce_fusion = f32[512]{0:T(512)S(1)} fusion(bf16[512,2048]{1,0:T(8,128)(2,1)} %param.7), kind=kLoop, calls=%fused_computation.1 | loop fusion | flops 3145216 | bytes 2099200 | tf_op jit(solution)/shard_map/reduce_sum | solution.py:54
  9.9 1.3 select_reduce_fusion
  11.9 2.0 convolution_convert_fusion.1
  13.9 43.0 %all_to_all.20 = bf16[8,96,2048]{2,1,0:T(8,128)(2,1)S(1)} all-to-all(bf16[8,96,2048]{2,1,0:T(8,128)(2,1)S(1)} %bitcast.59), channel_id=1, replica_groups=mesh['dp'=2,'ey'=4,'ex'=2,'mz'=8,'mx'=2] {'ey','ex'}, dimensions={0} | all-to-all | bytes 6291456 | tf_op jit(solution)/shard_map/all_to_all | solution.py:73
  56.9 1.7 copy-done.2
  58.6 2.4 %fusion.16 = f32[768,352]{0,1:T(8,128)} fusion(bf16[768,2048]{1,0:T(8,128)(2,1)S(1)} %bitcast.60, bf16[1,2048,352]{1,2,0:T(8,128)(2,1)S(1)} %copy-done.11), kind=kOutput, calls=%fused_computation.28 | convolution fusion | flops 1107296256 | bytes 5668864 | tf_op jit(solution)/shard_map/dot_general | solution.py:75
  61.0 8.0 %fusion.1 = bf16[2048,768]{0,1:T(8,128)(2,1)} fusion(bf16[1,352,2048]{2,1,0:T(8,128)(2,1)S(1)} %copy-done, bf16[768,2048]{1,0:T(8,128)(2,1)} %bitcast.61, bf16[1,2048,352]{1,2,0:T(8,128)(2,1)} %param.12, f32[768,352]{0,1:T(8,128)} %fusion.16), kind=kOutput, calls=%fused_computation.7 | convolution fusion | flops 2217787392 | bytes 10256384 | tf_op jit(solution)/shard_map/dot_general | solution.py:78
  69.0 2.7 %convolution_convert_fusion.3 = bf16[768,2048]{1,0:T(8,128)(2,1)S(1)} fusion(s32[512]{0:T(512)S(1)} %get-tuple-element.19, s32[512]{0:T(512)S(1)} %get-tuple-element.17, f32[2048]{0:T(1024)} %param.8, f32[512]{0:T(512)S(1)} %add_rsqrt_fusion, bf16[512,2048]{1,0:T(8,128)(2,1)S(1)} %copy-done.1), kind=kOutput, calls=%fused_computation.5 | convolution fusion | flops 1617559552 | bytes 5257216 | tf_op jit(solution)/shard_map/dot_general | solution.py:71
  71.8 40.2 %all_to_all.21 = bf16[8,96,2048]{2,1,0:T(8,128)(2,1)S(1)} all-to-all(bf16[8,96,2048]{2,1,0:T(8,128)(2,1)S(1)} %bitcast.58), channel_id=1, replica_groups=mesh['dp'=2,'ey'=4,'ex'=2,'mz'=8,'mx'=2] {'ey','ex'}, dimensions={0} | all-to-all | bytes 6291456 | tf_op jit(solution)/shard_map/all_to_all | solution.py:73
  112.0 1.7 copy-done.3
  113.7 2.3 %fusion.18 = f32[768,352]{0,1:T(8,128)} fusion(bf16[768,2048]{1,0:T(8,128)(2,1)S(1)} %bitcast.62, bf16[1,2048,352]{1,2,0:T(8,128)(2,1)S(1)} %copy-done.12), kind=kOutput, calls=%fused_computation.30 | convolution fusion | flops 1107296256 | bytes 5668864 | tf_op jit(solution)/shard_map/dot_general | solution.py:75
  116.0 8.1 %fusion = bf16[2048,768]{0,1:T(8,128)(2,1)} fusion(bf16[1,352,2048]{2,1,0:T(8,128)(2,1)S(1)} %copy-done, bf16[768,2048]{1,0:T(8,128)(2,1)} %bitcast.63, bf16[1,2048,352]{1,2,0:T(8,128)(2,1)} %param.12, f32[768,352]{0,1:T(8,128)} %fusion.18), kind=kOutput, calls=%fused_computation.6 | convolution fusion | flops 2217787392 | bytes 10256384 | tf_op jit(solution)/shard_map/dot_general | solution.py:78
  127.4 1.6 constant_dynamic-slice_fusion
  129.1 2.1 %collective-permute-start.1 = (bf16[128,768]{0,1:T(8,128)(2,1)}, bf16[128,768]{0,1:T(8,128)(2,1)}, u32[]{:S(2)}, u32[]{:S(2)}) collective-permute-start(bf16[128,768]{0,1:T(8,128)(2,1)} %constant_dynamic-slice_fusion), channel_id=1, source_target_pairs={{0,1},{1,0},{2,3},{3,2},{4,5},{5,4},{6,7},{7,6},{8,9},{9,8},{10,11... | collective-permute-start | bytes 589832 | tf_op jit(solution)/shard_map/ppermute | solution.py:41
  131.2 2.6 %convert_element_type.117 = f32[512,2048]{1,0:T(8,128)} convert(bf16[512,2048]{1,0:T(8,128)(2,1)S(1)} %copy-done.1) | non-fusion elementwise | flops 1048576 | bytes 6291456 | tf_op jit(solution)/shard_map/convert_element_type | solution.py:51
  133.8 38.8 %reduce-scatter.3.cloned.1.call-done = bf16[256,768]{0,1:T(8,128)(2,1)} async-done(((bf16[2048,768]{0,1:T(8,128)(2,1)}), bf16[256,768]{0,1:T(8,128)(2,1)}) %reduce-scatter.3.cloned.1.call-update) | async-done | bytes 393232 | tf_op jit(solution)/shard_map/reduce_scatter | solution.py:81
  173.5 2.2 %collective-permute-start = (bf16[128,768]{0,1:T(8,128)(2,1)S(1)}, bf16[128,768]{0,1:T(8,128)(2,1)S(1)}, u32[]{:S(2)}, u32[]{:S(2)}) collective-permute-start(bf16[128,768]{0,1:T(8,128)(2,1)S(1)} %constant_dynamic-slice_fusion.1), channel_id=1, source_target_pairs={{0,1},{1,0},{2,3},{3,2},{4,5},{5,4},{6,7},{7,6},{8,9},{9,8},{10,11... | collective-permute-start | bytes 589832 | tf_op jit(solution)/shard_map/ppermute | solution.py:41
  175.7 1.8 add_convert_fusion
  177.5 5.8 %all-to-all-start.3 = ((bf16[128,8,96]{0,2,1:T(8,128)(2,1)}), bf16[128,8,96]{0,2,1:T(8,128)(2,1)S(1)}, u32[]{:S(2)}, u32[]{:S(2)}) async-start(bf16[128,8,96]{0,2,1:T(8,128)(2,1)} %bitcast.20), calls=%async_computation.5 | async-start | bytes 393216 | tf_op jit(solution)/shard_map/all_to_all | solution.py:84
  183.3 1.7 add_convert_fusion.1
  184.9 4.1 %all-to-all-done.3 = bf16[128,8,96]{0,2,1:T(8,128)(2,1)S(1)} async-done(((bf16[128,8,96]{0,2,1:T(8,128)(2,1)}), bf16[128,8,96]{0,2,1:T(8,128)(2,1)S(1)}, u32[]{:S(2)}, u32[]{:S(2)}) %all-to-all-start.3) | async-done | bytes 196640 | tf_op jit(solution)/shard_map/all_to_all | solution.py:84
  189.0 4.5 %all-to-all-start.1 = ((bf16[128,8,96]{0,2,1:T(8,128)(2,1)}), bf16[128,8,96]{0,2,1:T(8,128)(2,1)S(1)}, u32[]{:S(2)}, u32[]{:S(2)}) async-start(bf16[128,8,96]{0,2,1:T(8,128)(2,1)} %bitcast.11), calls=%async_computation.2 | async-start | bytes 393216 | tf_op jit(solution)/shard_map/all_to_all | solution.py:84
  193.9 5.4 %all-to-all-done.1 = bf16[128,8,96]{0,2,1:T(8,128)(2,1)S(1)} async-done(((bf16[128,8,96]{0,2,1:T(8,128)(2,1)}), bf16[128,8,96]{0,2,1:T(8,128)(2,1)S(1)}, u32[]{:S(2)}, u32[]{:S(2)}) %all-to-all-start.1) | async-done | bytes 196640 | tf_op jit(solution)/shard_map/all_to_all | solution.py:84
  200.2 2.1 fusion.40
  (51 shorter events, 7.3 us)
Async XLA Ops:
  6.5 54.4 %copy-start = (bf16[1,352,2048]{2,1,0:T(8,128)(2,1)S(1)}, bf16[1,352,2048]{2,1,0:T(8,128)(2,1)}, u32[]{:S(2)}) copy-start(bf16[1,352,2048]{2,1,0:T(8,128)(2,1)} %param.13) | copy-start | bytes 4325380
  6.5 3.3 %copy-start.1 = (bf16[512,2048]{1,0:T(8,128)(2,1)S(1)}, bf16[512,2048]{1,0:T(8,128)(2,1)}, u32[]{:S(2)}) copy-start(bf16[512,2048]{1,0:T(8,128)(2,1)} %param.7) | copy-start | bytes 6291460
  6.5 3.3 %copy-start.14 = (f32[2048]{0:T(1024)S(1)}, f32[2048]{0:T(1024)}, u32[]{:S(2)}) copy-start(f32[2048]{0:T(1024)} %param.8) | copy-start | bytes 24580
  6.5 120.9 %reduce-scatter.5.cloned.1.call-start = ((), (), s32[]{:S(2)}) async-start(), calls=%async_computation.7 | async-start | bytes 3538944 | tf_op jit(solution)/shard_map/reduce_scatter | solution.py:81
  6.5 3.3 %copy-start.13 = (bf16[2048,8]{0,1:T(8,128)(2,1)S(1)}, bf16[2048,8]{0,1:T(8,128)(2,1)}, u32[]{:S(2)}) copy-start(bf16[2048,8]{0,1:T(8,128)(2,1)} %param.9) | copy-start | bytes 98308
  9.8 2.0 copy-start.15
  11.2 0.7 copy-start.5
  11.2 0.6 copy-start.6
  13.9 44.7 %copy-start.11 = (bf16[1,2048,352]{1,2,0:T(8,128)(2,1)S(1)}, bf16[1,2048,352]{1,2,0:T(8,128)(2,1)}, u32[]{:S(2)}) copy-start(bf16[1,2048,352]{1,2,0:T(8,128)(2,1)} %param.11) | copy-start | bytes 4325380
  56.9 1.7 copy-start.2
  69.0 103.6 %reduce-scatter.3.cloned.1.call-start = ((), (), s32[]{:S(2)}) async-start(), calls=%async_computation.6 | async-start | bytes 3538944 | tf_op jit(solution)/shard_map/reduce_scatter | solution.py:81
  71.7 42.0 %copy-start.12 = (bf16[1,2048,352]{1,2,0:T(8,128)(2,1)S(1)}, bf16[1,2048,352]{1,2,0:T(8,128)(2,1)}, u32[]{:S(2)}) copy-start(bf16[1,2048,352]{1,2,0:T(8,128)(2,1)} %param.11) | copy-start | bytes 4325380
  112.0 1.7 copy-start.3
  124.1 0.7 copy-start.4
  129.1 46.7 %collective-permute-start.1 = (bf16[128,768]{0,1:T(8,128)(2,1)}, bf16[128,768]{0,1:T(8,128)(2,1)}, u32[]{:S(2)}, u32[]{:S(2)}) collective-permute-start(bf16[128,768]{0,1:T(8,128)(2,1)} %constant_dynamic-slice_fusion), channel_id=1, source_target_pairs={{0,1},{1,0},{2,3},{3,2},{4,5},{5,4},{6,7},{7,6},{8,9},{9,8},{10,11... | collective-permute-start | bytes 589832 | tf_op jit(solution)/shard_map/ppermute | solution.py:41
  133.8 59.7 %copy-start.10 = (f32[512]{0:T(512)S(1)}, f32[512]{0:T(512)}, u32[]{:S(2)}) copy-start(f32[512]{0:T(512)} %get-tuple-element.21) | copy-start | bytes 6148
  133.8 65.5 %copy-start.8 = (s32[512,1]{0,1:T(1,128)S(1)}, s32[512,1]{0,1:T(1,128)}, u32[]{:S(2)}) copy-start(s32[512,1]{0,1:T(1,128)} %get-tuple-element.23) | copy-start | bytes 6148
  173.5 9.7 %collective-permute-start = (bf16[128,768]{0,1:T(8,128)(2,1)S(1)}, bf16[128,768]{0,1:T(8,128)(2,1)S(1)}, u32[]{:S(2)}, u32[]{:S(2)}) collective-permute-start(bf16[128,768]{0,1:T(8,128)(2,1)S(1)} %constant_dynamic-slice_fusion.1), channel_id=1, source_target_pairs={{0,1},{1,0},{2,3},{3,2},{4,5},{5,4},{6,7},{7,6},{8,9},{9,8},{10,11... | collective-permute-start | bytes 589832 | tf_op jit(solution)/shard_map/ppermute | solution.py:41
  177.5 22.3 %copy-start.9 = (f32[512]{0:T(512)S(1)}, f32[512]{0:T(512)}, u32[]{:S(2)}) copy-start(f32[512]{0:T(512)} %get-tuple-element.22) | copy-start | bytes 6148
  177.5 11.6 %all-to-all-start.3 = ((bf16[128,8,96]{0,2,1:T(8,128)(2,1)}), bf16[128,8,96]{0,2,1:T(8,128)(2,1)S(1)}, u32[]{:S(2)}, u32[]{:S(2)}) async-start(bf16[128,8,96]{0,2,1:T(8,128)(2,1)} %bitcast.20), calls=%async_computation.5 | async-start | bytes 393216 | tf_op jit(solution)/shard_map/all_to_all | solution.py:84
  184.9 15.3 %copy-start.7 = (s32[512,1]{0,1:T(1,128)S(1)}, s32[512,1]{0,1:T(1,128)}, u32[]{:S(2)}) copy-start(s32[512,1]{0,1:T(1,128)} %get-tuple-element.11) | copy-start | bytes 6148
  189.0 10.3 %all-to-all-start.1 = ((bf16[128,8,96]{0,2,1:T(8,128)(2,1)}), bf16[128,8,96]{0,2,1:T(8,128)(2,1)S(1)}, u32[]{:S(2)}, u32[]{:S(2)}) async-start(bf16[128,8,96]{0,2,1:T(8,128)(2,1)} %bitcast.11), calls=%async_computation.2 | async-start | bytes 393216 | tf_op jit(solution)/shard_map/all_to_all | solution.py:84
Sparse Core Ops, SparseCore 0:
  69.1 48.5 reduce-scatter.4
  124.3 48.2 reduce-scatter.2

commit v5 on v4

--- a/solution.py
+++ b/solution.py
@@ -79,10 +79,12 @@
                 w_down[0], hidden, (((0,), (1,)), ((), ())), preferred_element_type=jnp.float32
             ).astype(jnp.bfloat16)
             summed = lax.psum_scatter(partial_t, mp_axes[0], scatter_dimension=0, tiled=True)
-            summed = pair_exchange(summed, mp_axes[1])
-            summed = summed.reshape(slice_width, experts, chunk)
-            returned = lax.all_to_all(summed, expert_axes, split_axis=1, concat_axis=1, tiled=True)
-            returned = returned.reshape(slice_width, experts * chunk)
+            halves = lax.axis_size(mp_axes[1])
+            blocks = summed.reshape(halves, slice_width, experts, chunk).transpose(2, 0, 1, 3)
+            blocks = blocks.reshape(experts * halves, slice_width, chunk)
+            got = lax.all_to_all(blocks, expert_axes + mp_axes[1:], split_axis=0, concat_axis=0, tiled=True)
+            got = got.reshape(experts, halves, slice_width, chunk).astype(jnp.float32).sum(axis=1)
+            returned = got.astype(jnp.bfloat16).transpose(1, 0, 2).reshape(slice_width, experts * chunk)
             results.append((r0, r1, returned))
         logits = jnp.dot(normed, router_w, preferred_element_type=jnp.float32)
         w0, w1 = pair_weights(logits, oh0, oh1)

time: 210 us -> 203 us (0.967)
  waiting for transfers between devices: 48.3 us -> 38.7 us
  local copies, waits for them, and re-layouts: 7.52 us -> 12.2 us
    reshape x0 -> x4, local copies, waits for them, and re-layouts: none -> 7.25 us  [per_device(): summed.reshape(halves, slice_width, experts, chunk).transpose(2, 0, 1, 3)]
    all_to_all x2, waiting for transfers between devices: 9.46 us -> 3.63 us  [per_device(): lax.all_to_all(blocks, expert_axes + mp_axes[1:], split_axis=0, concat_ax...]
    ppermute x2 -> x0, starting transfers between devices: 4.3 us -> none  [pair_exchange(): got = lax.ppermute(give, axis, [(0, 1), (1, 0)])]
    reduce_scatter x2, waiting for transfers between devices: 38.8 us -> 35 us  [per_device(): lax.psum_scatter(partial_t, mp_axes[0], scatter_dimension=0, tiled=True)]
    convert_element_type x2 -> x0, other arithmetic: 3.42 us -> none  [pair_exchange(): (keep.astype(jnp.float32) + got.astype(jnp.float32)).astype(jnp.bfloat16)]
    all_to_all x2, starting transfers between devices: 10.3 us -> 13.2 us  [per_device(): lax.all_to_all(blocks, expert_axes + mp_axes[1:], split_axis=0, concat_ax...]
    dynamic_slice x2 -> x0, local copies, waits for them, and re-layouts: 2.56 us -> none  [pair_exchange(): give = lax.dynamic_slice_in_dim(summed, (1 - own) * width, width, 0)]
  transfers between devices with their start and end apart: 6 -> 4, of which waited for: 3 -> 2; matrix products, arithmetic and copies ran while one was open for 12% -> 14% of each run, Pallas kernels for 0% -> 0%
where the time goes in v5:
time: 203 us; the launch traced here: 202 us
  blocking collectives  83.3 us (41%)
  waiting for transfers between devices  38.7 us (19%)
  matrix products  30.4 us (15%)
  between operations  13.6 us (7%)
  starting transfers between devices  13.3 us (7%)
  local copies, waits for them, and re-layouts  12.2 us (6%)
  other arithmetic  10.5 us (5%)
    all_to_all x2, blocking collectives, per_device(): lax.all_to_all(part, expert_axes, split_axis=0, concat_axis=0, tiled=True)  83.3 us
    reduce_scatter x2, waiting for transfers between devices, per_device(): lax.psum_scatter(partial_t, mp_axes[0], scatter_dimension=0, tiled=True)  35 us
    dot_general x2, matrix products, per_device(): lax.dot_general(w_down[0], hidden, (((0,), (1,)), ((), ())), preferred_el...  16.1 us
    all_to_all x2, starting transfers between devices, per_device(): lax.all_to_all(blocks, expert_axes + mp_axes[1:], split_axis=0, concat_ax...  13.2 us
    reshape x4, local copies, waits for them, and re-layouts, per_device(): summed.reshape(halves, slice_width, experts, chunk).transpose(2, 0, 1, 3)  7.25 us
    dot_general x2, matrix products, per_device(): jnp.dot(dispatch, normed, preferred_element_type=jnp.float32)  4.77 us
    dot_general x2, matrix products, per_device(): jnp.dot(expert_rows, w_gate[0], preferred_element_type=jnp.float32)  4.63 us
    unnamed x36, local copies, waits for them, and re-layouts  4.08 us
  transfers between devices with their start and end apart: 4, of which 2 were waited for; matrix products, arithmetic and copies ran while one was open for 14% of the time, Pallas kernels for 0%

profile of v5, /device:TPU:2, one launch (start us, length us, event | category | flops | bytes accessed | tf_op | source)
XLA Modules:
  0.0 201.9 jit_solution(6711938094195079070)
XLA Ops:
  7.4 2.1 %multiply_reduce_fusion = f32[512]{0:T(512)S(1)} fusion(bf16[512,2048]{1,0:T(8,128)(2,1)} %param.7), kind=kLoop, calls=%fused_computation.1 | loop fusion | flops 3145216 | bytes 2099200 | tf_op jit(solution)/shard_map/reduce_sum | solution.py:54
  9.9 1.3 select_reduce_fusion
  11.9 2.0 %convolution_convert_fusion.1 = bf16[768,2048]{1,0:T(8,128)(2,1)S(1)} fusion(s32[512]{0:T(512)S(1)} %get-tuple-element.32, s32[512]{0:T(512)S(1)} %get-tuple-element.35, f32[2048]{0:T(1024)S(1)} %copy-done.17, f32[512]{0:T(512)S(1)} %add_rsqrt_fusion, bf16[512,2048]{1,0:T(8,128)(2,1)S(1)} %copy-done.1), kind=kOutput, calls=%fused_computation.3 | convolution fusion | flops 1617559552 | bytes 5257216 | tf_op jit(solution)/shard_map/dot_general | solution.py:71
  13.9 43.0 %all_to_all.20 = bf16[8,96,2048]{2,1,0:T(8,128)(2,1)S(1)} all-to-all(bf16[8,96,2048]{2,1,0:T(8,128)(2,1)S(1)} %bitcast.75), channel_id=1, replica_groups=mesh['dp'=2,'ey'=4,'ex'=2,'mz'=8,'mx'=2] {'ey','ex'}, dimensions={0} | all-to-all | bytes 6291456 | tf_op jit(solution)/shard_map/all_to_all | solution.py:73
  56.9 1.6 copy-done.2
  58.6 2.3 %fusion.16 = f32[768,352]{0,1:T(8,128)} fusion(bf16[768,2048]{1,0:T(8,128)(2,1)S(1)} %bitcast.76, bf16[1,2048,352]{1,2,0:T(8,128)(2,1)S(1)} %copy-done.13), kind=kOutput, calls=%fused_computation.28 | convolution fusion | flops 1107296256 | bytes 5668864 | tf_op jit(solution)/shard_map/dot_general | solution.py:75
  60.9 8.1 %fusion.1 = bf16[2048,768]{0,1:T(8,128)(2,1)} fusion(bf16[1,352,2048]{2,1,0:T(8,128)(2,1)S(1)} %copy-done, bf16[768,2048]{1,0:T(8,128)(2,1)} %bitcast.77, bf16[1,2048,352]{1,2,0:T(8,128)(2,1)} %param.12, f32[768,352]{0,1:T(8,128)} %fusion.16), kind=kOutput, calls=%fused_computation.7 | convolution fusion | flops 2217787392 | bytes 10256384 | tf_op jit(solution)/shard_map/dot_general | solution.py:78
  69.0 2.7 %convolution_convert_fusion.3 = bf16[768,2048]{1,0:T(8,128)(2,1)S(1)} fusion(s32[512]{0:T(512)S(1)} %get-tuple-element.19, s32[512]{0:T(512)S(1)} %get-tuple-element.17, f32[2048]{0:T(1024)} %param.8, f32[512]{0:T(512)S(1)} %add_rsqrt_fusion, bf16[512,2048]{1,0:T(8,128)(2,1)S(1)} %copy-done.1), kind=kOutput, calls=%fused_computation.5 | convolution fusion | flops 1617559552 | bytes 5257216 | tf_op jit(solution)/shard_map/dot_general | solution.py:71
  71.8 40.3 %all_to_all.21 = bf16[8,96,2048]{2,1,0:T(8,128)(2,1)S(1)} all-to-all(bf16[8,96,2048]{2,1,0:T(8,128)(2,1)S(1)} %bitcast.74), channel_id=1, replica_groups=mesh['dp'=2,'ey'=4,'ex'=2,'mz'=8,'mx'=2] {'ey','ex'}, dimensions={0} | all-to-all | bytes 6291456 | tf_op jit(solution)/shard_map/all_to_all | solution.py:73
  112.0 1.7 copy-done.3
  113.8 2.3 %fusion.18 = f32[768,352]{0,1:T(8,128)} fusion(bf16[768,2048]{1,0:T(8,128)(2,1)S(1)} %bitcast.78, bf16[1,2048,352]{1,2,0:T(8,128)(2,1)S(1)} %copy-done.14), kind=kOutput, calls=%fused_computation.30 | convolution fusion | flops 1107296256 | bytes 5668864 | tf_op jit(solution)/shard_map/dot_general | solution.py:75
  116.0 8.1 %fusion = bf16[2048,768]{0,1:T(8,128)(2,1)} fusion(bf16[1,352,2048]{2,1,0:T(8,128)(2,1)S(1)} %copy-done, bf16[768,2048]{1,0:T(8,128)(2,1)} %bitcast.79, bf16[1,2048,352]{1,2,0:T(8,128)(2,1)} %param.12, f32[768,352]{0,1:T(8,128)} %fusion.18), kind=kOutput, calls=%fused_computation.6 | convolution fusion | flops 2217787392 | bytes 10256384 | tf_op jit(solution)/shard_map/dot_general | solution.py:78
  124.8 1.3 compare_select_fusion.3
  126.1 1.8 reshape.255
  127.9 1.8 copy.9
  129.7 5.8 %all-to-all-start.3 = ((bf16[16,128,96]{1,2,0:T(8,128)(2,1)}), bf16[16,128,96]{1,2,0:T(8,128)(2,1)}, u32[]{:S(2)}, u32[]{:S(2)}) async-start(bf16[16,128,96]{1,2,0:T(8,128)(2,1)} %bitcast.81), calls=%async_computation.5 | async-start | bytes 786432 | tf_op jit(solution)/shard_map/all_to_all | solution.py:85
  136.1 1.3 broadcast_subtract_fusion
  137.4 35.0 %reduce-scatter.3.cloned.1.call-done = bf16[256,768]{0,1:T(8,128)(2,1)} async-done(((bf16[2048,768]{0,1:T(8,128)(2,1)}), bf16[256,768]{0,1:T(8,128)(2,1)}) %reduce-scatter.3.cloned.1.call-update) | async-done | bytes 393232 | tf_op jit(solution)/shard_map/reduce_scatter | solution.py:81
  172.4 1.8 reshape.249
  174.2 1.8 copy.8
  176.0 7.4 %all-to-all-start.1 = ((bf16[16,128,96]{1,2,0:T(8,128)(2,1)}), bf16[16,128,96]{1,2,0:T(8,128)(2,1)}, u32[]{:S(2)}, u32[]{:S(2)}) async-start(bf16[16,128,96]{1,2,0:T(8,128)(2,1)} %bitcast.80), calls=%async_computation.2 | async-start | bytes 786432 | tf_op jit(solution)/shard_map/all_to_all | solution.py:85
  183.5 2.5 %convert_element_type.103 = f32[512,2048]{1,0:T(8,128)} convert(bf16[512,2048]{1,0:T(8,128)(2,1)S(1)} %copy-done.1) | non-fusion elementwise | flops 1048576 | bytes 6291456 | tf_op jit(solution)/shard_map/convert_element_type | solution.py:51
  187.4 3.6 %all-to-all-done.1 = bf16[16,128,96]{1,2,0:T(8,128)(2,1)} async-done(((bf16[16,128,96]{1,2,0:T(8,128)(2,1)}), bf16[16,128,96]{1,2,0:T(8,128)(2,1)}, u32[]{:S(2)}, u32[]{:S(2)}) %all-to-all-start.1) | async-done | bytes 393248 | tf_op jit(solution)/shard_map/all_to_all | solution.py:85
  193.0 2.1 %fusion.40 = bf16[512,128]{1,0:T(8,128)(2,1)} fusion(f32[512,128]{1,0:T(8,128)S(1)} %fusion.39, f32[512,128]{1,0:T(8,128)S(1)} %fusion.34, bf16[128,768]{0,1:T(8,128)(2,1)S(1)} %bitcast.85, s32[512]{0:T(512)S(1)} %bitcast.98, f32[512,2048]{1,0:T(8,128)} %convert_element_type.103, s32[]{:T(128)S(6)} %select_n.143, f32[512]{0:T(512)S(1)} %copy-done.11), kind=kOutput, calls=%fused_computation.44 | convolution fusion | flops 101384192 | bytes 1118212 | tf_op jit(solution)/shard_map/dot_general | solution.py:95
  (53 shorter events, 6.5 us)
Async XLA Ops:
  6.5 54.4 %copy-start = (bf16[1,352,2048]{2,1,0:T(8,128)(2,1)S(1)}, bf16[1,352,2048]{2,1,0:T(8,128)(2,1)}, u32[]{:S(2)}) copy-start(bf16[1,352,2048]{2,1,0:T(8,128)(2,1)} %param.13) | copy-start | bytes 4325380
  6.5 3.3 %copy-start.1 = (bf16[512,2048]{1,0:T(8,128)(2,1)S(1)}, bf16[512,2048]{1,0:T(8,128)(2,1)}, u32[]{:S(2)}) copy-start(bf16[512,2048]{1,0:T(8,128)(2,1)} %param.7) | copy-start | bytes 6291460
  6.5 3.3 %copy-start.16 = (f32[2048]{0:T(1024)S(1)}, f32[2048]{0:T(1024)}, u32[]{:S(2)}) copy-start(f32[2048]{0:T(1024)} %param.8) | copy-start | bytes 24580
  6.5 119.6 %reduce-scatter.5.cloned.1.call-start = ((), (), s32[]{:S(2)}) async-start(), calls=%async_computation.7 | async-start | bytes 3538944 | tf_op jit(solution)/shard_map/reduce_scatter | solution.py:81
  6.5 3.3 %copy-start.15 = (bf16[2048,8]{0,1:T(8,128)(2,1)S(1)}, bf16[2048,8]{0,1:T(8,128)(2,1)}, u32[]{:S(2)}) copy-start(bf16[2048,8]{0,1:T(8,128)(2,1)} %param.9) | copy-start | bytes 98308
  9.8 2.0 %copy-start.17 = (f32[2048]{0:T(1024)S(1)}, f32[2048]{0:T(1024)}, u32[]{:S(2)}) copy-start(f32[2048]{0:T(1024)} %param.8) | copy-start | bytes 24580
  11.2 0.6 copy-start.6
  11.2 0.6 copy-start.7
  13.9 44.6 %copy-start.13 = (bf16[1,2048,352]{1,2,0:T(8,128)(2,1)S(1)}, bf16[1,2048,352]{1,2,0:T(8,128)(2,1)}, u32[]{:S(2)}) copy-start(bf16[1,2048,352]{1,2,0:T(8,128)(2,1)} %param.11) | copy-start | bytes 4325380
  56.9 1.6 copy-start.2
  69.0 103.4 %reduce-scatter.3.cloned.1.call-start = ((), (), s32[]{:S(2)}) async-start(), calls=%async_computation.6 | async-start | bytes 3538944 | tf_op jit(solution)/shard_map/reduce_scatter | solution.py:81
  71.8 42.0 %copy-start.14 = (bf16[1,2048,352]{1,2,0:T(8,128)(2,1)S(1)}, bf16[1,2048,352]{1,2,0:T(8,128)(2,1)}, u32[]{:S(2)}) copy-start(bf16[1,2048,352]{1,2,0:T(8,128)(2,1)} %param.11) | copy-start | bytes 4325380
  112.0 1.7 copy-start.3
  124.1 0.7 copy-start.4
  126.1 9.4 %copy-start.5 = (s32[512,1]{0,1:T(1,128)S(1)}, s32[512,1]{0,1:T(1,128)}, u32[]{:S(2)}) copy-start(s32[512,1]{0,1:T(1,128)} %get-tuple-element.25) | copy-start | bytes 6148
  129.7 46.3 %all-to-all-start.3 = ((bf16[16,128,96]{1,2,0:T(8,128)(2,1)}), bf16[16,128,96]{1,2,0:T(8,128)(2,1)}, u32[]{:S(2)}, u32[]{:S(2)}) async-start(bf16[16,128,96]{1,2,0:T(8,128)(2,1)} %bitcast.81), calls=%async_computation.5 | async-start | bytes 786432 | tf_op jit(solution)/shard_map/all_to_all | solution.py:85
  176.0 15.1 %all-to-all-start.1 = ((bf16[16,128,96]{1,2,0:T(8,128)(2,1)}), bf16[16,128,96]{1,2,0:T(8,128)(2,1)}, u32[]{:S(2)}, u32[]{:S(2)}) async-start(bf16[16,128,96]{1,2,0:T(8,128)(2,1)} %bitcast.80), calls=%async_computation.2 | async-start | bytes 786432 | tf_op jit(solution)/shard_map/all_to_all | solution.py:85
  183.4 3.5 %copy-start.10 = (s32[512,1]{0,1:T(1,128)S(1)}, s32[512,1]{0,1:T(1,128)}, u32[]{:S(2)}) copy-start(s32[512,1]{0,1:T(1,128)} %compare_select_fusion) | copy-start | bytes 6148
  183.5 3.5 %copy-start.12 = (f32[512]{0:T(512)S(1)}, f32[512]{0:T(512)}, u32[]{:S(2)}) copy-start(f32[512]{0:T(512)} %get-tuple-element.21) | copy-start | bytes 6148
  185.9 6.2 %copy-start.9 = (s32[512,1]{0,1:T(1,128)S(1)}, s32[512,1]{0,1:T(1,128)}, u32[]{:S(2)}) copy-start(s32[512,1]{0,1:T(1,128)} %get-tuple-element.23) | copy-start | bytes 6148
  185.9 6.6 %copy-start.11 = (f32[512]{0:T(512)S(1)}, f32[512]{0:T(512)}, u32[]{:S(2)}) copy-start(f32[512]{0:T(512)} %get-tuple-element.22) | copy-start | bytes 6148
  187.0 6.0 %copy-start.8 = (s32[512,1]{0,1:T(1,128)S(1)}, s32[512,1]{0,1:T(1,128)}, u32[]{:S(2)}) copy-start(s32[512,1]{0,1:T(1,128)} %get-tuple-element.11) | copy-start | bytes 6148
Sparse Core Ops, SparseCore 0:
  69.1 48.6 reduce-scatter.4
  124.3 48.0 reduce-scatter.2

commit v6 on v5

--- a/solution.py
+++ b/solution.py
@@ -59,8 +59,10 @@
         e0, e1 = choices[:, 0], choices[:, 1]
         chunk_rows = jnp.arange(experts * chunk, dtype=jnp.int32)
         column = lax.axis_index(mp_axes) * slice_width
-        residual = lax.dynamic_slice_in_dim(wide_in, column, slice_width, 1)
+        residual = lax.dynamic_slice_in_dim(hidden_in, column, slice_width, 1).astype(jnp.float32)
         mixture = None
+        ff_share = w_gate.shape[2]
+        gate_up = jnp.concatenate([w_gate[0], w_up[0]], axis=1)
         results = []
         for c in range(n_chunks):
             r0 = jnp.where(slot0 // chunk == c, e0 * chunk + slot0 % chunk, -1)
@@ -72,8 +74,8 @@
             part = part.reshape(experts, chunk, model_width)
             arrived = lax.all_to_all(part, expert_axes, split_axis=0, concat_axis=0, tiled=True)
             expert_rows = arrived.reshape(experts * chunk, model_width)
-            gate_proj = jnp.dot(expert_rows, w_gate[0], preferred_element_type=jnp.float32)
-            up_proj = jnp.dot(expert_rows, w_up[0], preferred_element_type=jnp.float32)
+            both = jnp.dot(expert_rows, gate_up, preferred_element_type=jnp.float32)
+            gate_proj, up_proj = both[:, :ff_share], both[:, ff_share:]
             hidden = (jax.nn.silu(gate_proj) * up_proj).astype(jnp.bfloat16)
             partial_t = lax.dot_general(
                 w_down[0], hidden, (((0,), (1,)), ((), ())), preferred_element_type=jnp.float32

time: 203 us -> 192 us (0.946)
  matrix products: 30.4 us -> 24.5 us
  local copies, waits for them, and re-layouts: 12.2 us -> 9.5 us
    dot_general x2, matrix products: 16.1 us -> 7.12 us  [per_device(): lax.dot_general(w_down[0], hidden, (((0,), (1,)), ((), ())), preferred_el...]
    unnamed x36 -> x34, local copies, waits for them, and re-layouts: 4.08 us -> 1.4 us
    convert_element_type x1 -> x0, other arithmetic: 2.46 us -> none  [per_device(): wide_in = hidden_in.astype(jnp.float32)]
    dot_general x2, matrix products: 0.85 us -> 2.91 us  [per_device(): lax.dot_general(sel1, returned, dims, preferred_element_type=jnp.float32)]
  transfers between devices with their start and end apart: 4 -> 4, of which waited for: 2 -> 2; matrix products, arithmetic and copies ran while one was open for 14% -> 12% of each run, Pallas kernels for 0% -> 0%
where the time goes in v6:
time: 192 us
  blocking collectives  83.5 us (43%)
  waiting for transfers between devices  38.9 us (20%)
  matrix products  24.5 us (13%)
  between operations  13.6 us (7%)
  starting transfers between devices  13 us (7%)
  local copies, waits for them, and re-layouts  9.5 us (5%)
  other arithmetic  8.67 us (5%)
    all_to_all x2, blocking collectives, per_device(): lax.all_to_all(part, expert_axes, split_axis=0, concat_axis=0, tiled=True)  83.5 us
    reduce_scatter x2, waiting for transfers between devices, per_device(): lax.psum_scatter(partial_t, mp_axes[0], scatter_dimension=0, tiled=True)  35.3 us
    all_to_all x2, starting transfers between devices, per_device(): lax.all_to_all(blocks, expert_axes + mp_axes[1:], split_axis=0, concat_ax...  12.9 us
    reshape x4, local copies, waits for them, and re-layouts, per_device(): summed.reshape(halves, slice_width, experts, chunk).transpose(2, 0, 1, 3)  7.24 us
    dot_general x2, matrix products, per_device(): lax.dot_general(w_down[0], hidden, (((0,), (1,)), ((), ())), preferred_el...  7.12 us
    dot_general x2, matrix products, per_device(): both = jnp.dot(expert_rows, gate_up, preferred_element_type=jnp.float32)  4.89 us
    dot_general x2, matrix products, per_device(): jnp.dot(dispatch, normed, preferred_element_type=jnp.float32)  4.77 us
  transfers between devices with their start and end apart: 4, of which 2 were waited for; matrix products, arithmetic and copies ran while one was open for 12% of the time, Pallas kernels for 0%

profile of v6, /device:TPU:2, one launch (start us, length us, event | category | flops | bytes accessed | tf_op | source)
XLA Modules:
  0.0 191.6 jit_solution(8083260381905102226)
XLA Ops:
  7.4 2.1 %fusion = f32[512]{0:T(512)S(1)} fusion(bf16[512,2048]{1,0:T(8,128)(2,1)} %param.7), kind=kLoop, calls=%fused_computation.2 | loop fusion | flops 3145216 | bytes 2099200 | tf_op jit(solution)/shard_map/reduce_sum | solution.py:54
  9.8 1.3 select_reduce_fusion
  11.9 2.0 %convolution_convert_fusion.1 = bf16[768,2048]{1,0:T(8,128)(2,1)S(1)} fusion(s32[512]{0:T(512)S(1)} %get-tuple-element.32, s32[512]{0:T(512)S(1)} %get-tuple-element.35, bf16[512,2048]{1,0:T(8,128)(2,1)S(1)} %copy-done.1, f32[2048]{0:T(1024)S(1)} %copy-done.16, f32[512]{0:T(512)S(1)} %add_rsqrt_fusion), kind=kOutput, calls=%fused_computation.6 | convolution fusion | flops 1617559552 | bytes 5257216 | tf_op jit(solution)/shard_map/dot_general | solution.py:73
  13.9 43.1 %all_to_all.20 = bf16[8,96,2048]{2,1,0:T(8,128)(2,1)S(1)} all-to-all(bf16[8,96,2048]{2,1,0:T(8,128)(2,1)S(1)} %bitcast.53), channel_id=1, replica_groups=mesh['dp'=2,'ey'=4,'ex'=2,'mz'=8,'mx'=2] {'ey','ex'}, dimensions={0} | all-to-all | bytes 6291456 | tf_op jit(solution)/shard_map/all_to_all | solution.py:75
  57.1 2.4 %fusion.5 = f32[768,704]{0,1:T(8,128)S(1)} fusion(bf16[768,2048]{1,0:T(8,128)(2,1)S(1)} %bitcast.54, bf16[2048,352]{0,1:T(8,128)(2,1)S(1)} %bitcast.78, bf16[2048,352]{0,1:T(8,128)(2,1)S(1)} %bitcast.80), kind=kOutput, calls=%fused_computation.12 | convolution fusion | flops 2220359680 | bytes 8192000 | tf_op jit(solution)/shard_map/dot_general | solution.py:77
  59.5 3.6 %fusion.4 = bf16[2048,768]{0,1:T(8,128)(2,1)} fusion(bf16[1,352,2048]{2,1,0:T(8,128)(2,1)S(1)} %copy-done, f32[768,704]{0,1:T(8,128)S(1)} %fusion.5), kind=kOutput, calls=%fused_computation.10 | convolution fusion | flops 1110491136 | bytes 6750208 | tf_op jit(solution)/shard_map/dot_general | solution.py:80
  63.2 2.7 %convolution_convert_fusion.3 = bf16[768,2048]{1,0:T(8,128)(2,1)S(1)} fusion(s32[512]{0:T(512)S(1)} %get-tuple-element.19, s32[512]{0:T(512)S(1)} %get-tuple-element.17, bf16[512,2048]{1,0:T(8,128)(2,1)S(1)} %copy-done.1, f32[2048]{0:T(1024)} %param.8, f32[512]{0:T(512)S(1)} %add_rsqrt_fusion), kind=kOutput, calls=%fused_computation.8 | convolution fusion | flops 1617559552 | bytes 5257216 | tf_op jit(solution)/shard_map/dot_general | solution.py:73
  65.9 40.4 %all_to_all.21 = bf16[8,96,2048]{2,1,0:T(8,128)(2,1)S(1)} all-to-all(bf16[8,96,2048]{2,1,0:T(8,128)(2,1)S(1)} %bitcast.52), channel_id=1, replica_groups=mesh['dp'=2,'ey'=4,'ex'=2,'mz'=8,'mx'=2] {'ey','ex'}, dimensions={0} | all-to-all | bytes 6291456 | tf_op jit(solution)/shard_map/all_to_all | solution.py:75
  106.3 2.5 %fusion.6 = f32[768,704]{0,1:T(8,128)S(1)} fusion(bf16[768,2048]{1,0:T(8,128)(2,1)S(1)} %bitcast.55, bf16[2048,352]{0,1:T(8,128)(2,1)S(1)} %bitcast.79, bf16[2048,352]{0,1:T(8,128)(2,1)S(1)} %bitcast.81), kind=kOutput, calls=%fused_computation.13 | convolution fusion | flops 2220359680 | bytes 8192000 | tf_op jit(solution)/shard_map/dot_general | solution.py:77
  108.8 3.6 %fusion.3 = bf16[2048,768]{0,1:T(8,128)(2,1)} fusion(bf16[1,352,2048]{2,1,0:T(8,128)(2,1)S(1)} %copy-done, f32[768,704]{0,1:T(8,128)S(1)} %fusion.6), kind=kOutput, calls=%fused_computation.9 | convolution fusion | flops 1110491136 | bytes 6750208 | tf_op jit(solution)/shard_map/dot_general | solution.py:80
  113.0 1.3 compare_select_fusion.3
  114.3 1.8 reshape.255
  116.2 1.8 copy.9
  118.0 5.7 %all-to-all-start.3 = ((bf16[16,128,96]{1,2,0:T(8,128)(2,1)}), bf16[16,128,96]{1,2,0:T(8,128)(2,1)}, u32[]{:S(2)}, u32[]{:S(2)}) async-start(bf16[16,128,96]{1,2,0:T(8,128)(2,1)} %bitcast.57), calls=%async_computation.5 | async-start | bytes 786432 | tf_op jit(solution)/shard_map/all_to_all | solution.py:87
  124.3 1.3 broadcast_subtract_fusion
  125.6 35.3 %reduce-scatter.3.cloned.1.call-done = bf16[256,768]{0,1:T(8,128)(2,1)} async-done(((bf16[2048,768]{0,1:T(8,128)(2,1)}), bf16[256,768]{0,1:T(8,128)(2,1)}) %reduce-scatter.3.cloned.1.call-update) | async-done | bytes 393232 | tf_op jit(solution)/shard_map/reduce_scatter | solution.py:83
  160.9 1.8 reshape.249
  162.7 1.8 copy.8
  164.5 7.2 %all-to-all-start.1 = ((bf16[16,128,96]{1,2,0:T(8,128)(2,1)}), bf16[16,128,96]{1,2,0:T(8,128)(2,1)}, u32[]{:S(2)}, u32[]{:S(2)}) async-start(bf16[16,128,96]{1,2,0:T(8,128)(2,1)} %bitcast.56), calls=%async_computation.2 | async-start | bytes 786432 | tf_op jit(solution)/shard_map/all_to_all | solution.py:87
  174.0 1.8 fusion.17
  175.8 3.5 %all-to-all-done.1 = bf16[16,128,96]{1,2,0:T(8,128)(2,1)} async-done(((bf16[16,128,96]{1,2,0:T(8,128)(2,1)}), bf16[16,128,96]{1,2,0:T(8,128)(2,1)}, u32[]{:S(2)}, u32[]{:S(2)}) %all-to-all-start.1) | async-done | bytes 393248 | tf_op jit(solution)/shard_map/all_to_all | solution.py:87
  180.4 1.1 fusion.19
  181.5 1.4 fusion.24
  183.0 1.8 fusion.25
  (50 shorter events, 6.5 us)
Async XLA Ops:
  6.5 53.0 %copy-start = (bf16[1,352,2048]{2,1,0:T(8,128)(2,1)S(1)}, bf16[1,352,2048]{2,1,0:T(8,128)(2,1)}, u32[]{:S(2)}) copy-start(bf16[1,352,2048]{2,1,0:T(8,128)(2,1)} %param.13) | copy-start | bytes 4325380
  6.5 3.3 %copy-start.1 = (bf16[512,2048]{1,0:T(8,128)(2,1)S(1)}, bf16[512,2048]{1,0:T(8,128)(2,1)}, u32[]{:S(2)}) copy-start(bf16[512,2048]{1,0:T(8,128)(2,1)} %param.7) | copy-start | bytes 6291460
  6.5 3.3 %copy-start.15 = (f32[2048]{0:T(1024)S(1)}, f32[2048]{0:T(1024)}, u32[]{:S(2)}) copy-start(f32[2048]{0:T(1024)} %param.8) | copy-start | bytes 24580
  6.5 107.8 %reduce-scatter.5.cloned.1.call-start = ((), (), s32[]{:S(2)}) async-start(), calls=%async_computation.7 | async-start | bytes 3538944 | tf_op jit(solution)/shard_map/reduce_scatter | solution.py:83
  6.5 3.3 %copy-start.14 = (bf16[2048,8]{0,1:T(8,128)(2,1)S(1)}, bf16[2048,8]{0,1:T(8,128)(2,1)}, u32[]{:S(2)}) copy-start(bf16[2048,8]{0,1:T(8,128)(2,1)} %param.9) | copy-start | bytes 98308
  9.6 2.3 %copy-start.16 = (f32[2048]{0:T(1024)S(1)}, f32[2048]{0:T(1024)}, u32[]{:S(2)}) copy-start(f32[2048]{0:T(1024)} %param.8) | copy-start | bytes 24580
  11.2 0.7 copy-start.5
  11.2 0.6 copy-start.6
  13.9 43.1 %copy-start.10 = (bf16[1,2048,352]{1,2,0:T(8,128)(2,1)S(1)}, bf16[1,2048,352]{1,2,0:T(8,128)(2,1)}, u32[]{:S(2)}) copy-start(bf16[1,2048,352]{1,2,0:T(8,128)(2,1)} %param.12) | copy-start | bytes 4325380
  13.9 43.1 %copy-start.12 = (bf16[1,2048,352]{1,2,0:T(8,128)(2,1)S(1)}, bf16[1,2048,352]{1,2,0:T(8,128)(2,1)}, u32[]{:S(2)}) copy-start(bf16[1,2048,352]{1,2,0:T(8,128)(2,1)} %param.11) | copy-start | bytes 4325380
  63.1 97.8 %reduce-scatter.3.cloned.1.call-start = ((), (), s32[]{:S(2)}) async-start(), calls=%async_computation.6 | async-start | bytes 3538944 | tf_op jit(solution)/shard_map/reduce_scatter | solution.py:83
  65.9 40.4 %copy-start.11 = (bf16[1,2048,352]{1,2,0:T(8,128)(2,1)S(1)}, bf16[1,2048,352]{1,2,0:T(8,128)(2,1)}, u32[]{:S(2)}) copy-start(bf16[1,2048,352]{1,2,0:T(8,128)(2,1)} %param.12) | copy-start | bytes 4325380
  65.9 40.4 %copy-start.13 = (bf16[1,2048,352]{1,2,0:T(8,128)(2,1)S(1)}, bf16[1,2048,352]{1,2,0:T(8,128)(2,1)}, u32[]{:S(2)}) copy-start(bf16[1,2048,352]{1,2,0:T(8,128)(2,1)} %param.11) | copy-start | bytes 4325380
  112.3 0.7 copy-start.3
  114.3 9.4 %copy-start.4 = (s32[512,1]{0,1:T(1,128)S(1)}, s32[512,1]{0,1:T(1,128)}, u32[]{:S(2)}) copy-start(s32[512,1]{0,1:T(1,128)} %get-tuple-element.25) | copy-start | bytes 6148
  118.0 46.6 %all-to-all-start.3 = ((bf16[16,128,96]{1,2,0:T(8,128)(2,1)}), bf16[16,128,96]{1,2,0:T(8,128)(2,1)}, u32[]{:S(2)}, u32[]{:S(2)}) async-start(bf16[16,128,96]{1,2,0:T(8,128)(2,1)} %bitcast.57), calls=%async_computation.5 | async-start | bytes 786432 | tf_op jit(solution)/shard_map/all_to_all | solution.py:87
  125.6 54.8 %copy-start.8 = (s32[512,1]{0,1:T(1,128)S(1)}, s32[512,1]{0,1:T(1,128)}, u32[]{:S(2)}) copy-start(s32[512,1]{0,1:T(1,128)} %get-tuple-element.23) | copy-start | bytes 6148
  164.5 14.8 %all-to-all-start.1 = ((bf16[16,128,96]{1,2,0:T(8,128)(2,1)}), bf16[16,128,96]{1,2,0:T(8,128)(2,1)}, u32[]{:S(2)}, u32[]{:S(2)}) async-start(bf16[16,128,96]{1,2,0:T(8,128)(2,1)} %bitcast.56), calls=%async_computation.2 | async-start | bytes 786432 | tf_op jit(solution)/shard_map/all_to_all | solution.py:87
  171.7 11.3 %copy-start.7 = (s32[512,1]{0,1:T(1,128)S(1)}, s32[512,1]{0,1:T(1,128)}, u32[]{:S(2)}) copy-start(s32[512,1]{0,1:T(1,128)} %get-tuple-element.11) | copy-start | bytes 6148
  172.3 9.2 %copy-start.9 = (s32[512,1]{0,1:T(1,128)S(1)}, s32[512,1]{0,1:T(1,128)}, u32[]{:S(2)}) copy-start(s32[512,1]{0,1:T(1,128)} %compare_select_fusion.1) | copy-start | bytes 6148
  173.3 0.7 copy-start.2
Sparse Core Ops, SparseCore 0:
  63.2 48.5 reduce-scatter.4
  114.4 46.4 reduce-scatter.2

commit v7 on v6

--- a/solution.py
+++ b/solution.py
@@ -65,15 +65,15 @@
         gate_up = jnp.concatenate([w_gate[0], w_up[0]], axis=1)
         results = []
         for c in range(n_chunks):
-            r0 = jnp.where(slot0 // chunk == c, e0 * chunk + slot0 % chunk, -1)
-            r1 = jnp.where(slot1 // chunk == c, e1 * chunk + slot1 % chunk, -1)
+            r0 = jnp.where(slot0 // chunk == c, (slot0 % chunk) * experts + e0, -1)
+            r1 = jnp.where(slot1 // chunk == c, (slot1 % chunk) * experts + e1, -1)
             dispatch = (
                 (r0[None, :] == chunk_rows[:, None]) | (r1[None, :] == chunk_rows[:, None])
             ).astype(jnp.bfloat16)
             part = jnp.dot(dispatch, normed, preferred_element_type=jnp.float32).astype(jnp.bfloat16)
-            part = part.reshape(experts, chunk, model_width)
-            arrived = lax.all_to_all(part, expert_axes, split_axis=0, concat_axis=0, tiled=True)
-            expert_rows = arrived.reshape(experts * chunk, model_width)
+            part = part.reshape(chunk, experts, model_width)
+            arrived = lax.all_to_all(part, expert_axes, split_axis=1, concat_axis=1, tiled=True)
+            expert_rows = arrived.reshape(chunk * experts, model_width)
             both = jnp.dot(expert_rows, gate_up, preferred_element_type=jnp.float32)
             gate_proj, up_proj = both[:, :ff_share], both[:, ff_share:]
             hidden = (jax.nn.silu(gate_proj) * up_proj).astype(jnp.bfloat16)
@@ -82,15 +82,15 @@
             ).astype(jnp.bfloat16)
             summed = lax.psum_scatter(partial_t, mp_axes[0], scatter_dimension=0, tiled=True)
             halves = lax.axis_size(mp_axes[1])
-            blocks = summed.reshape(halves, slice_width, experts, chunk).transpose(2, 0, 1, 3)
-            blocks = blocks.reshape(experts * halves, slice_width, chunk)
-            got = lax.all_to_all(blocks, expert_axes + mp_axes[1:], split_axis=0, concat_axis=0, tiled=True)
-            got = got.reshape(experts, halves, slice_width, chunk).astype(jnp.float32).sum(axis=1)
-            returned = got.astype(jnp.bfloat16).transpose(1, 0, 2).reshape(slice_width, experts * chunk)
+            blocks = summed.reshape(halves, slice_width, chunk, experts).transpose(2, 3, 0, 1)
+            blocks = blocks.reshape(chunk, experts * halves, slice_width)
+            got = lax.all_to_all(blocks, expert_axes + mp_axes[1:], split_axis=1, concat_axis=1, tiled=True)
+            got = got.reshape(chunk, experts, halves, slice_width).astype(jnp.float32).sum(axis=2)
+            returned = got.astype(jnp.bfloat16).reshape(chunk * experts, slice_width)
             results.append((r0, r1, returned))
         logits = jnp.dot(normed, router_w, preferred_element_type=jnp.float32)
         w0, w1 = pair_weights(logits, oh0, oh1)
-        dims = (((1,), (1,)), ((), ()))
+        dims = (((1,), (0,)), ((), ()))
         for r0, r1, returned in results:
             sel0 = (r0[:, None] == chunk_rows[None, :]).astype(jnp.bfloat16)
             sel1 = (r1[:, None] == chunk_rows[None, :]).astype(jnp.bfloat16)

time: 192 us -> 194 us (1.010)
  transfers between devices with their start and end apart: 4 -> 4, of which waited for: 2 -> 2; matrix products, arithmetic and copies ran while one was open for 12% -> 11% of each run, Pallas kernels for 0% -> 0%
where the time goes in v7:
time: 194 us
  blocking collectives  83.5 us (43%)
  waiting for transfers between devices  39.6 us (20%)
  matrix products  24.3 us (13%)
  between operations  13.6 us (7%)
  starting transfers between devices  13.3 us (7%)
  other arithmetic  9.94 us (5%)
  local copies, waits for them, and re-layouts  9.4 us (5%)
    all_to_all x2, blocking collectives, per_device(): lax.all_to_all(part, expert_axes, split_axis=1, concat_axis=1, tiled=True)  83.5 us
    reduce_scatter x2, waiting for transfers between devices, per_device(): lax.psum_scatter(partial_t, mp_axes[0], scatter_dimension=0, tiled=True)  36.1 us
    all_to_all x2, starting transfers between devices, per_device(): lax.all_to_all(blocks, expert_axes + mp_axes[1:], split_axis=1, concat_ax...  13.1 us
    dot_general x2, matrix products, per_device(): lax.dot_general(w_down[0], hidden, (((0,), (1,)), ((), ())), preferred_el...  7.1 us
    dot_general x2, matrix products, per_device(): both = jnp.dot(expert_rows, gate_up, preferred_element_type=jnp.float32)  5.44 us
    dot_general x2, matrix products, per_device(): jnp.dot(dispatch, normed, preferred_element_type=jnp.float32)  4.77 us
  transfers between devices with their start and end apart: 4, of which 2 were waited for; matrix products, arithmetic and copies ran while one was open for 11% of the time, Pallas kernels for 0%

profile of v7, /device:TPU:2, one launch (start us, length us, event | category | flops | bytes accessed | tf_op | source)
XLA Modules:
  0.0 193.7 jit_solution(16030327362680095952)
XLA Ops:
  7.4 2.1 %fusion = f32[512]{0:T(512)S(1)} fusion(bf16[512,2048]{1,0:T(8,128)(2,1)} %param.7), kind=kLoop, calls=%fused_computation.2 | loop fusion | flops 3145216 | bytes 2099200 | tf_op jit(solution)/shard_map/reduce_sum | solution.py:54
  9.8 1.3 select_reduce_fusion
  12.4 2.0 %fusion.12 = bf16[96,8,2048]{2,1,0:T(8,128)(2,1)S(1)} fusion(s32[512]{0:T(512)S(1)} %get-tuple-element.31, s32[512]{0:T(512)S(1)} %get-tuple-element.29, bf16[512,2048]{1,0:T(8,128)(2,1)S(1)} %copy-done.1, f32[2048]{0:T(1024)S(1)} %copy-done.17, f32[512]{0:T(512)S(1)} %add_rsqrt_fusion), kind=kOutput, calls=%fused_computation.18 | convolution fusion | flops 1617559552 | bytes 5257216 | tf_op jit(solution)/shard_map/dot_general | solution.py:73
  14.5 1.7 copy.18
  16.2 43.1 %all_to_all.20 = bf16[96,8,2048]{2,0,1:T(8,128)(2,1)S(1)} all-to-all(bf16[96,8,2048]{2,0,1:T(8,128)(2,1)S(1)} %copy.18), channel_id=1, replica_groups=mesh['dp'=2,'ey'=4,'ex'=2,'mz'=8,'mx'=2] {'ey','ex'}, dimensions={1} | all-to-all | bytes 6291456 | tf_op jit(solution)/shard_map/all_to_all | solution.py:75
  59.4 2.7 %fusion.3 = f32[768,704]{0,1:T(8,128)S(1)} fusion(bf16[96,8,2048]{2,0,1:T(8,128)(2,1)S(1)} %all_to_all.20, bf16[2048,352]{0,1:T(8,128)(2,1)S(1)} %bitcast.74, bf16[2048,352]{0,1:T(8,128)(2,1)S(1)} %bitcast.76), kind=kOutput, calls=%fused_computation.9 | convolution fusion | flops 2220359680 | bytes 8192000 | tf_op jit(solution)/shard_map/dot_general | solution.py:77
  62.1 3.6 %fusion.10 = bf16[2048,768]{0,1:T(8,128)(2,1)} fusion(bf16[1,352,2048]{2,1,0:T(8,128)(2,1)S(1)} %copy-done, f32[768,704]{0,1:T(8,128)S(1)} %fusion.3), kind=kOutput, calls=%fused_computation.16 | convolution fusion | flops 1110491136 | bytes 6750208 | tf_op jit(solution)/shard_map/dot_general | solution.py:80
  65.9 2.7 %fusion.11 = bf16[96,8,2048]{2,1,0:T(8,128)(2,1)S(1)} fusion(s32[512]{0:T(512)S(1)} %get-tuple-element.34, s32[512]{0:T(512)} %get-tuple-element.14, bf16[512,2048]{1,0:T(8,128)(2,1)S(1)} %copy-done.1, f32[2048]{0:T(1024)} %param.8, f32[512]{0:T(512)S(1)} %add_rsqrt_fusion), kind=kOutput, calls=%fused_computation.17 | convolution fusion | flops 1617559552 | bytes 5257216 | tf_op jit(solution)/shard_map/dot_general | solution.py:73
  68.7 1.7 copy.14
  70.4 40.4 %all_to_all.21 = bf16[96,8,2048]{2,0,1:T(8,128)(2,1)S(1)} all-to-all(bf16[96,8,2048]{2,0,1:T(8,128)(2,1)S(1)} %copy.14), channel_id=1, replica_groups=mesh['dp'=2,'ey'=4,'ex'=2,'mz'=8,'mx'=2] {'ey','ex'}, dimensions={1} | all-to-all | bytes 6291456 | tf_op jit(solution)/shard_map/all_to_all | solution.py:75
  110.8 2.7 %fusion.5 = f32[768,704]{0,1:T(8,128)S(1)} fusion(bf16[96,8,2048]{2,0,1:T(8,128)(2,1)S(1)} %all_to_all.21, bf16[2048,352]{0,1:T(8,128)(2,1)S(1)} %bitcast.75, bf16[2048,352]{0,1:T(8,128)(2,1)S(1)} %bitcast.77), kind=kOutput, calls=%fused_computation.11 | convolution fusion | flops 2220359680 | bytes 8192000 | tf_op jit(solution)/shard_map/dot_general | solution.py:77
  113.6 3.5 %fusion.9 = bf16[2048,768]{0,1:T(8,128)(2,1)} fusion(bf16[1,352,2048]{2,1,0:T(8,128)(2,1)S(1)} %copy-done, f32[768,704]{0,1:T(8,128)S(1)} %fusion.5), kind=kOutput, calls=%fused_computation.15 | convolution fusion | flops 1110491136 | bytes 6750208 | tf_op jit(solution)/shard_map/dot_general | solution.py:80
  117.8 1.3 compare_select_fusion.3
  119.1 1.8 copy.20
  120.9 5.9 %all-to-all-start.3 = ((bf16[96,16,128]{2,0,1:T(8,128)(2,1)}), bf16[96,16,128]{2,0,1:T(8,128)(2,1)}, u32[]{:S(2)}, u32[]{:S(2)}) async-start(bf16[96,16,128]{2,0,1:T(8,128)(2,1)} %bitcast.55), calls=%async_computation.5 | async-start | bytes 786432 | tf_op jit(solution)/shard_map/all_to_all | solution.py:87
  126.8 1.3 compare_select_fusion
  128.0 1.3 broadcast_subtract_fusion
  129.3 36.1 %reduce-scatter.3.cloned.1.call-done = bf16[256,768]{0,1:T(8,128)(2,1)} async-done(((bf16[2048,768]{0,1:T(8,128)(2,1)}), bf16[256,768]{0,1:T(8,128)(2,1)}) %reduce-scatter.3.cloned.1.call-update) | async-done | bytes 393232 | tf_op jit(solution)/shard_map/reduce_scatter | solution.py:83
  165.4 1.8 copy.16
  167.3 7.3 %all-to-all-start.1 = ((bf16[96,16,128]{2,0,1:T(8,128)(2,1)}), bf16[96,16,128]{2,0,1:T(8,128)(2,1)}, u32[]{:S(2)}, u32[]{:S(2)}) async-start(bf16[96,16,128]{2,0,1:T(8,128)(2,1)} %bitcast.54), calls=%async_computation.2 | async-start | bytes 786432 | tf_op jit(solution)/shard_map/all_to_all | solution.py:87
  176.9 1.8 fusion.23
  178.7 3.5 %all-to-all-done.1 = bf16[96,16,128]{2,0,1:T(8,128)(2,1)} async-done(((bf16[96,16,128]{2,0,1:T(8,128)(2,1)}), bf16[96,16,128]{2,0,1:T(8,128)(2,1)}, u32[]{:S(2)}, u32[]{:S(2)}) %all-to-all-start.1) | async-done | bytes 393248 | tf_op jit(solution)/shard_map/all_to_all | solution.py:87
  183.7 1.4 fusion.30
  185.1 1.8 fusion.31
  (52 shorter events, 7.1 us)
Async XLA Ops:
  6.5 55.6 %copy-start = (bf16[1,352,2048]{2,1,0:T(8,128)(2,1)S(1)}, bf16[1,352,2048]{2,1,0:T(8,128)(2,1)}, u32[]{:S(2)}) copy-start(bf16[1,352,2048]{2,1,0:T(8,128)(2,1)} %param.13) | copy-start | bytes 4325380
  6.5 3.3 %copy-start.1 = (bf16[512,2048]{1,0:T(8,128)(2,1)S(1)}, bf16[512,2048]{1,0:T(8,128)(2,1)}, u32[]{:S(2)}) copy-start(bf16[512,2048]{1,0:T(8,128)(2,1)} %param.7) | copy-start | bytes 6291460
  6.5 3.3 %copy-start.16 = (f32[2048]{0:T(1024)S(1)}, f32[2048]{0:T(1024)}, u32[]{:S(2)}) copy-start(f32[2048]{0:T(1024)} %param.8) | copy-start | bytes 24580
  6.5 112.5 %reduce-scatter.5.cloned.1.call-start = ((), (), s32[]{:S(2)}) async-start(), calls=%async_computation.7 | async-start | bytes 3538944 | tf_op jit(solution)/shard_map/reduce_scatter | solution.py:83
  6.5 3.3 %copy-start.15 = (bf16[2048,8]{0,1:T(8,128)(2,1)S(1)}, bf16[2048,8]{0,1:T(8,128)(2,1)}, u32[]{:S(2)}) copy-start(bf16[2048,8]{0,1:T(8,128)(2,1)} %param.9) | copy-start | bytes 98308
  9.6 2.9 %copy-start.17 = (f32[2048]{0:T(1024)S(1)}, f32[2048]{0:T(1024)}, u32[]{:S(2)}) copy-start(f32[2048]{0:T(1024)} %param.8) | copy-start | bytes 24580
  11.8 0.6 copy-start.5
  11.8 0.6 copy-start.6
  16.2 43.2 %copy-start.11 = (bf16[1,2048,352]{1,2,0:T(8,128)(2,1)S(1)}, bf16[1,2048,352]{1,2,0:T(8,128)(2,1)}, u32[]{:S(2)}) copy-start(bf16[1,2048,352]{1,2,0:T(8,128)(2,1)} %param.12) | copy-start | bytes 4325380
  16.2 43.1 %copy-start.13 = (bf16[1,2048,352]{1,2,0:T(8,128)(2,1)S(1)}, bf16[1,2048,352]{1,2,0:T(8,128)(2,1)}, u32[]{:S(2)}) copy-start(bf16[1,2048,352]{1,2,0:T(8,128)(2,1)} %param.11) | copy-start | bytes 4325380
  65.7 99.7 %reduce-scatter.3.cloned.1.call-start = ((), (), s32[]{:S(2)}) async-start(), calls=%async_computation.6 | async-start | bytes 3538944 | tf_op jit(solution)/shard_map/reduce_scatter | solution.py:83
  70.4 40.4 %copy-start.12 = (bf16[1,2048,352]{1,2,0:T(8,128)(2,1)S(1)}, bf16[1,2048,352]{1,2,0:T(8,128)(2,1)}, u32[]{:S(2)}) copy-start(bf16[1,2048,352]{1,2,0:T(8,128)(2,1)} %param.12) | copy-start | bytes 4325380
  70.4 40.4 %copy-start.14 = (bf16[1,2048,352]{1,2,0:T(8,128)(2,1)S(1)}, bf16[1,2048,352]{1,2,0:T(8,128)(2,1)}, u32[]{:S(2)}) copy-start(bf16[1,2048,352]{1,2,0:T(8,128)(2,1)} %param.11) | copy-start | bytes 4325380
  117.1 0.7 copy-start.3
  119.1 55.4 %copy-start.4 = (s32[512,1]{0,1:T(1,128)S(1)}, s32[512,1]{0,1:T(1,128)}, u32[]{:S(2)}) copy-start(s32[512,1]{0,1:T(1,128)} %get-tuple-element.13) | copy-start | bytes 6148
  120.9 62.3 %copy-start.8 = (s32[512,1]{0,1:T(1,128)S(1)}, s32[512,1]{0,1:T(1,128)}, u32[]{:S(2)}) copy-start(s32[512,1]{0,1:T(1,128)} %get-tuple-element.23) | copy-start | bytes 6148
  120.9 46.3 %all-to-all-start.3 = ((bf16[96,16,128]{2,0,1:T(8,128)(2,1)}), bf16[96,16,128]{2,0,1:T(8,128)(2,1)}, u32[]{:S(2)}, u32[]{:S(2)}) async-start(bf16[96,16,128]{2,0,1:T(8,128)(2,1)} %bitcast.55), calls=%async_computation.5 | async-start | bytes 786432 | tf_op jit(solution)/shard_map/all_to_all | solution.py:87
  167.3 14.9 %all-to-all-start.1 = ((bf16[96,16,128]{2,0,1:T(8,128)(2,1)}), bf16[96,16,128]{2,0,1:T(8,128)(2,1)}, u32[]{:S(2)}, u32[]{:S(2)}) async-start(bf16[96,16,128]{2,0,1:T(8,128)(2,1)} %bitcast.54), calls=%async_computation.2 | async-start | bytes 786432 | tf_op jit(solution)/shard_map/all_to_all | solution.py:87
  174.5 10.6 %copy-start.7 = (s32[512,1]{0,1:T(1,128)S(1)}, s32[512,1]{0,1:T(1,128)}, u32[]{:S(2)}) copy-start(s32[512,1]{0,1:T(1,128)} %get-tuple-element.11) | copy-start | bytes 6148
  175.1 8.1 %copy-start.10 = (f32[512]{0:T(512)S(1)}, f32[512]{0:T(512)}, u32[]{:S(2)}) copy-start(f32[512]{0:T(512)} %get-tuple-element.21) | copy-start | bytes 6148
  175.1 8.5 %copy-start.9 = (s32[512,1]{0,1:T(1,128)S(1)}, s32[512,1]{0,1:T(1,128)}, u32[]{:S(2)}) copy-start(s32[512,1]{0,1:T(1,128)} %compare_select_fusion.1) | copy-start | bytes 6148
  176.2 0.7 copy-start.2
Sparse Core Ops, SparseCore 0:
  65.8 48.5 reduce-scatter.4
  117.2 48.1 reduce-scatter.2

commit v8 on v6

--- a/solution.py
+++ b/solution.py
@@ -42,7 +42,7 @@
     return (keep.astype(jnp.float32) + got.astype(jnp.float32)).astype(jnp.bfloat16)
 
 
-def make_per_device(expert_axes, mp_axes, experts, mp_count, n_chunks=2):
+def make_per_device(expert_axes, mp_axes, experts, mp_count, n_chunks=2, tc_rows=320):
     def per_device(hidden_in, norm_gain, router_w, choices, w_gate, w_up, w_down):
         tokens_dev, model_width = hidden_in.shape
         capacity = 3 * tokens_dev // experts
@@ -72,6 +72,8 @@
             ).astype(jnp.bfloat16)
             part = jnp.dot(dispatch, normed, preferred_element_type=jnp.float32).astype(jnp.bfloat16)
             part = part.reshape(experts, chunk, model_width)
+            if results:
+                part = lax.optimization_barrier((part, previous))[0]
             arrived = lax.all_to_all(part, expert_axes, split_axis=0, concat_axis=0, tiled=True)
             expert_rows = arrived.reshape(experts * chunk, model_width)
             both = jnp.dot(expert_rows, gate_up, preferred_element_type=jnp.float32)
@@ -80,7 +82,17 @@
             partial_t = lax.dot_general(
                 w_down[0], hidden, (((0,), (1,)), ((), ())), preferred_element_type=jnp.float32
             ).astype(jnp.bfloat16)
-            summed = lax.psum_scatter(partial_t, mp_axes[0], scatter_dimension=0, tiled=True)
+            previous = partial_t
+            if c == n_chunks - 1 and tc_rows:
+                sc_rows = experts * chunk - tc_rows
+                on_sc = lax.psum_scatter(partial_t[:, :sc_rows], mp_axes[0], scatter_dimension=0, tiled=True)
+                z_parts = lax.axis_size(mp_axes[0])
+                on_tc = partial_t[:, sc_rows:].reshape(z_parts, model_width // z_parts, tc_rows)
+                on_tc = lax.all_to_all(on_tc, mp_axes[0], split_axis=0, concat_axis=0, tiled=True)
+                on_tc = on_tc.astype(jnp.float32).sum(axis=0).astype(jnp.bfloat16)
+                summed = jnp.concatenate([on_sc, on_tc], axis=1)
+            else:
+                summed = lax.psum_scatter(partial_t, mp_axes[0], scatter_dimension=0, tiled=True)
             halves = lax.axis_size(mp_axes[1])
             blocks = summed.reshape(halves, slice_width, experts, chunk).transpose(2, 0, 1, 3)
             blocks = blocks.reshape(experts * halves, slice_width, chunk)

time: 192 us -> 208 us (1.083)
  waiting for transfers between devices: 38.9 us -> 57 us
  starting transfers between devices: 13 us -> 18.8 us
  matrix products: 24.5 us -> 19.9 us
  other arithmetic: 8.67 us -> 5.89 us
    all_to_all x0 -> x1, waiting for transfers between devices: none -> 44.1 us  [per_device(): lax.all_to_all(on_tc, mp_axes[0], split_axis=0, concat_axis=0, tiled=True)]
    reduce_scatter x2 -> x1, waiting for transfers between devices: 35.3 us -> 0.02 us  [per_device(): lax.psum_scatter(partial_t, mp_axes[0], scatter_dimension=0, tiled=True)]
    all_to_all x2, waiting for transfers between devices: 3.52 us -> 12.9 us  [per_device(): lax.all_to_all(blocks, expert_axes + mp_axes[1:], split_axis=0, concat_ax...]
    all_to_all x0 -> x1, starting transfers between devices: none -> 8.6 us  [per_device(): lax.all_to_all(on_tc, mp_axes[0], split_axis=0, concat_axis=0, tiled=True)]
    reshape x4, local copies, waits for them, and re-layouts: 7.24 us -> 2.78 us  [per_device(): summed.reshape(halves, slice_width, experts, chunk).transpose(2, 0, 1, 3)]
    all_to_all x2, starting transfers between devices: 12.9 us -> 10.2 us  [per_device(): lax.all_to_all(blocks, expert_axes + mp_axes[1:], split_axis=0, concat_ax...]
    slice x0 -> x3, local copies, waits for them, and re-layouts: none -> 2.68 us  [the longest x1 1.39 us: per_device(): partial_t[:, :sc_rows]]
  transfers between devices with their start and end apart: 4 -> 5, of which waited for: 2 -> 3; matrix products, arithmetic and copies ran while one was open for 12% -> 7% of each run, Pallas kernels for 0% -> 0%
where the time goes in v8:
time: 208 us; the launch traced here: 207 us
  blocking collectives  83.5 us (40%)
  waiting for transfers between devices  57 us (27%)
  matrix products  19.9 us (10%)
  starting transfers between devices  18.8 us (9%)
  between operations  13.7 us (7%)
  local copies, waits for them, and re-layouts  8.37 us (4%)
  other arithmetic  5.89 us (3%)
    all_to_all x2, blocking collectives, per_device(): lax.all_to_all(part, expert_axes, split_axis=0, concat_axis=0, tiled=True)  83.5 us
    all_to_all x1, waiting for transfers between devices, per_device(): lax.all_to_all(on_tc, mp_axes[0], split_axis=0, concat_axis=0, tiled=True)  44.1 us
    all_to_all x2, waiting for transfers between devices, per_device(): lax.all_to_all(blocks, expert_axes + mp_axes[1:], split_axis=0, concat_ax...  12.9 us
    all_to_all x2, starting transfers between devices, per_device(): lax.all_to_all(blocks, expert_axes + mp_axes[1:], split_axis=0, concat_ax...  10.2 us
    all_to_all x1, starting transfers between devices, per_device(): lax.all_to_all(on_tc, mp_axes[0], split_axis=0, concat_axis=0, tiled=True)  8.6 us
    dot_general x2, matrix products, per_device(): lax.dot_general(w_down[0], hidden, (((0,), (1,)), ((), ())), preferred_el...  5.43 us
    dot_general x2, matrix products, per_device(): both = jnp.dot(expert_rows, gate_up, preferred_element_type=jnp.float32)  4.9 us
    dot_general x2, matrix products, per_device(): jnp.dot(dispatch, normed, preferred_element_type=jnp.float32)  4.76 us
  transfers between devices with their start and end apart: 5, of which 3 were waited for; matrix products, arithmetic and copies ran while one was open for 7% of the time, Pallas kernels for 0%

profile of v8, /device:TPU:2, one launch (start us, length us, event | category | flops | bytes accessed | tf_op | source)
XLA Modules:
  0.0 207.3 jit_solution(12082865592029638206)
XLA Ops:
  6.6 2.2 %fusion = f32[512]{0:T(512)S(1)} fusion(bf16[512,2048]{1,0:T(8,128)(2,1)} %param.7), kind=kLoop, calls=%fused_computation.2 | loop fusion | flops 3145216 | bytes 2099200 | tf_op jit(solution)/shard_map/reduce_sum | solution.py:54
  9.1 1.3 select_reduce_fusion
  11.5 2.0 convolution_convert_fusion.3
  13.5 43.1 %all_to_all.25 = bf16[8,96,2048]{2,1,0:T(8,128)(2,1)S(1)} all-to-all(bf16[8,96,2048]{2,1,0:T(8,128)(2,1)S(1)} %bitcast.59), channel_id=1, replica_groups=mesh['dp'=2,'ey'=4,'ex'=2,'mz'=8,'mx'=2] {'ey','ex'}, dimensions={0} | all-to-all | bytes 6291456 | tf_op jit(solution)/shard_map/all_to_all | solution.py:77
  56.7 2.5 %fusion.6 = f32[768,704]{0,1:T(8,128)S(1)} fusion(bf16[768,2048]{1,0:T(8,128)(2,1)S(1)} %bitcast.60, bf16[2048,352]{0,1:T(8,128)(2,1)S(1)} %bitcast.82, bf16[2048,352]{0,1:T(8,128)(2,1)S(1)} %bitcast.84), kind=kOutput, calls=%fused_computation.13 | convolution fusion | flops 2220359680 | bytes 8192000 | tf_op jit(solution)/shard_map/dot_general | solution.py:79
  59.1 3.5 %fusion.3 = bf16[2048,768]{0,1:T(8,128)(2,1)} fusion(bf16[1,352,2048]{2,1,0:T(8,128)(2,1)S(1)} %copy-done, f32[768,704]{0,1:T(8,128)S(1)} %fusion.6), kind=kOutput, calls=%fused_computation.9 | convolution fusion | flops 1110491136 | bytes 6750208 | tf_op jit(solution)/shard_map/dot_general | solution.py:82
  62.8 1.3 convert_remainder_fusion
  64.0 2.7 %convolution_convert_fusion.1 = bf16[768,2048]{1,0:T(8,128)(2,1)S(1)} fusion(s32[512]{0:T(512)S(1)} %get-tuple-element.34, s32[512]{0:T(512)S(1)} %get-tuple-element.37, bf16[512,2048]{1,0:T(8,128)(2,1)S(1)} %copy-done.2, f32[2048]{0:T(1024)} %param.8, f32[512]{0:T(512)} %copy-done.11), kind=kOutput, calls=%fused_computation.6 | convolution fusion | flops 1617559552 | bytes 5257216 | tf_op jit(solution)/shard_map/dot_general | solution.py:73
  66.8 40.4 %all_to_all.26 = bf16[8,96,2048]{2,1,0:T(8,128)(2,1)S(1)} all-to-all(bf16[8,96,2048]{2,1,0:T(8,128)(2,1)S(1)} %bitcast.58), channel_id=1, replica_groups=mesh['dp'=2,'ey'=4,'ex'=2,'mz'=8,'mx'=2] {'ey','ex'}, dimensions={0} | all-to-all | bytes 6291456 | tf_op jit(solution)/shard_map/all_to_all | solution.py:77
  107.2 2.5 %fusion.5 = f32[768,704]{0,1:T(8,128)S(1)} fusion(bf16[768,2048]{1,0:T(8,128)(2,1)S(1)} %bitcast.61, bf16[2048,352]{0,1:T(8,128)(2,1)S(1)} %bitcast.83, bf16[2048,352]{0,1:T(8,128)(2,1)S(1)} %bitcast.85), kind=kOutput, calls=%fused_computation.12 | convolution fusion | flops 2220359680 | bytes 8192000 | tf_op jit(solution)/shard_map/dot_general | solution.py:79
  109.7 1.9 fusion.4
  111.6 1.7 copy-done.1
  113.3 1.4 slice.38
  114.7 1.3 slice-done
  116.0 1.1 copy.15
  117.1 8.6 %all-to-all-start.3 = ((bf16[8,256,320]{1,2,0:T(8,128)(2,1)}), bf16[8,256,320]{1,2,0:T(8,128)(2,1)S(1)}, u32[]{:S(2)}, u32[]{:S(2)}) async-start(bf16[8,256,320]{1,2,0:T(8,128)(2,1)} %bitcast.56), calls=%async_computation.5 | async-start | bytes 2621440 | tf_op jit(solution)/shard_map/all_to_all | solution.py:91
  125.8 1.1 reshape.252
  127.7 44.1 %all-to-all-done.3 = bf16[8,256,320]{1,2,0:T(8,128)(2,1)S(1)} async-done(((bf16[8,256,320]{1,2,0:T(8,128)(2,1)}), bf16[8,256,320]{1,2,0:T(8,128)(2,1)S(1)}, u32[]{:S(2)}, u32[]{:S(2)}) %all-to-all-start.3) | async-done | bytes 1310752 | tf_op jit(solution)/shard_map/all_to_all | solution.py:91
  171.8 5.1 %all-to-all-start.1 = ((bf16[16,128,96]{1,2,0:T(8,128)(2,1)}), bf16[16,128,96]{1,2,0:T(8,128)(2,1)S(1)}, u32[]{:S(2)}, u32[]{:S(2)}) async-start(bf16[16,128,96]{1,2,0:T(8,128)(2,1)} %bitcast.12), calls=%async_computation.2 | async-start | bytes 786432 | tf_op jit(solution)/shard_map/all_to_all | solution.py:99
  177.2 1.0 pad_maximum_fusion.3
  179.1 5.8 %all-to-all-done.1 = bf16[16,128,96]{1,2,0:T(8,128)(2,1)S(1)} async-done(((bf16[16,128,96]{1,2,0:T(8,128)(2,1)}), bf16[16,128,96]{1,2,0:T(8,128)(2,1)S(1)}, u32[]{:S(2)}, u32[]{:S(2)}) %all-to-all-start.1) | async-done | bytes 393248 | tf_op jit(solution)/shard_map/all_to_all | solution.py:99
  184.9 5.1 %all-to-all-start.4 = ((bf16[16,128,96]{1,2,0:T(8,128)(2,1)}), bf16[16,128,96]{1,2,0:T(8,128)(2,1)S(1)}, u32[]{:S(2)}, u32[]{:S(2)}) async-start(bf16[16,128,96]{1,2,0:T(8,128)(2,1)} %bitcast.25), calls=%async_computation.6 | async-start | bytes 786432 | tf_op jit(solution)/shard_map/all_to_all | solution.py:99
  190.5 7.0 %all-to-all-done.4 = bf16[16,128,96]{1,2,0:T(8,128)(2,1)S(1)} async-done(((bf16[16,128,96]{1,2,0:T(8,128)(2,1)}), bf16[16,128,96]{1,2,0:T(8,128)(2,1)S(1)}, u32[]{:S(2)}, u32[]{:S(2)}) %all-to-all-start.4) | async-done | bytes 393248 | tf_op jit(solution)/shard_map/all_to_all | solution.py:99
  198.4 2.0 fusion.25
  (64 shorter events, 4.8 us)
Async XLA Ops:
  6.5 52.6 %copy-start = (bf16[1,352,2048]{2,1,0:T(8,128)(2,1)S(1)}, bf16[1,352,2048]{2,1,0:T(8,128)(2,1)}, u32[]{:S(2)}) copy-start(bf16[1,352,2048]{2,1,0:T(8,128)(2,1)} %param.13) | copy-start | bytes 4325380
  6.5 2.5 %copy-start.2 = (bf16[512,2048]{1,0:T(8,128)(2,1)S(1)}, bf16[512,2048]{1,0:T(8,128)(2,1)}, u32[]{:S(2)}) copy-start(bf16[512,2048]{1,0:T(8,128)(2,1)} %param.7) | copy-start | bytes 6291460
  6.5 2.3 %copy-start.3 = (s32[512,2]{0,1:T(2,128)S(1)}, s32[512,2]{0,1:T(2,128)}, u32[]{:S(2)}) copy-start(s32[512,2]{0,1:T(2,128)} %param.10) | copy-start | bytes 12292
  6.5 119.3 %reduce-scatter.3.cloned.1.call-start = ((), (), s32[]{:S(2)}) async-start(), calls=%async_computation.7 | async-start | bytes 3538944 | tf_op jit(solution)/shard_map/reduce_scatter | solution.py:95
  6.5 2.5 %copy-start.18 = (bf16[2048,8]{0,1:T(8,128)(2,1)S(1)}, bf16[2048,8]{0,1:T(8,128)(2,1)}, u32[]{:S(2)}) copy-start(bf16[2048,8]{0,1:T(8,128)(2,1)} %param.9) | copy-start | bytes 98308
  6.6 2.5 %copy-start.19 = (f32[2048]{0:T(1024)S(1)}, f32[2048]{0:T(1024)}, u32[]{:S(2)}) copy-start(f32[2048]{0:T(1024)} %param.8) | copy-start | bytes 24580
  8.8 2.7 %copy-start.11 = (f32[512]{0:T(512)}, f32[512]{0:T(512)S(1)}, u32[]{:S(2)}) copy-start(f32[512]{0:T(512)S(1)} %add_rsqrt_fusion) | copy-start | bytes 6148
  13.5 43.2 %copy-start.14 = (bf16[1,2048,352]{1,2,0:T(8,128)(2,1)S(1)}, bf16[1,2048,352]{1,2,0:T(8,128)(2,1)}, u32[]{:S(2)}) copy-start(bf16[1,2048,352]{1,2,0:T(8,128)(2,1)} %param.12) | copy-start | bytes 4325380
  13.5 43.1 %copy-start.16 = (bf16[1,2048,352]{1,2,0:T(8,128)(2,1)S(1)}, bf16[1,2048,352]{1,2,0:T(8,128)(2,1)}, u32[]{:S(2)}) copy-start(bf16[1,2048,352]{1,2,0:T(8,128)(2,1)} %param.11) | copy-start | bytes 4325380
  62.7 114.5 %reduce-scatter.5.cloned.1.call-start = ((), (), s32[]{:S(2)}) async-start(), calls=%async_computation.8 | async-start | bytes 2064384 | tf_op jit(solution)/shard_map/reduce_scatter | solution.py:88
  66.8 40.4 %copy-start.15 = (bf16[1,2048,352]{1,2,0:T(8,128)(2,1)S(1)}, bf16[1,2048,352]{1,2,0:T(8,128)(2,1)}, u32[]{:S(2)}) copy-start(bf16[1,2048,352]{1,2,0:T(8,128)(2,1)} %param.12) | copy-start | bytes 4325380
  66.8 40.4 %copy-start.17 = (bf16[1,2048,352]{1,2,0:T(8,128)(2,1)S(1)}, bf16[1,2048,352]{1,2,0:T(8,128)(2,1)}, u32[]{:S(2)}) copy-start(bf16[1,2048,352]{1,2,0:T(8,128)(2,1)} %param.11) | copy-start | bytes 4325380
  111.6 1.7 copy-start.1
  114.6 1.3 slice-start
  116.0 9.8 %copy-start.4 = (s32[512]{0:T(512)S(1)}, s32[512]{0:T(512)}, u32[]{:S(2)}) copy-start(s32[512]{0:T(512)} %get-tuple-element.35) | copy-start | bytes 6148
  116.0 9.8 %copy-start.5 = (s32[512]{0:T(512)S(1)}, s32[512]{0:T(512)}, u32[]{:S(2)}) copy-start(s32[512]{0:T(512)} %get-tuple-element.36) | copy-start | bytes 6148
  116.0 9.8 %copy-start.6 = (s32[512]{0:T(512)S(1)}, s32[512]{0:T(512)}, u32[]{:S(2)}) copy-start(s32[512]{0:T(512)} %get-tuple-element.38) | copy-start | bytes 6148
  116.0 9.8 %copy-start.9 = (pred[512]{0:T(512)(128)(4,1)S(1)}, pred[512]{0:T(512)(128)(4,1)}, u32[]{:S(2)}) copy-start(pred[512]{0:T(512)(128)(4,1)} %get-tuple-element.24) | copy-start | bytes 1540
  116.0 9.8 %copy-start.10 = (pred[512]{0:T(512)(128)(4,1)S(1)}, pred[512]{0:T(512)(128)(4,1)}, u32[]{:S(2)}) copy-start(pred[512]{0:T(512)(128)(4,1)} %get-tuple-element.22) | copy-start | bytes 1540
  117.1 59.8 %copy-start.12 = (f32[512]{0:T(512)S(1)}, f32[512]{0:T(512)}, u32[]{:S(2)}) copy-start(f32[512]{0:T(512)} %get-tuple-element.9) | copy-start | bytes 6148
  117.1 59.8 %copy-start.13 = (f32[512]{0:T(512)S(1)}, f32[512]{0:T(512)}, u32[]{:S(2)}) copy-start(f32[512]{0:T(512)} %get-tuple-element.10) | copy-start | bytes 6148
  117.1 54.7 %all-to-all-start.3 = ((bf16[8,256,320]{1,2,0:T(8,128)(2,1)}), bf16[8,256,320]{1,2,0:T(8,128)(2,1)S(1)}, u32[]{:S(2)}, u32[]{:S(2)}) async-start(bf16[8,256,320]{1,2,0:T(8,128)(2,1)} %bitcast.56), calls=%async_computation.5 | async-start | bytes 2621440 | tf_op jit(solution)/shard_map/all_to_all | solution.py:91
  171.8 13.1 %all-to-all-start.1 = ((bf16[16,128,96]{1,2,0:T(8,128)(2,1)}), bf16[16,128,96]{1,2,0:T(8,128)(2,1)S(1)}, u32[]{:S(2)}, u32[]{:S(2)}) async-start(bf16[16,128,96]{1,2,0:T(8,128)(2,1)} %bitcast.12), calls=%async_computation.2 | async-start | bytes 786432 | tf_op jit(solution)/shard_map/all_to_all | solution.py:99
  184.9 12.6 %all-to-all-start.4 = ((bf16[16,128,96]{1,2,0:T(8,128)(2,1)}), bf16[16,128,96]{1,2,0:T(8,128)(2,1)S(1)}, u32[]{:S(2)}, u32[]{:S(2)}) async-start(bf16[16,128,96]{1,2,0:T(8,128)(2,1)} %bitcast.25), calls=%async_computation.6 | async-start | bytes 786432 | tf_op jit(solution)/shard_map/all_to_all | solution.py:99
  (2 other events, 2.1 us)
Sparse Core Ops, SparseCore 0:
  62.8 48.5 reduce-scatter.2
  114.8 59.7 reduce-scatter.4

commit v9 on v6

--- a/solution.py
+++ b/solution.py
@@ -92,11 +92,10 @@
         w0, w1 = pair_weights(logits, oh0, oh1)
         dims = (((1,), (1,)), ((), ()))
         for r0, r1, returned in results:
-            sel0 = (r0[:, None] == chunk_rows[None, :]).astype(jnp.bfloat16)
-            sel1 = (r1[:, None] == chunk_rows[None, :]).astype(jnp.bfloat16)
-            out0 = lax.dot_general(sel0, returned, dims, preferred_element_type=jnp.float32)
-            out1 = lax.dot_general(sel1, returned, dims, preferred_element_type=jnp.float32)
-            term = out0 * w0[:, None] + out1 * w1[:, None]
+            both_rows = jnp.concatenate([r0, r1])
+            sel = (both_rows[:, None] == chunk_rows[None, :]).astype(jnp.bfloat16)
+            out = lax.dot_general(sel, returned, dims, preferred_element_type=jnp.float32)
+            term = out[:tokens_dev] * w0[:, None] + out[tokens_dev:] * w1[:, None]
             mixture = term if mixture is None else mixture + term
         return (residual + mixture).astype(jnp.bfloat16)
 

time: 192 us -> 189 us (0.984)
  matrix products: 24.5 us -> 20.5 us
  waiting for transfers between devices: 38.9 us -> 42.1 us
  other arithmetic: 8.67 us -> 6.5 us
    dot_general x4 -> x2, matrix products: 6.14 us -> 2.17 us  [per_device(): lax.dot_general(sel, returned, dims, preferred_element_type=jnp.float32)]
  transfers between devices with their start and end apart: 4 -> 4, of which waited for: 2 -> 2; matrix products, arithmetic and copies ran while one was open for 12% -> 11% of each run, Pallas kernels for 0% -> 0%
where the time goes in v9:
time: 189 us; the launch traced here: 188 us
  blocking collectives  83.5 us (44%)
  waiting for transfers between devices  42.1 us (22%)
  matrix products  20.5 us (11%)
  starting transfers between devices  13.7 us (7%)
  between operations  13.6 us (7%)
  local copies, waits for them, and re-layouts  8.17 us (4%)
  other arithmetic  6.5 us (3%)
    all_to_all x2, blocking collectives, per_device(): lax.all_to_all(part, expert_axes, split_axis=0, concat_axis=0, tiled=True)  83.5 us
    reduce_scatter x2, waiting for transfers between devices, per_device(): lax.psum_scatter(partial_t, mp_axes[0], scatter_dimension=0, tiled=True)  37 us
    all_to_all x2, starting transfers between devices, per_device(): lax.all_to_all(blocks, expert_axes + mp_axes[1:], split_axis=0, concat_ax...  13.7 us
    reshape x4, local copies, waits for them, and re-layouts, per_device(): summed.reshape(halves, slice_width, experts, chunk).transpose(2, 0, 1, 3)  7.25 us
    dot_general x2, matrix products, per_device(): lax.dot_general(w_down[0], hidden, (((0,), (1,)), ((), ())), preferred_el...  7.15 us
    all_to_all x2, waiting for transfers between devices, per_device(): lax.all_to_all(blocks, expert_axes + mp_axes[1:], split_axis=0, concat_ax...  5.11 us
    dot_general x2, matrix products, per_device(): both = jnp.dot(expert_rows, gate_up, preferred_element_type=jnp.float32)  4.89 us
    dot_general x2, matrix products, per_device(): jnp.dot(dispatch, normed, preferred_element_type=jnp.float32)  4.77 us
  transfers between devices with their start and end apart: 4, of which 2 were waited for; matrix products, arithmetic and copies ran while one was open for 11% of the time, Pallas kernels for 0%

profile of v9, /device:TPU:2, one launch (start us, length us, event | category | flops | bytes accessed | tf_op | source)
XLA Modules:
  0.0 188.2 jit_solution(6413292991728165955)
XLA Ops:
  6.6 0.9 fusion.53
  7.4 2.1 %fusion = f32[512]{0:T(512)S(1)} fusion(bf16[512,2048]{1,0:T(8,128)(2,1)} %param.7), kind=kLoop, calls=%fused_computation.2 | loop fusion | flops 3145216 | bytes 2099200 | tf_op jit(solution)/shard_map/reduce_sum | solution.py:54
  9.9 1.3 select_reduce_fusion
  11.2 2.0 %convolution_convert_fusion.3 = bf16[768,2048]{1,0:T(8,128)(2,1)S(1)} fusion(s32[512]{0:T(512)S(1)} %get-tuple-element.15, s32[512]{0:T(512)S(1)} %get-tuple-element.20, bf16[512,2048]{1,0:T(8,128)(2,1)S(1)} %copy-done.1, f32[2048]{0:T(1024)S(1)} %copy-done.11, f32[512]{0:T(512)S(1)} %add_rsqrt_fusion), kind=kOutput, calls=%fused_computation.8 | convolution fusion | flops 1617559552 | bytes 5257216 | tf_op jit(solution)/shard_map/dot_general | solution.py:73
  13.3 43.1 %all_to_all.20 = bf16[8,96,2048]{2,1,0:T(8,128)(2,1)S(1)} all-to-all(bf16[8,96,2048]{2,1,0:T(8,128)(2,1)S(1)} %bitcast.45), channel_id=1, replica_groups=mesh['dp'=2,'ey'=4,'ex'=2,'mz'=8,'mx'=2] {'ey','ex'}, dimensions={0} | all-to-all | bytes 6291456 | tf_op jit(solution)/shard_map/all_to_all | solution.py:75
  56.4 2.4 %fusion.8 = f32[768,704]{0,1:T(8,128)S(1)} fusion(bf16[768,2048]{1,0:T(8,128)(2,1)S(1)} %bitcast.42, bf16[2048,352]{0,1:T(8,128)(2,1)S(1)} %bitcast.56, bf16[2048,352]{0,1:T(8,128)(2,1)S(1)} %bitcast.58), kind=kOutput, calls=%fused_computation.17 | convolution fusion | flops 2220359680 | bytes 8192000 | tf_op jit(solution)/shard_map/dot_general | solution.py:77
  58.9 3.6 %fusion.5 = bf16[2048,768]{0,1:T(8,128)(2,1)} fusion(bf16[1,352,2048]{2,1,0:T(8,128)(2,1)S(1)} %copy-done, f32[768,704]{0,1:T(8,128)S(1)} %fusion.8), kind=kOutput, calls=%fused_computation.13 | convolution fusion | flops 1110491136 | bytes 6750208 | tf_op jit(solution)/shard_map/dot_general | solution.py:80
  62.6 2.7 %convolution_convert_fusion.1 = bf16[768,2048]{1,0:T(8,128)(2,1)S(1)} fusion(s32[512]{0:T(512)S(1)} %get-tuple-element.16, s32[512]{0:T(512)S(1)} %get-tuple-element.19, bf16[512,2048]{1,0:T(8,128)(2,1)S(1)} %copy-done.1, f32[2048]{0:T(1024)} %param.8, f32[512]{0:T(512)} %copy-done.4), kind=kOutput, calls=%fused_computation.6 | convolution fusion | flops 1617559552 | bytes 5257216 | tf_op jit(solution)/shard_map/dot_general | solution.py:73
  65.3 40.4 %all_to_all.21 = bf16[8,96,2048]{2,1,0:T(8,128)(2,1)S(1)} all-to-all(bf16[8,96,2048]{2,1,0:T(8,128)(2,1)S(1)} %bitcast.43), channel_id=1, replica_groups=mesh['dp'=2,'ey'=4,'ex'=2,'mz'=8,'mx'=2] {'ey','ex'}, dimensions={0} | all-to-all | bytes 6291456 | tf_op jit(solution)/shard_map/all_to_all | solution.py:75
  105.7 2.5 %fusion.7 = f32[768,704]{0,1:T(8,128)S(1)} fusion(bf16[768,2048]{1,0:T(8,128)(2,1)S(1)} %bitcast.44, bf16[2048,352]{0,1:T(8,128)(2,1)S(1)} %bitcast.57, bf16[2048,352]{0,1:T(8,128)(2,1)S(1)} %bitcast.59), kind=kOutput, calls=%fused_computation.16 | convolution fusion | flops 2220359680 | bytes 8192000 | tf_op jit(solution)/shard_map/dot_general | solution.py:77
  108.2 3.6 %fusion.6 = bf16[2048,768]{0,1:T(8,128)(2,1)} fusion(bf16[1,352,2048]{2,1,0:T(8,128)(2,1)S(1)} %copy-done, f32[768,704]{0,1:T(8,128)S(1)} %fusion.7), kind=kOutput, calls=%fused_computation.14 | convolution fusion | flops 1110491136 | bytes 6750208 | tf_op jit(solution)/shard_map/dot_general | solution.py:80
  111.8 1.8 reshape.123
  113.6 1.8 copy.8
  115.4 6.7 %all-to-all-start.1 = ((bf16[16,128,96]{1,2,0:T(8,128)(2,1)}), bf16[16,128,96]{1,2,0:T(8,128)(2,1)}, u32[]{:S(2)}, u32[]{:S(2)}) async-start(bf16[16,128,96]{1,2,0:T(8,128)(2,1)} %bitcast.46), calls=%async_computation.2 | async-start | bytes 786432 | tf_op jit(solution)/shard_map/all_to_all | solution.py:87
  122.7 0.7 broadcast_subtract_fusion
  123.4 37.0 %reduce-scatter.5.cloned.1.call-done = bf16[256,768]{0,1:T(8,128)(2,1)} async-done(((bf16[2048,768]{0,1:T(8,128)(2,1)}), bf16[256,768]{0,1:T(8,128)(2,1)}) %reduce-scatter.5.cloned.1.call-update) | async-done | bytes 393232 | tf_op jit(solution)/shard_map/reduce_scatter | solution.py:83
  160.4 1.8 reshape.129
  162.2 1.8 copy.9
  164.0 7.0 %all-to-all-start.3 = ((bf16[16,128,96]{1,2,0:T(8,128)(2,1)}), bf16[16,128,96]{1,2,0:T(8,128)(2,1)}, u32[]{:S(2)}, u32[]{:S(2)}) async-start(bf16[16,128,96]{1,2,0:T(8,128)(2,1)} %bitcast.47), calls=%async_computation.5 | async-start | bytes 786432 | tf_op jit(solution)/shard_map/all_to_all | solution.py:87
  171.0 1.0 bitcast_reduce_fusion.1
  172.1 1.5 fusion.3
  173.6 5.1 %all-to-all-done.3 = bf16[16,128,96]{1,2,0:T(8,128)(2,1)} async-done(((bf16[16,128,96]{1,2,0:T(8,128)(2,1)}), bf16[16,128,96]{1,2,0:T(8,128)(2,1)}, u32[]{:S(2)}, u32[]{:S(2)}) %all-to-all-start.3) | async-done | bytes 393248 | tf_op jit(solution)/shard_map/all_to_all | solution.py:87
  178.7 1.1 bitcast_reduce_fusion
  180.5 0.9 fusion.31
  (36 shorter events, 1.7 us)
Async XLA Ops:
  6.5 52.4 %copy-start = (bf16[1,352,2048]{2,1,0:T(8,128)(2,1)S(1)}, bf16[1,352,2048]{2,1,0:T(8,128)(2,1)}, u32[]{:S(2)}) copy-start(bf16[1,352,2048]{2,1,0:T(8,128)(2,1)} %param.13) | copy-start | bytes 4325380
  6.5 3.3 %copy-start.1 = (bf16[512,2048]{1,0:T(8,128)(2,1)S(1)}, bf16[512,2048]{1,0:T(8,128)(2,1)}, u32[]{:S(2)}) copy-start(bf16[512,2048]{1,0:T(8,128)(2,1)} %param.7) | copy-start | bytes 6291460
  6.5 3.3 %copy-start.10 = (f32[2048]{0:T(1024)S(1)}, f32[2048]{0:T(1024)}, u32[]{:S(2)}) copy-start(f32[2048]{0:T(1024)} %param.8) | copy-start | bytes 24580
  6.5 105.3 %reduce-scatter.3.cloned.1.call-start = ((), (), s32[]{:S(2)}) async-start(), calls=%async_computation.6 | async-start | bytes 3538944 | tf_op jit(solution)/shard_map/reduce_scatter | solution.py:83
  6.5 3.3 %copy-start.9 = (bf16[2048,8]{0,1:T(8,128)(2,1)S(1)}, bf16[2048,8]{0,1:T(8,128)(2,1)}, u32[]{:S(2)}) copy-start(bf16[2048,8]{0,1:T(8,128)(2,1)} %param.9) | copy-start | bytes 98308
  9.6 1.7 copy-start.11
  9.6 3.7 %copy-start.4 = (f32[512]{0:T(512)}, f32[512]{0:T(512)S(1)}, u32[]{:S(2)}) copy-start(f32[512]{0:T(512)S(1)} %add_rsqrt_fusion) | copy-start | bytes 6148
  13.3 43.1 %copy-start.5 = (bf16[1,2048,352]{1,2,0:T(8,128)(2,1)S(1)}, bf16[1,2048,352]{1,2,0:T(8,128)(2,1)}, u32[]{:S(2)}) copy-start(bf16[1,2048,352]{1,2,0:T(8,128)(2,1)} %param.12) | copy-start | bytes 4325380
  13.3 43.1 %copy-start.7 = (bf16[1,2048,352]{1,2,0:T(8,128)(2,1)S(1)}, bf16[1,2048,352]{1,2,0:T(8,128)(2,1)}, u32[]{:S(2)}) copy-start(bf16[1,2048,352]{1,2,0:T(8,128)(2,1)} %param.11) | copy-start | bytes 4325380
  62.5 97.9 %reduce-scatter.5.cloned.1.call-start = ((), (), s32[]{:S(2)}) async-start(), calls=%async_computation.7 | async-start | bytes 3538944 | tf_op jit(solution)/shard_map/reduce_scatter | solution.py:83
  65.3 40.4 %copy-start.6 = (bf16[1,2048,352]{1,2,0:T(8,128)(2,1)S(1)}, bf16[1,2048,352]{1,2,0:T(8,128)(2,1)}, u32[]{:S(2)}) copy-start(bf16[1,2048,352]{1,2,0:T(8,128)(2,1)} %param.12) | copy-start | bytes 4325380
  65.3 40.4 %copy-start.8 = (bf16[1,2048,352]{1,2,0:T(8,128)(2,1)S(1)}, bf16[1,2048,352]{1,2,0:T(8,128)(2,1)}, u32[]{:S(2)}) copy-start(bf16[1,2048,352]{1,2,0:T(8,128)(2,1)} %param.11) | copy-start | bytes 4325380
  115.4 48.6 %all-to-all-start.1 = ((bf16[16,128,96]{1,2,0:T(8,128)(2,1)}), bf16[16,128,96]{1,2,0:T(8,128)(2,1)}, u32[]{:S(2)}, u32[]{:S(2)}) async-start(bf16[16,128,96]{1,2,0:T(8,128)(2,1)} %bitcast.46), calls=%async_computation.2 | async-start | bytes 786432 | tf_op jit(solution)/shard_map/all_to_all | solution.py:87
  122.7 49.4 %copy-start.3 = (s32[1024]{0:T(1024)S(1)}, s32[1024]{0:T(1024)}, u32[]{:S(2)}) copy-start(s32[1024]{0:T(1024)} %pad_add_fusion) | copy-start | bytes 12292
  164.0 14.7 %all-to-all-start.3 = ((bf16[16,128,96]{1,2,0:T(8,128)(2,1)}), bf16[16,128,96]{1,2,0:T(8,128)(2,1)}, u32[]{:S(2)}, u32[]{:S(2)}) async-start(bf16[16,128,96]{1,2,0:T(8,128)(2,1)} %bitcast.47), calls=%async_computation.5 | async-start | bytes 786432 | tf_op jit(solution)/shard_map/all_to_all | solution.py:87
  178.7 1.8 copy-start.2
Sparse Core Ops, SparseCore 0:
  62.6 48.5 reduce-scatter.2
  113.8 46.5 reduce-scatter.4

commit v10 on v9

--- a/solution.py
+++ b/solution.py
@@ -42,7 +42,7 @@
     return (keep.astype(jnp.float32) + got.astype(jnp.float32)).astype(jnp.bfloat16)
 
 
-def make_per_device(expert_axes, mp_axes, experts, mp_count, n_chunks=2):
+def make_per_device(expert_axes, mp_axes, experts, mp_count):
     def per_device(hidden_in, norm_gain, router_w, choices, w_gate, w_up, w_down):
         tokens_dev, model_width = hidden_in.shape
         capacity = 3 * tokens_dev // experts
@@ -55,23 +55,29 @@
             * norm_gain
         ).astype(jnp.bfloat16)
         slot0, slot1, oh0, oh1 = pair_slots(choices, experts)
-        chunk = capacity // n_chunks
+        lead = capacity // 2 + capacity // 24
+        sizes = [lead, capacity - lead]
+        offsets = [0, lead]
         e0, e1 = choices[:, 0], choices[:, 1]
-        chunk_rows = jnp.arange(experts * chunk, dtype=jnp.int32)
         column = lax.axis_index(mp_axes) * slice_width
         residual = lax.dynamic_slice_in_dim(hidden_in, column, slice_width, 1).astype(jnp.float32)
         mixture = None
         ff_share = w_gate.shape[2]
         gate_up = jnp.concatenate([w_gate[0], w_up[0]], axis=1)
         results = []
-        for c in range(n_chunks):
-            r0 = jnp.where(slot0 // chunk == c, e0 * chunk + slot0 % chunk, -1)
-            r1 = jnp.where(slot1 // chunk == c, e1 * chunk + slot1 % chunk, -1)
+        for chunk, first in zip(sizes, offsets):
+            chunk_rows = jnp.arange(experts * chunk, dtype=jnp.int32)
+            inside0 = (slot0 >= first) & (slot0 < first + chunk)
+            inside1 = (slot1 >= first) & (slot1 < first + chunk)
+            r0 = jnp.where(inside0, e0 * chunk + slot0 - first, -1)
+            r1 = jnp.where(inside1, e1 * chunk + slot1 - first, -1)
             dispatch = (
                 (r0[None, :] == chunk_rows[:, None]) | (r1[None, :] == chunk_rows[:, None])
             ).astype(jnp.bfloat16)
             part = jnp.dot(dispatch, normed, preferred_element_type=jnp.float32).astype(jnp.bfloat16)
             part = part.reshape(experts, chunk, model_width)
+            if results:
+                part = lax.optimization_barrier((part, previous))[0]
             arrived = lax.all_to_all(part, expert_axes, split_axis=0, concat_axis=0, tiled=True)
             expert_rows = arrived.reshape(experts * chunk, model_width)
             both = jnp.dot(expert_rows, gate_up, preferred_element_type=jnp.float32)
@@ -80,6 +86,7 @@
             partial_t = lax.dot_general(
                 w_down[0], hidden, (((0,), (1,)), ((), ())), preferred_element_type=jnp.float32
             ).astype(jnp.bfloat16)
+            previous = partial_t
             summed = lax.psum_scatter(partial_t, mp_axes[0], scatter_dimension=0, tiled=True)
             halves = lax.axis_size(mp_axes[1])
             blocks = summed.reshape(halves, slice_width, experts, chunk).transpose(2, 0, 1, 3)
@@ -87,11 +94,11 @@
             got = lax.all_to_all(blocks, expert_axes + mp_axes[1:], split_axis=0, concat_axis=0, tiled=True)
             got = got.reshape(experts, halves, slice_width, chunk).astype(jnp.float32).sum(axis=1)
             returned = got.astype(jnp.bfloat16).transpose(1, 0, 2).reshape(slice_width, experts * chunk)
-            results.append((r0, r1, returned))
+            results.append((r0, r1, returned, chunk_rows))
         logits = jnp.dot(normed, router_w, preferred_element_type=jnp.float32)
         w0, w1 = pair_weights(logits, oh0, oh1)
         dims = (((1,), (1,)), ((), ()))
-        for r0, r1, returned in results:
+        for r0, r1, returned, chunk_rows in results:
             both_rows = jnp.concatenate([r0, r1])
             sel = (both_rows[:, None] == chunk_rows[None, :]).astype(jnp.bfloat16)
             out = lax.dot_general(sel, returned, dims, preferred_element_type=jnp.float32)

time: 189 us -> 192 us (1.016)
  transfers between devices with their start and end apart: 4 -> 4, of which waited for: 2 -> 3; matrix products, arithmetic and copies ran while one was open for 11% -> 10% of each run, Pallas kernels for 0% -> 0%
where the time goes in v10:
time: 192 us
  blocking collectives  83.5 us (43%)
  waiting for transfers between devices  43.8 us (23%)
  matrix products  21.3 us (11%)
  starting transfers between devices  14.6 us (8%)
  between operations  13.6 us (7%)
  local copies, waits for them, and re-layouts  8.2 us (4%)
  other arithmetic  6.49 us (3%)
    all_to_all x2, blocking collectives, per_device(): lax.all_to_all(part, expert_axes, split_axis=0, concat_axis=0, tiled=True)  83.5 us
    reduce_scatter x2, waiting for transfers between devices, per_device(): lax.psum_scatter(partial_t, mp_axes[0], scatter_dimension=0, tiled=True)  38.9 us
    all_to_all x2, starting transfers between devices, per_device(): lax.all_to_all(blocks, expert_axes + mp_axes[1:], split_axis=0, concat_ax...  14.6 us
    reshape x4, local copies, waits for them, and re-layouts, per_device(): summed.reshape(halves, slice_width, experts, chunk).transpose(2, 0, 1, 3)  7.28 us
    dot_general x2, matrix products, per_device(): lax.dot_general(w_down[0], hidden, (((0,), (1,)), ((), ())), preferred_el...  7.08 us
    dot_general x2, matrix products, per_device(): both = jnp.dot(expert_rows, gate_up, preferred_element_type=jnp.float32)  5.61 us
    all_to_all x2, waiting for transfers between devices, per_device(): lax.all_to_all(blocks, expert_axes + mp_axes[1:], split_axis=0, concat_ax...  4.88 us
    dot_general x2, matrix products, per_device(): jnp.dot(dispatch, normed, preferred_element_type=jnp.float32)  4.74 us
  transfers between devices with their start and end apart: 4, of which 3 were waited for; matrix products, arithmetic and copies ran while one was open for 10% of the time, Pallas kernels for 0%

profile of v10, /device:TPU:2, one launch (start us, length us, event | category | flops | bytes accessed | tf_op | source)
XLA Modules:
  0.0 191.5 jit_solution(3284839402353592228)
XLA Ops:
  6.6 0.9 fusion.51
  7.4 2.1 %fusion = f32[512]{0:T(512)S(1)} fusion(bf16[512,2048]{1,0:T(8,128)(2,1)} %param.7), kind=kLoop, calls=%fused_computation.2 | loop fusion | flops 3145216 | bytes 2099200 | tf_op jit(solution)/shard_map/reduce_sum | solution.py:54
  9.9 1.3 select_reduce_fusion
  11.2 2.2 %convolution_convert_fusion.1 = bf16[832,2048]{1,0:T(8,128)(2,1)S(1)} fusion(s32[512]{0:T(512)S(1)} %get-tuple-element.17, s32[512]{0:T(512)S(1)} %get-tuple-element.22, bf16[512,2048]{1,0:T(8,128)(2,1)S(1)} %copy-done.1, f32[2048]{0:T(1024)S(1)} %copy-done.11, f32[512]{0:T(512)S(1)} %add_rsqrt_fusion), kind=kOutput, calls=%fused_computation.8 | convolution fusion | flops 1752006656 | bytes 5519360 | tf_op jit(solution)/shard_map/dot_general | solution.py:77
  13.4 46.0 %all_to_all.20 = bf16[8,104,2048]{2,1,0:T(8,128)(2,1)S(1)} all-to-all(bf16[8,104,2048]{2,1,0:T(8,128)(2,1)S(1)} %bitcast.43), channel_id=1, replica_groups=mesh['dp'=2,'ey'=4,'ex'=2,'mz'=8,'mx'=2] {'ey','ex'}, dimensions={0} | all-to-all | bytes 6815744 | tf_op jit(solution)/shard_map/all_to_all | solution.py:81
  59.4 3.2 %fusion.8 = f32[832,704]{0,1:T(8,128)S(1)} fusion(bf16[832,2048]{1,0:T(8,128)(2,1)S(1)} %bitcast.42, bf16[2048,352]{0,1:T(8,128)(2,1)S(1)} %bitcast.56, bf16[2048,352]{0,1:T(8,128)(2,1)S(1)} %bitcast.58), kind=kOutput, calls=%fused_computation.17 | convolution fusion | flops 2404909056 | bytes 8634368 | tf_op jit(solution)/shard_map/dot_general | solution.py:83
  62.6 3.7 %fusion.5 = bf16[2048,832]{0,1:T(8,128)(2,1)} fusion(bf16[1,352,2048]{2,1,0:T(8,128)(2,1)S(1)} %copy-done, f32[832,704]{0,1:T(8,128)S(1)} %fusion.8), kind=kOutput, calls=%fused_computation.13 | convolution fusion | flops 1203032064 | bytes 7192576 | tf_op jit(solution)/shard_map/dot_general | solution.py:86
  66.4 2.6 %convolution_convert_fusion.3 = bf16[704,2048]{1,0:T(8,128)(2,1)S(1)} fusion(s32[512]{0:T(512)S(1)} %get-tuple-element.18, s32[512]{0:T(512)S(1)} %get-tuple-element.21, bf16[512,2048]{1,0:T(8,128)(2,1)S(1)} %copy-done.1, f32[2048]{0:T(1024)} %param.8, f32[512]{0:T(512)} %copy-done.4), kind=kOutput, calls=%fused_computation.10 | convolution fusion | flops 1483112448 | bytes 4995072 | tf_op jit(solution)/shard_map/dot_general | solution.py:77
  69.0 37.6 %all_to_all.21 = bf16[8,88,2048]{2,1,0:T(8,128)(2,1)S(1)} all-to-all(bf16[8,88,2048]{2,1,0:T(8,128)(2,1)S(1)} %bitcast.44), channel_id=1, replica_groups=mesh['dp'=2,'ey'=4,'ex'=2,'mz'=8,'mx'=2] {'ey','ex'}, dimensions={0} | all-to-all | bytes 5767168 | tf_op jit(solution)/shard_map/all_to_all | solution.py:81
  106.6 2.4 %fusion.7 = f32[704,704]{1,0:T(8,128)S(1)} fusion(bf16[704,2048]{1,0:T(8,128)(2,1)S(1)} %bitcast.45, bf16[2048,352]{0,1:T(8,128)(2,1)S(1)} %bitcast.57, bf16[2048,352]{0,1:T(8,128)(2,1)S(1)} %bitcast.59), kind=kOutput, calls=%fused_computation.16 | convolution fusion | flops 2035810304 | bytes 7749632 | tf_op jit(solution)/shard_map/dot_general | solution.py:83
  109.0 3.3 %fusion.6 = bf16[2048,704]{0,1:T(8,128)(2,1)} fusion(bf16[1,352,2048]{2,1,0:T(8,128)(2,1)S(1)} %copy-done, f32[704,704]{1,0:T(8,128)S(1)} %fusion.7), kind=kOutput, calls=%fused_computation.14 | convolution fusion | flops 1017950208 | bytes 6307840 | tf_op jit(solution)/shard_map/dot_general | solution.py:86
  112.4 3.6 %reduce-scatter.3.cloned.1.call-done = bf16[256,832]{0,1:T(8,128)(2,1)} async-done(((bf16[2048,832]{0,1:T(8,128)(2,1)}), bf16[256,832]{0,1:T(8,128)(2,1)}) %reduce-scatter.3.cloned.1.call-update) | async-done | bytes 426000 | tf_op jit(solution)/shard_map/reduce_scatter | solution.py:90
  116.0 1.9 reshape.115
  117.8 1.8 copy.8
  119.6 7.3 %all-to-all-start.1 = ((bf16[16,128,104]{1,2,0:T(8,128)(2,1)}), bf16[16,128,104]{1,2,0:T(8,128)(2,1)}, u32[]{:S(2)}, u32[]{:S(2)}) async-start(bf16[16,128,104]{1,2,0:T(8,128)(2,1)} %bitcast.46), calls=%async_computation.2 | async-start | bytes 851968 | tf_op jit(solution)/shard_map/all_to_all | solution.py:94
  128.2 35.3 %reduce-scatter.5.cloned.1.call-done = bf16[256,704]{0,1:T(8,128)(2,1)} async-done(((bf16[2048,704]{0,1:T(8,128)(2,1)}), bf16[256,704]{0,1:T(8,128)(2,1)}) %reduce-scatter.5.cloned.1.call-update) | async-done | bytes 360464 | tf_op jit(solution)/shard_map/reduce_scatter | solution.py:90
  163.6 1.8 reshape.121
  165.4 1.8 copy.9
  167.2 7.3 %all-to-all-start.3 = ((bf16[16,128,88]{1,2,0:T(8,128)(2,1)}), bf16[16,128,88]{1,2,0:T(8,128)(2,1)}, u32[]{:S(2)}, u32[]{:S(2)}) async-start(bf16[16,128,88]{1,2,0:T(8,128)(2,1)} %bitcast.47), calls=%async_computation.5 | async-start | bytes 720896 | tf_op jit(solution)/shard_map/all_to_all | solution.py:94
  174.5 1.1 bitcast_reduce_fusion
  175.5 1.6 fusion.3
  177.1 4.9 %all-to-all-done.3 = bf16[16,128,88]{1,2,0:T(8,128)(2,1)} async-done(((bf16[16,128,88]{1,2,0:T(8,128)(2,1)}), bf16[16,128,88]{1,2,0:T(8,128)(2,1)}, u32[]{:S(2)}, u32[]{:S(2)}) %all-to-all-start.3) | async-done | bytes 360480 | tf_op jit(solution)/shard_map/all_to_all | solution.py:94
  182.0 1.1 bitcast_reduce_fusion.1
  183.8 0.9 fusion.31
  (36 shorter events, 2.4 us)
Async XLA Ops:
  6.5 56.0 %copy-start = (bf16[1,352,2048]{2,1,0:T(8,128)(2,1)S(1)}, bf16[1,352,2048]{2,1,0:T(8,128)(2,1)}, u32[]{:S(2)}) copy-start(bf16[1,352,2048]{2,1,0:T(8,128)(2,1)} %param.13) | copy-start | bytes 4325380
  6.5 3.3 %copy-start.1 = (bf16[512,2048]{1,0:T(8,128)(2,1)S(1)}, bf16[512,2048]{1,0:T(8,128)(2,1)}, u32[]{:S(2)}) copy-start(bf16[512,2048]{1,0:T(8,128)(2,1)} %param.7) | copy-start | bytes 6291460
  6.5 3.3 %copy-start.10 = (f32[2048]{0:T(1024)S(1)}, f32[2048]{0:T(1024)}, u32[]{:S(2)}) copy-start(f32[2048]{0:T(1024)} %param.8) | copy-start | bytes 24580
  6.5 109.4 %reduce-scatter.3.cloned.1.call-start = ((), (), s32[]{:S(2)}) async-start(), calls=%async_computation.6 | async-start | bytes 3833856 | tf_op jit(solution)/shard_map/reduce_scatter | solution.py:90
  6.5 3.3 %copy-start.9 = (bf16[2048,8]{0,1:T(8,128)(2,1)S(1)}, bf16[2048,8]{0,1:T(8,128)(2,1)}, u32[]{:S(2)}) copy-start(bf16[2048,8]{0,1:T(8,128)(2,1)} %param.9) | copy-start | bytes 98308
  9.6 1.6 copy-start.11
  9.6 3.8 %copy-start.4 = (f32[512]{0:T(512)}, f32[512]{0:T(512)S(1)}, u32[]{:S(2)}) copy-start(f32[512]{0:T(512)S(1)} %add_rsqrt_fusion) | copy-start | bytes 6148
  13.4 46.0 %copy-start.5 = (bf16[1,2048,352]{1,2,0:T(8,128)(2,1)S(1)}, bf16[1,2048,352]{1,2,0:T(8,128)(2,1)}, u32[]{:S(2)}) copy-start(bf16[1,2048,352]{1,2,0:T(8,128)(2,1)} %param.12) | copy-start | bytes 4325380
  13.4 46.0 %copy-start.7 = (bf16[1,2048,352]{1,2,0:T(8,128)(2,1)S(1)}, bf16[1,2048,352]{1,2,0:T(8,128)(2,1)}, u32[]{:S(2)}) copy-start(bf16[1,2048,352]{1,2,0:T(8,128)(2,1)} %param.11) | copy-start | bytes 4325380
  66.4 97.2 %reduce-scatter.5.cloned.1.call-start = ((), (), s32[]{:S(2)}) async-start(), calls=%async_computation.7 | async-start | bytes 3244032 | tf_op jit(solution)/shard_map/reduce_scatter | solution.py:90
  69.0 37.6 %copy-start.6 = (bf16[1,2048,352]{1,2,0:T(8,128)(2,1)S(1)}, bf16[1,2048,352]{1,2,0:T(8,128)(2,1)}, u32[]{:S(2)}) copy-start(bf16[1,2048,352]{1,2,0:T(8,128)(2,1)} %param.12) | copy-start | bytes 4325380
  69.0 37.6 %copy-start.8 = (bf16[1,2048,352]{1,2,0:T(8,128)(2,1)S(1)}, bf16[1,2048,352]{1,2,0:T(8,128)(2,1)}, u32[]{:S(2)}) copy-start(bf16[1,2048,352]{1,2,0:T(8,128)(2,1)} %param.11) | copy-start | bytes 4325380
  119.6 47.5 %all-to-all-start.1 = ((bf16[16,128,104]{1,2,0:T(8,128)(2,1)}), bf16[16,128,104]{1,2,0:T(8,128)(2,1)}, u32[]{:S(2)}, u32[]{:S(2)}) async-start(bf16[16,128,104]{1,2,0:T(8,128)(2,1)} %bitcast.46), calls=%async_computation.2 | async-start | bytes 851968 | tf_op jit(solution)/shard_map/all_to_all | solution.py:94
  165.4 17.7 %copy-start.3 = (s32[1024]{0:T(1024)S(1)}, s32[1024]{0:T(1024)}, u32[]{:S(2)}) copy-start(s32[1024]{0:T(1024)} %pad_add_fusion.1) | copy-start | bytes 12292
  167.2 14.8 %all-to-all-start.3 = ((bf16[16,128,88]{1,2,0:T(8,128)(2,1)}), bf16[16,128,88]{1,2,0:T(8,128)(2,1)}, u32[]{:S(2)}, u32[]{:S(2)}) async-start(bf16[16,128,88]{1,2,0:T(8,128)(2,1)} %bitcast.47), calls=%async_computation.5 | async-start | bytes 720896 | tf_op jit(solution)/shard_map/all_to_all | solution.py:94
  182.0 1.8 copy-start.2
Sparse Core Ops, SparseCore 0:
  66.5 49.4 reduce-scatter.2
  118.5 44.9 reduce-scatter.4

commit v11 on v9

--- a/solution.py
+++ b/solution.py
@@ -49,11 +49,15 @@
         slice_width = model_width // mp_count
         rows_total = experts * capacity
         wide_in = hidden_in.astype(jnp.float32)
-        normed = (
-            wide_in
-            * lax.rsqrt(jnp.mean(wide_in * wide_in, axis=1, keepdims=True) + eps_norm)
-            * norm_gain
-        ).astype(jnp.bfloat16)
+        squares = wide_in * wide_in
+        high = squares.astype(jnp.bfloat16)
+        low = (squares - high.astype(jnp.float32)).astype(jnp.bfloat16)
+        ones = jnp.ones((model_width, 128), jnp.bfloat16)
+        row_sums = jnp.dot(high, ones, preferred_element_type=jnp.float32) + jnp.dot(
+            low, ones, preferred_element_type=jnp.float32
+        )
+        mean_sq = row_sums[:, :1] / model_width
+        normed = (wide_in * lax.rsqrt(mean_sq + eps_norm) * norm_gain).astype(jnp.bfloat16)
         slot0, slot1, oh0, oh1 = pair_slots(choices, experts)
         chunk = capacity // n_chunks
         e0, e1 = choices[:, 0], choices[:, 1]

time: 189 us -> 187 us (0.989)
  waiting for transfers between devices: 42.1 us -> 46.7 us
  other arithmetic: 6.5 us -> 1.96 us
  local copies, waits for them, and re-layouts: 8.17 us -> 3.85 us
  matrix products: 20.5 us -> 23 us
    reshape x4, local copies, waits for them, and re-layouts: 7.25 us -> 3.78 us  [per_device(): summed.reshape(halves, slice_width, experts, chunk).transpose(2, 0, 1, 3)]
    dot_general x0 -> x2, matrix products: none -> 3.31 us  [the longest x1 2.56 us: per_device(): jnp.dot(high, ones, preferred_element_type=jnp.float32)]
    reduce_scatter x2, waiting for transfers between devices: 37 us -> 39.9 us  [per_device(): lax.psum_scatter(partial_t, mp_axes[0], scatter_dimension=0, tiled=True)]
    reduce_sum x1 -> x0, other arithmetic: 2.15 us -> none  [per_device(): jnp.mean(wide_in * wide_in, axis=1, keepdims=True) + eps_norm]
    reduce_sum x2, other arithmetic: 2.15 us -> 0.11 us  [per_device(): got.reshape(experts, halves, slice_width, chunk).astype(jnp.float32)]
  transfers between devices with their start and end apart: 4 -> 4, of which waited for: 2 -> 2; matrix products, arithmetic and copies ran while one was open for 11% -> 7% of each run, Pallas kernels for 0% -> 0%
where the time goes in v11:
time: 187 us
  blocking collectives  83.5 us (45%)
  waiting for transfers between devices  46.7 us (25%)
  matrix products  23 us (12%)
  starting transfers between devices  13.8 us (7%)
  between operations  13.7 us (7%)
  local copies, waits for them, and re-layouts  3.85 us (2%)
  other arithmetic  1.96 us (1%)
    all_to_all x2, blocking collectives, per_device(): lax.all_to_all(part, expert_axes, split_axis=0, concat_axis=0, tiled=True)  83.5 us
    reduce_scatter x2, waiting for transfers between devices, per_device(): lax.psum_scatter(partial_t, mp_axes[0], scatter_dimension=0, tiled=True)  39.9 us
    all_to_all x2, starting transfers between devices, per_device(): lax.all_to_all(blocks, expert_axes + mp_axes[1:], split_axis=0, concat_ax...  13.8 us
    dot_general x2, matrix products, per_device(): lax.dot_general(w_down[0], hidden, (((0,), (1,)), ((), ())), preferred_el...  7.13 us
    all_to_all x2, waiting for transfers between devices, per_device(): lax.all_to_all(blocks, expert_axes + mp_axes[1:], split_axis=0, concat_ax...  6.78 us
    dot_general x2, matrix products, per_device(): both = jnp.dot(expert_rows, gate_up, preferred_element_type=jnp.float32)  4.88 us
    dot_general x2, matrix products, per_device(): jnp.dot(dispatch, normed, preferred_element_type=jnp.float32)  4.77 us
    reshape x4, local copies, waits for them, and re-layouts, per_device(): summed.reshape(halves, slice_width, experts, chunk).transpose(2, 0, 1, 3)  3.78 us
  transfers between devices with their start and end apart: 4, of which 2 were waited for; matrix products, arithmetic and copies ran while one was open for 7% of the time, Pallas kernels for 0%

profile of v11, /device:TPU:2, one launch (start us, length us, event | category | flops | bytes accessed | tf_op | source)
XLA Modules:
  0.0 186.6 jit_solution(17399999637092132147)
XLA Ops:
  6.5 2.6 %fusion.14 = f32[512,128]{0,1:T(8,128)S(1)} fusion(bf16[512,2048]{1,0:T(8,128)(2,1)} %param.7), kind=kOutput, calls=%fused_computation.21 | convolution fusion | flops 271581184 | bytes 2359296 | tf_op jit(solution)/shard_map/dot_general | solution.py:56
  9.2 0.7 fusion.9
  9.9 0.2 fusion.26
  10.2 1.3 select_reduce_fusion
  11.6 2.0 %convolution_convert_fusion.3 = bf16[768,2048]{1,0:T(8,128)(2,1)S(1)} fusion(s32[512]{0:T(512)S(1)} %get-tuple-element.15, s32[512]{0:T(512)S(1)} %get-tuple-element.20, bf16[512,2048]{1,0:T(8,128)(2,1)S(1)} %copy-done.1, f32[2048]{0:T(1024)S(1)} %copy-done.11, f32[512]{0:T(512)S(1)} %bitcast.56), kind=kOutput, calls=%fused_computation.10 | convolution fusion | flops 1617559552 | bytes 5257216 | tf_op jit(solution)/shard_map/dot_general | solution.py:77
  13.7 43.1 %all_to_all.20 = bf16[8,96,2048]{2,1,0:T(8,128)(2,1)S(1)} all-to-all(bf16[8,96,2048]{2,1,0:T(8,128)(2,1)S(1)} %bitcast.46), channel_id=1, replica_groups=mesh['dp'=2,'ey'=4,'ex'=2,'mz'=8,'mx'=2] {'ey','ex'}, dimensions={0} | all-to-all | bytes 6291456 | tf_op jit(solution)/shard_map/all_to_all | solution.py:79
  56.8 2.4 %fusion.12 = f32[768,704]{0,1:T(8,128)S(1)} fusion(bf16[768,2048]{1,0:T(8,128)(2,1)S(1)} %bitcast.43, bf16[2048,352]{0,1:T(8,128)(2,1)S(1)} %bitcast.58, bf16[2048,352]{0,1:T(8,128)(2,1)S(1)} %bitcast.60), kind=kOutput, calls=%fused_computation.20 | convolution fusion | flops 2220359680 | bytes 8192000 | tf_op jit(solution)/shard_map/dot_general | solution.py:81
  59.2 3.6 %fusion.7 = bf16[2048,768]{0,1:T(8,128)(2,1)} fusion(bf16[1,352,2048]{2,1,0:T(8,128)(2,1)S(1)} %copy-done, f32[768,704]{0,1:T(8,128)S(1)} %fusion.12), kind=kOutput, calls=%fused_computation.15 | convolution fusion | flops 1110491136 | bytes 6750208 | tf_op jit(solution)/shard_map/dot_general | solution.py:84
  62.9 2.7 %convolution_convert_fusion.1 = bf16[768,2048]{1,0:T(8,128)(2,1)S(1)} fusion(s32[512]{0:T(512)S(1)} %get-tuple-element.16, s32[512]{0:T(512)S(1)} %get-tuple-element.19, bf16[512,2048]{1,0:T(8,128)(2,1)S(1)} %copy-done.1, f32[2048]{0:T(1024)} %param.8, f32[512]{0:T(512)} %bitcast.57), kind=kOutput, calls=%fused_computation.8 | convolution fusion | flops 1617559552 | bytes 5257216 | tf_op jit(solution)/shard_map/dot_general | solution.py:77
  65.6 40.4 %all_to_all.21 = bf16[8,96,2048]{2,1,0:T(8,128)(2,1)S(1)} all-to-all(bf16[8,96,2048]{2,1,0:T(8,128)(2,1)S(1)} %bitcast.44), channel_id=1, replica_groups=mesh['dp'=2,'ey'=4,'ex'=2,'mz'=8,'mx'=2] {'ey','ex'}, dimensions={0} | all-to-all | bytes 6291456 | tf_op jit(solution)/shard_map/all_to_all | solution.py:79
  106.1 2.5 %fusion.11 = f32[768,704]{0,1:T(8,128)S(1)} fusion(bf16[768,2048]{1,0:T(8,128)(2,1)S(1)} %bitcast.45, bf16[2048,352]{0,1:T(8,128)(2,1)S(1)} %bitcast.59, bf16[2048,352]{0,1:T(8,128)(2,1)S(1)} %bitcast.61), kind=kOutput, calls=%fused_computation.19 | convolution fusion | flops 2220359680 | bytes 8192000 | tf_op jit(solution)/shard_map/dot_general | solution.py:81
  108.5 3.6 %fusion.8 = bf16[2048,768]{0,1:T(8,128)(2,1)} fusion(bf16[1,352,2048]{2,1,0:T(8,128)(2,1)S(1)} %copy-done, f32[768,704]{0,1:T(8,128)S(1)} %fusion.11), kind=kOutput, calls=%fused_computation.16 | convolution fusion | flops 1110491136 | bytes 6750208 | tf_op jit(solution)/shard_map/dot_general | solution.py:84
  112.1 1.1 reshape.115
  113.2 0.8 copy.8
  114.0 6.6 %all-to-all-start.1 = ((bf16[16,128,96]{1,2,0:T(8,128)(2,1)}), bf16[16,128,96]{1,2,0:T(8,128)(2,1)S(1)}, u32[]{:S(2)}, u32[]{:S(2)}) async-start(bf16[16,128,96]{1,2,0:T(8,128)(2,1)} %bitcast.10), calls=%async_computation.2 | async-start | bytes 786432 | tf_op jit(solution)/shard_map/all_to_all | solution.py:91
  120.7 39.9 %reduce-scatter.5.cloned.1.call-done = bf16[256,768]{0,1:T(8,128)(2,1)} async-done(((bf16[2048,768]{0,1:T(8,128)(2,1)}), bf16[256,768]{0,1:T(8,128)(2,1)}) %reduce-scatter.5.cloned.1.call-update) | async-done | bytes 393232 | tf_op jit(solution)/shard_map/reduce_scatter | solution.py:87
  160.6 1.1 reshape.121
  161.7 0.8 copy.9
  162.5 7.2 %all-to-all-start.3 = ((bf16[16,128,96]{1,2,0:T(8,128)(2,1)}), bf16[16,128,96]{1,2,0:T(8,128)(2,1)S(1)}, u32[]{:S(2)}, u32[]{:S(2)}) async-start(bf16[16,128,96]{1,2,0:T(8,128)(2,1)} %bitcast.18), calls=%async_computation.5 | async-start | bytes 786432 | tf_op jit(solution)/shard_map/all_to_all | solution.py:91
  169.7 0.1 bitcast_reduce_fusion.1
  169.8 0.7 fusion.5
  170.5 6.8 %all-to-all-done.3 = bf16[16,128,96]{1,2,0:T(8,128)(2,1)S(1)} async-done(((bf16[16,128,96]{1,2,0:T(8,128)(2,1)}), bf16[16,128,96]{1,2,0:T(8,128)(2,1)S(1)}, u32[]{:S(2)}, u32[]{:S(2)}) %all-to-all-start.3) | async-done | bytes 393248 | tf_op jit(solution)/shard_map/all_to_all | solution.py:91
  177.3 0.7 fusion.6
  178.0 1.8 fusion.38
  (37 shorter events, 0.3 us)
Async XLA Ops:
  6.5 52.7 %copy-start = (bf16[1,352,2048]{2,1,0:T(8,128)(2,1)S(1)}, bf16[1,352,2048]{2,1,0:T(8,128)(2,1)}, u32[]{:S(2)}) copy-start(bf16[1,352,2048]{2,1,0:T(8,128)(2,1)} %param.13) | copy-start | bytes 4325380
  6.5 2.6 %copy-start.1 = (bf16[512,2048]{1,0:T(8,128)(2,1)S(1)}, bf16[512,2048]{1,0:T(8,128)(2,1)}, u32[]{:S(2)}) copy-start(bf16[512,2048]{1,0:T(8,128)(2,1)} %param.7) | copy-start | bytes 6291460
  6.5 105.6 %reduce-scatter.3.cloned.1.call-start = ((), (), s32[]{:S(2)}) async-start(), calls=%async_computation.6 | async-start | bytes 3538944 | tf_op jit(solution)/shard_map/reduce_scatter | solution.py:87
  9.1 0.8 copy-start.2
  9.1 1.1 copy-start.10
  9.1 1.1 copy-start.11
  10.2 3.4 %copy-start.3 = (f32[512,1]{0,1:T(1,128)}, f32[512,1]{0,1:T(1,128)S(1)}, u32[]{:S(2)}) copy-start(f32[512,1]{0,1:T(1,128)S(1)} %add_rsqrt_fusion) | copy-start | bytes 6148
  13.6 43.1 %copy-start.6 = (bf16[1,2048,352]{1,2,0:T(8,128)(2,1)S(1)}, bf16[1,2048,352]{1,2,0:T(8,128)(2,1)}, u32[]{:S(2)}) copy-start(bf16[1,2048,352]{1,2,0:T(8,128)(2,1)} %param.12) | copy-start | bytes 4325380
  13.7 43.1 %copy-start.8 = (bf16[1,2048,352]{1,2,0:T(8,128)(2,1)S(1)}, bf16[1,2048,352]{1,2,0:T(8,128)(2,1)}, u32[]{:S(2)}) copy-start(bf16[1,2048,352]{1,2,0:T(8,128)(2,1)} %param.11) | copy-start | bytes 4325380
  62.8 97.8 %reduce-scatter.5.cloned.1.call-start = ((), (), s32[]{:S(2)}) async-start(), calls=%async_computation.7 | async-start | bytes 3538944 | tf_op jit(solution)/shard_map/reduce_scatter | solution.py:87
  65.6 40.4 %copy-start.7 = (bf16[1,2048,352]{1,2,0:T(8,128)(2,1)S(1)}, bf16[1,2048,352]{1,2,0:T(8,128)(2,1)}, u32[]{:S(2)}) copy-start(bf16[1,2048,352]{1,2,0:T(8,128)(2,1)} %param.12) | copy-start | bytes 4325380
  65.6 40.4 %copy-start.9 = (bf16[1,2048,352]{1,2,0:T(8,128)(2,1)S(1)}, bf16[1,2048,352]{1,2,0:T(8,128)(2,1)}, u32[]{:S(2)}) copy-start(bf16[1,2048,352]{1,2,0:T(8,128)(2,1)} %param.11) | copy-start | bytes 4325380
  112.1 8.6 %copy-start.4 = (f32[512]{0:T(512)S(1)}, f32[512]{0:T(512)}, u32[]{:S(2)}) copy-start(f32[512]{0:T(512)} %get-tuple-element.7) | copy-start | bytes 6148
  112.1 8.6 %copy-start.5 = (f32[512]{0:T(512)S(1)}, f32[512]{0:T(512)}, u32[]{:S(2)}) copy-start(f32[512]{0:T(512)} %get-tuple-element.8) | copy-start | bytes 6148
  114.0 48.5 %all-to-all-start.1 = ((bf16[16,128,96]{1,2,0:T(8,128)(2,1)}), bf16[16,128,96]{1,2,0:T(8,128)(2,1)S(1)}, u32[]{:S(2)}, u32[]{:S(2)}) async-start(bf16[16,128,96]{1,2,0:T(8,128)(2,1)} %bitcast.10), calls=%async_computation.2 | async-start | bytes 786432 | tf_op jit(solution)/shard_map/all_to_all | solution.py:91
  162.5 14.7 %all-to-all-start.3 = ((bf16[16,128,96]{1,2,0:T(8,128)(2,1)}), bf16[16,128,96]{1,2,0:T(8,128)(2,1)S(1)}, u32[]{:S(2)}, u32[]{:S(2)}) async-start(bf16[16,128,96]{1,2,0:T(8,128)(2,1)} %bitcast.18), calls=%async_computation.5 | async-start | bytes 786432 | tf_op jit(solution)/shard_map/all_to_all | solution.py:91
Sparse Core Ops, SparseCore 0:
  63.0 48.5 reduce-scatter.2
  114.1 46.4 reduce-scatter.4

commit v12 on v11

--- a/solution.py
+++ b/solution.py
@@ -80,7 +80,7 @@
             expert_rows = arrived.reshape(experts * chunk, model_width)
             both = jnp.dot(expert_rows, gate_up, preferred_element_type=jnp.float32)
             gate_proj, up_proj = both[:, :ff_share], both[:, ff_share:]
-            hidden = (jax.nn.silu(gate_proj) * up_proj).astype(jnp.bfloat16)
+            hidden = lax.optimization_barrier((jax.nn.silu(gate_proj) * up_proj).astype(jnp.bfloat16))
             partial_t = lax.dot_general(
                 w_down[0], hidden, (((0,), (1,)), ((), ())), preferred_element_type=jnp.float32
             ).astype(jnp.bfloat16)

time: 187 us -> 188 us (level)
  no operation moved by 1% of the time
where the time goes in v12:
time: 188 us; the launch traced here: 187 us
  blocking collectives  83.5 us (44%)
  waiting for transfers between devices  47 us (25%)
  matrix products  22.9 us (12%)
  between operations  13.7 us (7%)
  starting transfers between devices  13.4 us (7%)
  local copies, waits for them, and re-layouts  3.85 us (2%)
  other arithmetic  2.6 us (1%)
    all_to_all x2, blocking collectives, per_device(): lax.all_to_all(part, expert_axes, split_axis=0, concat_axis=0, tiled=True)  83.5 us
    reduce_scatter x2, waiting for transfers between devices, per_device(): lax.psum_scatter(partial_t, mp_axes[0], scatter_dimension=0, tiled=True)  40.2 us
    all_to_all x2, starting transfers between devices, per_device(): lax.all_to_all(blocks, expert_axes + mp_axes[1:], split_axis=0, concat_ax...  13.4 us
    dot_general x2, matrix products, per_device(): lax.dot_general(w_down[0], hidden, (((0,), (1,)), ((), ())), preferred_el...  7.02 us
    all_to_all x2, waiting for transfers between devices, per_device(): lax.all_to_all(blocks, expert_axes + mp_axes[1:], split_axis=0, concat_ax...  6.78 us
    dot_general x2, matrix products, per_device(): both = jnp.dot(expert_rows, gate_up, preferred_element_type=jnp.float32)  4.88 us
    dot_general x2, matrix products, per_device(): jnp.dot(dispatch, normed, preferred_element_type=jnp.float32)  4.77 us
    reshape x4, local copies, waits for them, and re-layouts, per_device(): summed.reshape(halves, slice_width, experts, chunk).transpose(2, 0, 1, 3)  3.78 us
  transfers between devices with their start and end apart: 4, of which 2 were waited for; matrix products, arithmetic and copies ran while one was open for 7% of the time, Pallas kernels for 0%

profile of v12, /device:TPU:2, one launch (start us, length us, event | category | flops | bytes accessed | tf_op | source)
XLA Modules:
  0.0 187.0 jit_solution(4877969260571066364)
XLA Ops:
  6.5 2.6 %fusion.14 = f32[512,128]{0,1:T(8,128)S(1)} fusion(bf16[512,2048]{1,0:T(8,128)(2,1)} %param.7), kind=kOutput, calls=%fused_computation.21 | convolution fusion | flops 271581184 | bytes 2359296 | tf_op jit(solution)/shard_map/dot_general | solution.py:56
  9.2 0.7 fusion.9
  10.2 1.3 select_reduce_fusion
  11.6 2.0 %convolution_convert_fusion.3 = bf16[768,2048]{1,0:T(8,128)(2,1)S(1)} fusion(s32[512]{0:T(512)S(1)} %get-tuple-element.15, s32[512]{0:T(512)S(1)} %get-tuple-element.20, bf16[512,2048]{1,0:T(8,128)(2,1)S(1)} %copy-done.1, f32[2048]{0:T(1024)S(1)} %copy-done.11, f32[512]{0:T(512)S(1)} %bitcast.58), kind=kOutput, calls=%fused_computation.10 | convolution fusion | flops 1617559552 | bytes 5257216 | tf_op jit(solution)/shard_map/dot_general | solution.py:77
  13.7 43.1 %all_to_all.20 = bf16[8,96,2048]{2,1,0:T(8,128)(2,1)S(1)} all-to-all(bf16[8,96,2048]{2,1,0:T(8,128)(2,1)S(1)} %bitcast.48), channel_id=1, replica_groups=mesh['dp'=2,'ey'=4,'ex'=2,'mz'=8,'mx'=2] {'ey','ex'}, dimensions={0} | all-to-all | bytes 6291456 | tf_op jit(solution)/shard_map/all_to_all | solution.py:79
  56.8 2.4 %fusion.12 = f32[768,704]{0,1:T(8,128)S(1)} fusion(bf16[768,2048]{1,0:T(8,128)(2,1)S(1)} %bitcast.45, bf16[2048,352]{0,1:T(8,128)(2,1)S(1)} %bitcast.60, bf16[2048,352]{0,1:T(8,128)(2,1)S(1)} %bitcast.62), kind=kOutput, calls=%fused_computation.20 | convolution fusion | flops 2220359680 | bytes 8192000 | tf_op jit(solution)/shard_map/dot_general | solution.py:81
  59.2 0.3 fusion.25
  59.6 3.5 %fusion.7 = bf16[2048,768]{0,1:T(8,128)(2,1)} fusion(bf16[768,352]{0,1:T(8,128)(2,1)S(1)} %fusion.25, bf16[1,352,2048]{2,1,0:T(8,128)(2,1)S(1)} %copy-done), kind=kOutput, calls=%fused_computation.15 | convolution fusion | flops 1108869120 | bytes 5128192 | tf_op jit(solution)/shard_map/dot_general | solution.py:84
  63.2 2.7 %convolution_convert_fusion.1 = bf16[768,2048]{1,0:T(8,128)(2,1)S(1)} fusion(s32[512]{0:T(512)S(1)} %get-tuple-element.16, s32[512]{0:T(512)S(1)} %get-tuple-element.19, bf16[512,2048]{1,0:T(8,128)(2,1)S(1)} %copy-done.1, f32[2048]{0:T(1024)} %param.8, f32[512]{0:T(512)} %bitcast.59), kind=kOutput, calls=%fused_computation.8 | convolution fusion | flops 1617559552 | bytes 5257216 | tf_op jit(solution)/shard_map/dot_general | solution.py:77
  65.9 40.4 %all_to_all.21 = bf16[8,96,2048]{2,1,0:T(8,128)(2,1)S(1)} all-to-all(bf16[8,96,2048]{2,1,0:T(8,128)(2,1)S(1)} %bitcast.46), channel_id=1, replica_groups=mesh['dp'=2,'ey'=4,'ex'=2,'mz'=8,'mx'=2] {'ey','ex'}, dimensions={0} | all-to-all | bytes 6291456 | tf_op jit(solution)/shard_map/all_to_all | solution.py:79
  106.3 2.5 %fusion.11 = f32[768,704]{0,1:T(8,128)S(1)} fusion(bf16[768,2048]{1,0:T(8,128)(2,1)S(1)} %bitcast.47, bf16[2048,352]{0,1:T(8,128)(2,1)S(1)} %bitcast.61, bf16[2048,352]{0,1:T(8,128)(2,1)S(1)} %bitcast.63), kind=kOutput, calls=%fused_computation.19 | convolution fusion | flops 2220359680 | bytes 8192000 | tf_op jit(solution)/shard_map/dot_general | solution.py:81
  108.8 0.3 fusion.24
  109.1 3.5 %fusion.8 = bf16[2048,768]{0,1:T(8,128)(2,1)} fusion(bf16[768,352]{0,1:T(8,128)(2,1)S(1)} %fusion.24, bf16[1,352,2048]{2,1,0:T(8,128)(2,1)S(1)} %copy-done), kind=kOutput, calls=%fused_computation.16 | convolution fusion | flops 1108869120 | bytes 5128192 | tf_op jit(solution)/shard_map/dot_general | solution.py:84
  112.7 1.1 reshape.115
  113.8 0.8 copy.8
  114.6 6.2 %all-to-all-start.1 = ((bf16[16,128,96]{1,2,0:T(8,128)(2,1)}), bf16[16,128,96]{1,2,0:T(8,128)(2,1)S(1)}, u32[]{:S(2)}, u32[]{:S(2)}) async-start(bf16[16,128,96]{1,2,0:T(8,128)(2,1)} %bitcast.10), calls=%async_computation.2 | async-start | bytes 786432 | tf_op jit(solution)/shard_map/all_to_all | solution.py:91
  120.9 40.2 %reduce-scatter.5.cloned.1.call-done = bf16[256,768]{0,1:T(8,128)(2,1)} async-done(((bf16[2048,768]{0,1:T(8,128)(2,1)}), bf16[256,768]{0,1:T(8,128)(2,1)}) %reduce-scatter.5.cloned.1.call-update) | async-done | bytes 393232 | tf_op jit(solution)/shard_map/reduce_scatter | solution.py:87
  161.0 1.1 reshape.121
  162.1 0.8 copy.9
  163.0 7.1 %all-to-all-start.3 = ((bf16[16,128,96]{1,2,0:T(8,128)(2,1)}), bf16[16,128,96]{1,2,0:T(8,128)(2,1)S(1)}, u32[]{:S(2)}, u32[]{:S(2)}) async-start(bf16[16,128,96]{1,2,0:T(8,128)(2,1)} %bitcast.18), calls=%async_computation.5 | async-start | bytes 786432 | tf_op jit(solution)/shard_map/all_to_all | solution.py:91
  170.2 0.7 fusion.5
  170.9 6.8 %all-to-all-done.3 = bf16[16,128,96]{1,2,0:T(8,128)(2,1)S(1)} async-done(((bf16[16,128,96]{1,2,0:T(8,128)(2,1)}), bf16[16,128,96]{1,2,0:T(8,128)(2,1)S(1)}, u32[]{:S(2)}, u32[]{:S(2)}) %all-to-all-start.3) | async-done | bytes 393248 | tf_op jit(solution)/shard_map/all_to_all | solution.py:91
  177.7 0.7 fusion.6
  178.4 1.8 fusion.34
  (39 shorter events, 0.6 us)
Async XLA Ops:
  6.5 53.0 %copy-start = (bf16[1,352,2048]{2,1,0:T(8,128)(2,1)S(1)}, bf16[1,352,2048]{2,1,0:T(8,128)(2,1)}, u32[]{:S(2)}) copy-start(bf16[1,352,2048]{2,1,0:T(8,128)(2,1)} %param.13) | copy-start | bytes 4325380
  6.5 2.6 %copy-start.1 = (bf16[512,2048]{1,0:T(8,128)(2,1)S(1)}, bf16[512,2048]{1,0:T(8,128)(2,1)}, u32[]{:S(2)}) copy-start(bf16[512,2048]{1,0:T(8,128)(2,1)} %param.7) | copy-start | bytes 6291460
  6.5 106.1 %reduce-scatter.3.cloned.1.call-start = ((), (), s32[]{:S(2)}) async-start(), calls=%async_computation.6 | async-start | bytes 3538944 | tf_op jit(solution)/shard_map/reduce_scatter | solution.py:87
  9.1 0.8 copy-start.2
  9.1 1.1 copy-start.10
  9.1 1.1 copy-start.11
  10.2 3.4 %copy-start.3 = (f32[512,1]{0,1:T(1,128)}, f32[512,1]{0,1:T(1,128)S(1)}, u32[]{:S(2)}) copy-start(f32[512,1]{0,1:T(1,128)S(1)} %add_rsqrt_fusion) | copy-start | bytes 6148
  13.6 43.1 %copy-start.6 = (bf16[1,2048,352]{1,2,0:T(8,128)(2,1)S(1)}, bf16[1,2048,352]{1,2,0:T(8,128)(2,1)}, u32[]{:S(2)}) copy-start(bf16[1,2048,352]{1,2,0:T(8,128)(2,1)} %param.12) | copy-start | bytes 4325380
  13.7 43.1 %copy-start.8 = (bf16[1,2048,352]{1,2,0:T(8,128)(2,1)S(1)}, bf16[1,2048,352]{1,2,0:T(8,128)(2,1)}, u32[]{:S(2)}) copy-start(bf16[1,2048,352]{1,2,0:T(8,128)(2,1)} %param.11) | copy-start | bytes 4325380
  63.1 97.9 %reduce-scatter.5.cloned.1.call-start = ((), (), s32[]{:S(2)}) async-start(), calls=%async_computation.7 | async-start | bytes 3538944 | tf_op jit(solution)/shard_map/reduce_scatter | solution.py:87
  65.9 40.4 %copy-start.7 = (bf16[1,2048,352]{1,2,0:T(8,128)(2,1)S(1)}, bf16[1,2048,352]{1,2,0:T(8,128)(2,1)}, u32[]{:S(2)}) copy-start(bf16[1,2048,352]{1,2,0:T(8,128)(2,1)} %param.12) | copy-start | bytes 4325380
  65.9 40.4 %copy-start.9 = (bf16[1,2048,352]{1,2,0:T(8,128)(2,1)S(1)}, bf16[1,2048,352]{1,2,0:T(8,128)(2,1)}, u32[]{:S(2)}) copy-start(bf16[1,2048,352]{1,2,0:T(8,128)(2,1)} %param.11) | copy-start | bytes 4325380
  112.6 8.2 %copy-start.4 = (f32[512]{0:T(512)S(1)}, f32[512]{0:T(512)}, u32[]{:S(2)}) copy-start(f32[512]{0:T(512)} %get-tuple-element.7) | copy-start | bytes 6148
  112.6 8.2 %copy-start.5 = (f32[512]{0:T(512)S(1)}, f32[512]{0:T(512)}, u32[]{:S(2)}) copy-start(f32[512]{0:T(512)} %get-tuple-element.8) | copy-start | bytes 6148
  114.6 48.4 %all-to-all-start.1 = ((bf16[16,128,96]{1,2,0:T(8,128)(2,1)}), bf16[16,128,96]{1,2,0:T(8,128)(2,1)S(1)}, u32[]{:S(2)}, u32[]{:S(2)}) async-start(bf16[16,128,96]{1,2,0:T(8,128)(2,1)} %bitcast.10), calls=%async_computation.2 | async-start | bytes 786432 | tf_op jit(solution)/shard_map/all_to_all | solution.py:91
  163.0 14.7 %all-to-all-start.3 = ((bf16[16,128,96]{1,2,0:T(8,128)(2,1)}), bf16[16,128,96]{1,2,0:T(8,128)(2,1)S(1)}, u32[]{:S(2)}, u32[]{:S(2)}) async-start(bf16[16,128,96]{1,2,0:T(8,128)(2,1)} %bitcast.18), calls=%async_computation.5 | async-start | bytes 786432 | tf_op jit(solution)/shard_map/all_to_all | solution.py:91
Sparse Core Ops, SparseCore 0:
  63.2 48.5 reduce-scatter.2
  114.3 46.6 reduce-scatter.4

commit v13 on v9

--- a/solution.py
+++ b/solution.py
@@ -30,6 +30,19 @@
     return first_weight, 1.0 - first_weight
 
 
+def rms_norm(wide_in, norm_gain):
+    model_width = wide_in.shape[1]
+    squares = wide_in * wide_in
+    high = squares.astype(jnp.bfloat16)
+    low = (squares - high.astype(jnp.float32)).astype(jnp.bfloat16)
+    ones = jnp.ones((model_width, 128), jnp.bfloat16)
+    row_sums = jnp.dot(high, ones, preferred_element_type=jnp.float32) + jnp.dot(
+        low, ones, preferred_element_type=jnp.float32
+    )
+    mean_sq = row_sums[:, :1] / model_width
+    return (wide_in * lax.rsqrt(mean_sq + eps_norm) * norm_gain).astype(jnp.bfloat16)
+
+
 def pair_exchange(summed, axis):
     n = lax.axis_size(axis)
     if n == 1:
@@ -49,11 +62,7 @@
         slice_width = model_width // mp_count
         rows_total = experts * capacity
         wide_in = hidden_in.astype(jnp.float32)
-        normed = (
-            wide_in
-            * lax.rsqrt(jnp.mean(wide_in * wide_in, axis=1, keepdims=True) + eps_norm)
-            * norm_gain
-        ).astype(jnp.bfloat16)
+        normed = rms_norm(wide_in, norm_gain)
         slot0, slot1, oh0, oh1 = pair_slots(choices, experts)
         chunk = capacity // n_chunks
         e0, e1 = choices[:, 0], choices[:, 1]
@@ -80,6 +89,7 @@
             partial_t = lax.dot_general(
                 w_down[0], hidden, (((0,), (1,)), ((), ())), preferred_element_type=jnp.float32
             ).astype(jnp.bfloat16)
+            previous = partial_t
             summed = lax.psum_scatter(partial_t, mp_axes[0], scatter_dimension=0, tiled=True)
             halves = lax.axis_size(mp_axes[1])
             blocks = summed.reshape(halves, slice_width, experts, chunk).transpose(2, 0, 1, 3)
@@ -88,7 +98,9 @@
             got = got.reshape(experts, halves, slice_width, chunk).astype(jnp.float32).sum(axis=1)
             returned = got.astype(jnp.bfloat16).transpose(1, 0, 2).reshape(slice_width, experts * chunk)
             results.append((r0, r1, returned))
-        logits = jnp.dot(normed, router_w, preferred_element_type=jnp.float32)
+        late_in = lax.optimization_barrier((hidden_in, previous))[0]
+        late_normed = rms_norm(late_in.astype(jnp.float32), norm_gain)
+        logits = jnp.dot(late_normed, router_w, preferred_element_type=jnp.float32)
         w0, w1 = pair_weights(logits, oh0, oh1)
         dims = (((1,), (1,)), ((), ()))
         for r0, r1, returned in results:
@@ -96,8 +108,8 @@
             sel = (both_rows[:, None] == chunk_rows[None, :]).astype(jnp.bfloat16)
             out = lax.dot_general(sel, returned, dims, preferred_element_type=jnp.float32)
             term = out[:tokens_dev] * w0[:, None] + out[tokens_dev:] * w1[:, None]
-            mixture = term if mixture is None else mixture + term
-        return (residual + mixture).astype(jnp.bfloat16)
+            mixture = residual + term if mixture is None else mixture + term
+        return mixture.astype(jnp.bfloat16)
 
     return per_device
 

time: 189 us -> 186 us (0.984)
  matrix products: 20.5 us -> 25.8 us
  local copies, waits for them, and re-layouts: 8.17 us -> 3.87 us
  other arithmetic: 6.5 us -> 4.4 us
    dot_general x1 -> x5, matrix products: 1.34 us -> 7.23 us  [the longest x2 3.23 us: rms_norm(): jnp.dot(low, ones, preferred_element_type=jnp.float32)]
    reshape x4, local copies, waits for them, and re-layouts: 7.25 us -> 3.79 us  [per_device(): summed.reshape(halves, slice_width, experts, chunk).transpose(2, 0, 1, 3)]
    reduce_sum x1 -> x0, other arithmetic: 2.15 us -> none  [per_device(): jnp.mean(wide_in * wide_in, axis=1, keepdims=True) + eps_norm]
    reduce_scatter x2, waiting for transfers between devices: 37 us -> 34.9 us  [per_device(): lax.psum_scatter(partial_t, mp_axes[0], scatter_dimension=0, tiled=True)]
    reduce_sum x2, other arithmetic: 2.15 us -> 0.11 us  [per_device(): got.reshape(experts, halves, slice_width, chunk).astype(jnp.float32)]
  transfers between devices with their start and end apart: 4 -> 4, of which waited for: 2 -> 2; matrix products, arithmetic and copies ran while one was open for 11% -> 10% of each run, Pallas kernels for 0% -> 0%
where the time goes in v13:
time: 186 us
  blocking collectives  83.5 us (45%)
  waiting for transfers between devices  41.7 us (22%)
  matrix products  25.8 us (14%)
  between operations  13.7 us (7%)
  starting transfers between devices  13 us (7%)
  other arithmetic  4.4 us (2%)
  local copies, waits for them, and re-layouts  3.87 us (2%)
    all_to_all x2, blocking collectives, per_device(): lax.all_to_all(part, expert_axes, split_axis=0, concat_axis=0, tiled=True)  83.5 us
    reduce_scatter x2, waiting for transfers between devices, per_device(): lax.psum_scatter(partial_t, mp_axes[0], scatter_dimension=0, tiled=True)  34.9 us
    all_to_all x2, starting transfers between devices, per_device(): lax.all_to_all(blocks, expert_axes + mp_axes[1:], split_axis=0, concat_ax...  12.9 us
    dot_general x2, matrix products, per_device(): lax.dot_general(w_down[0], hidden, (((0,), (1,)), ((), ())), preferred_el...  7.13 us
    all_to_all x2, waiting for transfers between devices, per_device(): lax.all_to_all(blocks, expert_axes + mp_axes[1:], split_axis=0, concat_ax...  6.77 us
    dot_general x2, matrix products, per_device(): both = jnp.dot(expert_rows, gate_up, preferred_element_type=jnp.float32)  4.89 us
    dot_general x2, matrix products, per_device(): jnp.dot(dispatch, normed, preferred_element_type=jnp.float32)  4.85 us
    reshape x4, local copies, waits for them, and re-layouts, per_device(): summed.reshape(halves, slice_width, experts, chunk).transpose(2, 0, 1, 3)  3.79 us
  transfers between devices with their start and end apart: 4, of which 2 were waited for; matrix products, arithmetic and copies ran while one was open for 10% of the time, Pallas kernels for 0%

profile of v13, /device:TPU:2, one launch (start us, length us, event | category | flops | bytes accessed | tf_op | source)
XLA Modules:
  0.0 185.9 jit_solution(15917002367183888476)
XLA Ops:
  6.5 2.5 %fusion.16 = f32[512,128]{0,1:T(8,128)S(1)} fusion(bf16[512,2048]{1,0:T(8,128)(2,1)} %param.7), kind=kOutput, calls=%fused_computation.26 | convolution fusion | flops 274726912 | bytes 2359296 | tf_op jit(solution)/shard_map/dot_general | solution.py:39
  9.1 0.8 fusion.28
  10.8 2.1 %convolution_convert_fusion.1 = bf16[768,2048]{1,0:T(8,128)(2,1)S(1)} fusion(s32[512]{0:T(512)S(1)} %get-tuple-element.16, s32[512]{0:T(512)S(1)} %get-tuple-element.19, bf16[512,2048]{1,0:T(8,128)(2,1)S(1)} %copy-done.1, f32[2048]{0:T(1024)S(1)} %copy-done.11, f32[512]{0:T(512)S(1)} %bitcast.56), kind=kOutput, calls=%fused_computation.15 | convolution fusion | flops 1617559552 | bytes 5257216 | tf_op jit(solution)/shard_map/dot_general | solution.py:82
  12.9 43.1 %all_to_all.20 = bf16[8,96,2048]{2,1,0:T(8,128)(2,1)S(1)} all-to-all(bf16[8,96,2048]{2,1,0:T(8,128)(2,1)S(1)} %bitcast.47), channel_id=1, replica_groups=mesh['dp'=2,'ey'=4,'ex'=2,'mz'=8,'mx'=2] {'ey','ex'}, dimensions={0} | all-to-all | bytes 6291456 | tf_op jit(solution)/shard_map/all_to_all | solution.py:84
  56.1 2.4 %fusion.22 = f32[768,704]{0,1:T(8,128)S(1)} fusion(bf16[768,2048]{1,0:T(8,128)(2,1)S(1)} %bitcast.44, bf16[2048,352]{0,1:T(8,128)(2,1)S(1)} %bitcast.59, bf16[2048,352]{0,1:T(8,128)(2,1)S(1)} %bitcast.61), kind=kOutput, calls=%fused_computation.30 | convolution fusion | flops 2220359680 | bytes 8192000 | tf_op jit(solution)/shard_map/dot_general | solution.py:86
  58.5 3.5 %fusion.13 = bf16[2048,768]{0,1:T(8,128)(2,1)} fusion(bf16[1,352,2048]{2,1,0:T(8,128)(2,1)S(1)} %copy-done, f32[768,704]{0,1:T(8,128)S(1)} %fusion.22), kind=kOutput, calls=%fused_computation.23 | convolution fusion | flops 1110491136 | bytes 6750208 | tf_op jit(solution)/shard_map/dot_general | solution.py:89
  62.2 2.8 %convolution_convert_fusion.3 = bf16[768,2048]{1,0:T(8,128)(2,1)S(1)} fusion(s32[512]{0:T(512)} %get-tuple-element.15, s32[512]{0:T(512)} %get-tuple-element.20, bf16[512,2048]{1,0:T(8,128)(2,1)S(1)} %copy-done.1, f32[2048]{0:T(1024)} %param.8, f32[512]{0:T(512)} %bitcast.57), kind=kOutput, calls=%fused_computation.17 | convolution fusion | flops 1617559552 | bytes 5257216 | tf_op jit(solution)/shard_map/dot_general | solution.py:82
  65.0 40.4 %all_to_all.21 = bf16[8,96,2048]{2,1,0:T(8,128)(2,1)S(1)} all-to-all(bf16[8,96,2048]{2,1,0:T(8,128)(2,1)S(1)} %bitcast.45), channel_id=1, replica_groups=mesh['dp'=2,'ey'=4,'ex'=2,'mz'=8,'mx'=2] {'ey','ex'}, dimensions={0} | all-to-all | bytes 6291456 | tf_op jit(solution)/shard_map/all_to_all | solution.py:84
  105.4 2.4 %fusion.23 = f32[768,704]{0,1:T(8,128)S(1)} fusion(bf16[768,2048]{1,0:T(8,128)(2,1)S(1)} %bitcast.46, bf16[2048,352]{0,1:T(8,128)(2,1)S(1)} %bitcast.60, bf16[2048,352]{0,1:T(8,128)(2,1)S(1)} %bitcast.62), kind=kOutput, calls=%fused_computation.31 | convolution fusion | flops 2220359680 | bytes 8192000 | tf_op jit(solution)/shard_map/dot_general | solution.py:86
  107.8 3.6 %fusion.12 = bf16[2048,768]{0,1:T(8,128)(2,1)} fusion(bf16[1,352,2048]{2,1,0:T(8,128)(2,1)S(1)} %copy-done, f32[768,704]{0,1:T(8,128)S(1)} %fusion.23), kind=kOutput, calls=%fused_computation.22 | convolution fusion | flops 1110491136 | bytes 6750208 | tf_op jit(solution)/shard_map/dot_general | solution.py:89
  111.4 1.3 pad_add_fusion
  113.3 0.7 fusion.18
  114.1 0.8 fusion.25
  115.0 1.1 reshape.121
  116.1 0.8 copy.9
  116.9 5.7 %all-to-all-start.3 = ((bf16[16,128,96]{1,2,0:T(8,128)(2,1)}), bf16[16,128,96]{1,2,0:T(8,128)(2,1)S(1)}, u32[]{:S(2)}, u32[]{:S(2)}) async-start(bf16[16,128,96]{1,2,0:T(8,128)(2,1)} %bitcast.19), calls=%async_computation.5 | async-start | bytes 786432 | tf_op jit(solution)/shard_map/all_to_all | solution.py:97
  122.6 2.4 %select_reduce_fusion = (f32[512]{0:T(512)S(1)}, f32[512]{0:T(512)S(1)}) fusion(s32[512]{0:T(512)S(1)} %bitcast.55, s32[512]{0:T(512)S(1)} %bitcast.52, bf16[2048,8]{0,1:T(8,128)(2,1)S(1)} %copy-done.10, bf16[512,2048]{1,0:T(8,128)(2,1)} %param.7, f32[512]{0:T(512)S(1)} %bitcast.58, f32[2048]{0:T(1024)S(1)} %copy-done.12), kind=kOutput, calls=%fused_computation.76 | convolution fusion | flops 20995072 | bytes 2148352 | tf_op jit(solution)/shard_map/dot_general | solution.py:103
  125.0 34.9 %reduce-scatter.3.cloned.1.call-done = bf16[256,768]{0,1:T(8,128)(2,1)} async-done(((bf16[2048,768]{0,1:T(8,128)(2,1)}), bf16[256,768]{0,1:T(8,128)(2,1)}) %reduce-scatter.3.cloned.1.call-update) | async-done | bytes 393232 | tf_op jit(solution)/shard_map/reduce_scatter | solution.py:93
  159.9 1.1 reshape.115
  161.0 0.8 copy.8
  161.8 7.2 %all-to-all-start.1 = ((bf16[16,128,96]{1,2,0:T(8,128)(2,1)}), bf16[16,128,96]{1,2,0:T(8,128)(2,1)S(1)}, u32[]{:S(2)}, u32[]{:S(2)}) async-start(bf16[16,128,96]{1,2,0:T(8,128)(2,1)} %bitcast.10), calls=%async_computation.2 | async-start | bytes 786432 | tf_op jit(solution)/shard_map/all_to_all | solution.py:97
  169.8 6.8 %all-to-all-done.1 = bf16[16,128,96]{1,2,0:T(8,128)(2,1)S(1)} async-done(((bf16[16,128,96]{1,2,0:T(8,128)(2,1)}), bf16[16,128,96]{1,2,0:T(8,128)(2,1)S(1)}, u32[]{:S(2)}, u32[]{:S(2)}) %all-to-all-start.1) | async-done | bytes 393248 | tf_op jit(solution)/shard_map/all_to_all | solution.py:97
  176.6 0.7 fusion.10
  177.3 1.8 fusion.53
  (42 shorter events, 2.5 us)
Async XLA Ops:
  6.5 52.0 %copy-start = (bf16[1,352,2048]{2,1,0:T(8,128)(2,1)S(1)}, bf16[1,352,2048]{2,1,0:T(8,128)(2,1)}, u32[]{:S(2)}) copy-start(bf16[1,352,2048]{2,1,0:T(8,128)(2,1)} %param.13) | copy-start | bytes 4325380
  6.5 2.5 %copy-start.1 = (bf16[512,2048]{1,0:T(8,128)(2,1)S(1)}, bf16[512,2048]{1,0:T(8,128)(2,1)}, u32[]{:S(2)}) copy-start(bf16[512,2048]{1,0:T(8,128)(2,1)} %param.7) | copy-start | bytes 6291460
  6.5 108.4 %reduce-scatter.5.cloned.1.call-start = ((), (), s32[]{:S(2)}) async-start(), calls=%async_computation.7 | async-start | bytes 3538944 | tf_op jit(solution)/shard_map/reduce_scatter | solution.py:93
  9.0 0.9 copy-start.2
  9.1 1.8 copy-start.11
  10.8 2.1 %copy-start.5 = (f32[512,1]{0,1:T(1,128)}, f32[512,1]{0,1:T(1,128)S(1)}, u32[]{:S(2)}) copy-start(f32[512,1]{0,1:T(1,128)S(1)} %add_rsqrt_fusion.1) | copy-start | bytes 6148
  12.9 43.1 %copy-start.6 = (bf16[1,2048,352]{1,2,0:T(8,128)(2,1)S(1)}, bf16[1,2048,352]{1,2,0:T(8,128)(2,1)}, u32[]{:S(2)}) copy-start(bf16[1,2048,352]{1,2,0:T(8,128)(2,1)} %param.12) | copy-start | bytes 4325380
  12.9 43.1 %copy-start.8 = (bf16[1,2048,352]{1,2,0:T(8,128)(2,1)S(1)}, bf16[1,2048,352]{1,2,0:T(8,128)(2,1)}, u32[]{:S(2)}) copy-start(bf16[1,2048,352]{1,2,0:T(8,128)(2,1)} %param.11) | copy-start | bytes 4325380
  62.1 97.8 %reduce-scatter.3.cloned.1.call-start = ((), (), s32[]{:S(2)}) async-start(), calls=%async_computation.6 | async-start | bytes 3538944 | tf_op jit(solution)/shard_map/reduce_scatter | solution.py:93
  64.9 40.4 %copy-start.7 = (bf16[1,2048,352]{1,2,0:T(8,128)(2,1)S(1)}, bf16[1,2048,352]{1,2,0:T(8,128)(2,1)}, u32[]{:S(2)}) copy-start(bf16[1,2048,352]{1,2,0:T(8,128)(2,1)} %param.12) | copy-start | bytes 4325380
  64.9 40.4 %copy-start.9 = (bf16[1,2048,352]{1,2,0:T(8,128)(2,1)S(1)}, bf16[1,2048,352]{1,2,0:T(8,128)(2,1)}, u32[]{:S(2)}) copy-start(bf16[1,2048,352]{1,2,0:T(8,128)(2,1)} %param.11) | copy-start | bytes 4325380
  114.1 8.5 %copy-start.12 = (f32[2048]{0:T(1024)S(1)}, f32[2048]{0:T(1024)}, u32[]{:S(2)}) copy-start(f32[2048]{0:T(1024)} %param.8) | copy-start | bytes 24580
  114.9 7.7 %copy-start.10 = (bf16[2048,8]{0,1:T(8,128)(2,1)S(1)}, bf16[2048,8]{0,1:T(8,128)(2,1)}, u32[]{:S(2)}) copy-start(bf16[2048,8]{0,1:T(8,128)(2,1)} %param.9) | copy-start | bytes 98308
  116.9 44.9 %all-to-all-start.3 = ((bf16[16,128,96]{1,2,0:T(8,128)(2,1)}), bf16[16,128,96]{1,2,0:T(8,128)(2,1)S(1)}, u32[]{:S(2)}, u32[]{:S(2)}) async-start(bf16[16,128,96]{1,2,0:T(8,128)(2,1)} %bitcast.19), calls=%async_computation.5 | async-start | bytes 786432 | tf_op jit(solution)/shard_map/all_to_all | solution.py:97
  125.0 44.1 %copy-start.4 = (s32[1024]{0:T(1024)S(1)}, s32[1024]{0:T(1024)}, u32[]{:S(2)}) copy-start(s32[1024]{0:T(1024)} %pad_add_fusion.1) | copy-start | bytes 12292
  161.0 15.6 %copy-start.3 = (s32[1024]{0:T(1024)S(1)}, s32[1024]{0:T(1024)}, u32[]{:S(2)}) copy-start(s32[1024]{0:T(1024)} %pad_add_fusion) | copy-start | bytes 12292
  161.8 14.7 %all-to-all-start.1 = ((bf16[16,128,96]{1,2,0:T(8,128)(2,1)}), bf16[16,128,96]{1,2,0:T(8,128)(2,1)S(1)}, u32[]{:S(2)}, u32[]{:S(2)}) async-start(bf16[16,128,96]{1,2,0:T(8,128)(2,1)} %bitcast.10), calls=%async_computation.2 | async-start | bytes 786432 | tf_op jit(solution)/shard_map/all_to_all | solution.py:97
Sparse Core Ops, SparseCore 0:
  62.2 48.5 reduce-scatter.4
  113.4 46.4 reduce-scatter.2
